TPU v7x, 32 devices: a whole 2x2x4 slice. The times are simulated.
32 devices in a mesh: island: 4 (over z), fsdp: 8 (over y, x, core).
Axes of the slice: x: 2, y: 2, z: 4, core: 2. Of those that a mesh axis runs over, the one named last changes fastest.
Arguments:
- activations: bfloat16 [4, 4096, 8192], P('island', 'fsdp'), may hold values from -150 to 150
- key_cotangents: bfloat16 [4, 4096, 512], P('island', 'fsdp'), may hold values from -60 to 60
- master: float32 [8192, 512], P('fsdp'), may hold values from -6 to 6
- momentum: float32 [8192, 512], P('fsdp'), may hold values from -3 to 3
- island_weights: float32 [4, 8192, 512], P('island', 'fsdp'), may hold values from -6 to 6
- first_moment: float32 [4, 8192, 512], P('island', 'fsdp'), may hold values from -0.0024414062 to 0.0024414062
- second_moment: float32 [4, 8192, 512], P('island', 'fsdp'), may hold values from 5.9604645e-08 to 9.536743e-07
- tile_rows: int32 [48], replicated, may hold values from 1 to 512, 8192 in all
Outputs:
- master_out: float32 [8192, 512], P('fsdp')
- momentum_out: float32 [8192, 512], P('fsdp')
- tile_sums: float32 [48], replicated
Inputs may be any that keep to these rules, and one draw needn't show every extreme that they name: `tile_rows`: consecutive tiles covering all 8192 rows; the largest has exactly 512 rows.
All inputs are finite; a program needn't handle non-finite values.
Results may differ from a plain program's by a relative error of at most 0.0003.
Values may be sent and summed in bfloat16 or wider, within the bound.
No kernel may reach another device: no remote copies, remote signals or barrier semaphores. Data moves between devices by JAX's collectives and lax.ppermute only.
A program may use at most 128 MiB of HBM per device.

v0:
```python
import jax
import jax.numpy as jnp
from jax import lax
from jax.sharding import PartitionSpec as P

HEAD = 128
SEQ = 8192


beta_one = 0.9
beta_two = 0.95
bias_one = 1.0 - 0.9**3
bias_two = 1.0 - 0.95**3
inner_rate = 0.5
decay_rate = 0.1
outer_rate = 0.7
outer_moment = 0.9
adam_eps = 1e-08
norm_epsilon = 1e-06
rope_base = 500000.0


def unrotate(cotangent, first_row):
    rows = cotangent.shape[0]
    half = HEAD // 2
    positions = ((first_row + jnp.arange(rows, dtype=jnp.int32)) % SEQ).astype(jnp.float32)
    rates = rope_base ** (-2.0 * jnp.arange(half).astype(jnp.float32) / HEAD)
    angles = positions[:, None] * rates[None, :]
    cosine = jnp.cos(angles)[:, None, :]
    sine = jnp.sin(angles)[:, None, :]
    heads = cotangent.astype(jnp.float32).reshape(rows, -1, HEAD)
    lower = heads[:, :, :half]
    upper = heads[:, :, half:]
    turned = jnp.concatenate([lower * cosine + upper * sine, upper * cosine - lower * sine], axis=2)
    return turned.reshape(rows, -1).astype(jnp.bfloat16)


def adam_update(gradient, weights, first, second):
    first_new = beta_one * first + (1.0 - beta_one) * gradient
    second_new = beta_two * second + (1.0 - beta_two) * gradient * gradient
    ratio = first_new / bias_one / (jnp.sqrt(second_new / bias_two) + adam_eps)
    return weights - inner_rate * (ratio + decay_rate * weights)


def local_tiles(drift_rows, tile_rows, first_row):
    ends = jnp.cumsum(tile_rows, dtype=jnp.int32)
    starts = ends - tile_rows
    rows = first_row + jnp.arange(drift_rows.shape[0], dtype=jnp.int32)
    member = ((rows[:, None] >= starts[None, :]) & (rows[:, None] < ends[None, :])).astype(
        jnp.float32
    )
    return jnp.dot(jnp.sum(drift_rows, axis=1), member, precision=lax.Precision.HIGHEST)


def body(
    activations,
    key_cotangents,
    master,
    momentum,
    island_weights,
    first_moment,
    second_moment,
    tile_rows,
):
    tokens = activations[0]
    tok_rows = tokens.shape[0]
    own_rows = master.shape[0]
    position = lax.axis_index("fsdp")
    unrotated = unrotate(key_cotangents[0], position * tok_rows)
    gradient = lax.psum_scatter(
        lax.dot_general(
            tokens, unrotated, (((0,), (0,)), ((), ())), preferred_element_type=jnp.float32
        ),
        "fsdp",
        scatter_dimension=0,
        tiled=True,
    )
    squares = lax.psum(jnp.sum(gradient * gradient), "fsdp")
    factor = 1.0 / jnp.sqrt(squares + norm_epsilon)
    inner = adam_update(gradient * factor, island_weights[0], first_moment[0], second_moment[0])
    island_drift = master - inner
    replicas = lax.axis_size("island")
    drift = lax.psum(island_drift, "island") / replicas
    momentum_out = outer_moment * momentum + drift
    master_out = master - outer_rate * (drift + outer_moment * momentum_out)
    first_row = position * own_rows
    totals = (
        lax.psum(local_tiles(island_drift, tile_rows, first_row), ("island", "fsdp")) / replicas
    )
    tile_sums = totals / jnp.sqrt(tile_rows.astype(jnp.float32) * master.shape[1])
    return (master_out, momentum_out, tile_sums)


def solution(mesh):
    placed = (
        P("island", "fsdp", None),
        P("island", "fsdp", None),
        P("fsdp", None),
        P("fsdp", None),
        P("island", "fsdp", None),
        P("island", "fsdp", None),
        P("island", "fsdp", None),
        P(),
    )
    return jax.shard_map(
        body,
        mesh=mesh,
        in_specs=placed,
        out_specs=(P("fsdp", None), P("fsdp", None), P()),
        check_vma=False,
    )
```

profile of v0, /device:TPU:0, one launch (start us, length us, event | category | flops | bytes accessed | tf_op | source)
XLA Modules:
  0.0 272.2 jit_solution(8905218357389504971)
XLA Ops:
  7.2 0.0 reduce-scatter.2.cloned.1.call-start
  7.2 1.4 reshape.121
  8.6 1.0 multiply_cosine_fusion
  9.6 0.9 add_convert_fusion
  10.5 0.7 pad_maximum_fusion
  11.2 11.5 %convolution_bitcast_fusion = f32[8192,512]{0,1:T(8,128)} fusion(bf16[1,512,8192]{2,1,0:T(8,128)(2,1)} %param.8, bf16[64,8,4,128]{3,2,1,0:T(4,128)(2,1)S(1)} %bitcast.38), kind=kOutput, calls=%fused_computation | convolution fusion | flops 4294967296 | bytes 25690112 | tf_op jit(solution)/shard_map/dot_general | solution.py:71
  22.7 0.0 reduce-scatter.2.cloned.1.call-update
  22.7 0.0 all-reduce.2.cloned.1.call-start
  22.8 1.9 copy.25
  24.7 2.9 %copy.20 = f32[1,1024,512]{1,2,0:T(8,128)} copy(f32[1,1024,512]{2,1,0:T(8,128)} %param.12) | data formatting | bytes 4194304 | tf_op args[4]
  27.6 2.9 %copy.21 = f32[1,1024,512]{1,2,0:T(8,128)} copy(f32[1,1024,512]{2,1,0:T(8,128)} %param.13) | data formatting | bytes 4194304 | tf_op args[5]
  30.5 111.0 %reduce-scatter.2.cloned.1.call-done = f32[1024,512]{0,1:T(8,128)} async-done(((f32[8192,512]{0,1:T(8,128)}), f32[1024,512]{0,1:T(8,128)}) %reduce-scatter.2.cloned.1.call-update) | async-done | bytes 2097168 | tf_op jit(solution)/shard_map/reduce_scatter | solution.py:70
  141.5 2.7 %multiply_reduce_fusion = f32[]{:T(128)} fusion(f32[1024,512]{0,1:T(8,128)} %reduce-scatter.2.cloned.1.call-done), kind=kLoop, calls=%fused_computation.16 | loop fusion | flops 1048575 | bytes 2097156 | tf_op jit(solution)/shard_map/reduce_sum | solution.py:78
  144.3 2.9 %copy.22 = f32[1,1024,512]{1,2,0:T(8,128)} copy(f32[1,1024,512]{2,1,0:T(8,128)} %param.14) | data formatting | bytes 4194304 | tf_op args[6]
  147.2 13.3 %psum.21 = f32[]{:T(128)} all-reduce(f32[]{:T(128)} %multiply_reduce_fusion), channel_id=1, replica_groups=mesh['island'=4,'fsdp'=8] {'fsdp'}, use_global_device_ids=true, to_apply=%region_2.3 | all-reduce | flops 1 | bytes 8 | tf_op jit(solution)/shard_map/psum | solution.py:78
  161.2 6.6 %fusion.17 = (f32[1024]{0:T(1024)S(1)}, f32[1024,512]{0,1:T(8,128)}) fusion(f32[1024,512]{0,1:T(8,128)S(1)} %copy.25, f32[1,1024,512]{1,2,0:T(8,128)} %copy.22, f32[1024,512]{0,1:T(8,128)} %reduce-scatter.2.cloned.1.call-done, f32[]{:T(128)S(6)} %sqrt.9, f32[1,1024,512]{1,2,0:T(8,128)} %copy.21, f32[1,1024,512]{1,2,0:T(8,128)} %copy.20), kind=kLoop, calls=%fused_computation.38 | loop fusion | flops 9436160 | bytes 12587012 | tf_op jit(solution)/shard_map/reduce_sum | solution.py:52
  167.7 0.0 copy-start.1
  167.7 0.0 all-reduce.2.cloned.1.call-update
  167.7 0.6 copy-done.1
  168.4 0.1 copy.26
  168.5 0.1 reduce-window.8
  168.5 0.1 reduce
  168.7 2.9 %copy.24 = f32[1024,512]{0,1:T(8,128)} copy(f32[1024,512]{1,0:T(8,128)} %param.11) | data formatting | bytes 4194304 | tf_op args[3]
  171.6 0.4 convolution_bitcast_fusion.1
  171.9 42.2 %psum.23 = f32[48]{0:T(128)S(1)} all-reduce(f32[48]{0:T(128)S(1)} %convolution_bitcast_fusion.1), channel_id=1, replica_groups=mesh['island'=4,'fsdp'=8] {'island','fsdp'}, use_global_device_ids=true, to_apply=%region_6.7 | all-reduce | flops 48 | bytes 384 | tf_op jit(solution)/shard_map/psum | solution.py:88
  214.2 0.5 rsqrt_multiply_fusion
  214.7 40.7 %all-reduce.2.cloned.1.call-done = f32[1024,512]{0,1:T(8,128)} async-done(((f32[1024,512]{0,1:T(8,128)}), f32[1024,512]{0,1:T(8,128)}) %all-reduce.2.cloned.1.call-update) | async-done | bytes 2097168 | tf_op jit(solution)/shard_map/psum | solution.py:83
  255.3 5.2 %multiply_add_fusion = (f32[1024,512]{0,1:T(8,128)}, f32[1024,512]{0,1:T(8,128)}) fusion(f32[1024,512]{0,1:T(8,128)} %copy.24, f32[1024,512]{0,1:T(8,128)} %all-reduce.2.cloned.1.call-done, f32[1024,512]{0,1:T(8,128)S(1)} %copy.25), kind=kLoop, calls=%fused_computation.15 | loop fusion | flops 3670016 | bytes 10485760 | tf_op jit(solution)/shard_map/add | solution.py:84
  260.5 0.0 copy-start
  260.5 3.0 %copy.27 = f32[1024,512]{1,0:T(8,128)} copy(f32[1024,512]{0,1:T(8,128)} %get-tuple-element.12) | data formatting | bytes 4194304
  263.6 0.0 copy-done
  263.6 1.8 copy.28
  (4 shorter events, 0.0 us)
Async XLA Ops:
  7.2 134.4 %reduce-scatter.2.cloned.1.call-start = ((), (), s32[]{:S(2)}) async-start(), calls=%async_computation.1 | async-start | bytes 18874368 | tf_op jit(solution)/shard_map/reduce_scatter | solution.py:70
  22.7 232.6 %all-reduce.2.cloned.1.call-start = ((), (), s32[]{:S(2)}) async-start(), calls=%async_computation.2 | async-start | bytes 4194304 | tf_op jit(solution)/shard_map/psum | solution.py:83
  167.7 0.7 copy-start.1
  260.5 3.0 %copy-start = (f32[1024,512]{0,1:T(8,128)S(1)}, f32[1024,512]{0,1:T(8,128)}, u32[]{:S(2)}) copy-start(f32[1024,512]{0,1:T(8,128)} %get-tuple-element.11) | copy-start | bytes 6291460
Sparse Core Ops, SparseCore 0:
  22.9 118.6 reduce-scatter.1
  167.9 87.4 all-reduce.1
where the time goes:
time: 273 us; the launch traced here: 272 us
  waiting for transfers between devices  152 us (56%)
  blocking collectives  55.5 us (20%)
  local copies, waits for them, and re-layouts  20.4 us (7%)
  other arithmetic  17.8 us (7%)
  between operations  14.8 us (5%)
  matrix products  11.9 us (4%)
    reduce_scatter x1, waiting for transfers between devices, body(): lax.psum_scatter(lax.dot_general(tokens, unrotated, (((0,), (0,)), ((), (...  111 us
    psum x1, blocking collectives, body(): lax.psum(local_tiles(island_drift, tile_rows, first_row), ('island', 'fsd...  42.2 us
    psum x1, waiting for transfers between devices, body(): drift = lax.psum(island_drift, 'island') / replicas  40.7 us
    unnamed x11, local copies, waits for them, and re-layouts  18.9 us
    psum x1, blocking collectives, body(): squares = lax.psum(jnp.sum(gradient * gradient), 'fsdp')  13.3 us
    dot_general x1, matrix products, body(): lax.dot_general(tokens, unrotated, (((0,), (0,)), ((), ())), preferred_el...  11.5 us
    reduce_sum x1, other arithmetic, local_tiles(): jnp.sum(drift_rows, axis=1)  6.56 us
  transfers between devices with their start and end apart: 2, of which 2 were waited for; matrix products, arithmetic and copies ran while one was open for 4% of the time, Pallas kernels for 0%

commit v1 on v0

--- a/solution.py
+++ b/solution.py
@@ -62,18 +62,15 @@
     second_moment,
     tile_rows,
 ):
-    tokens = activations[0]
-    tok_rows = tokens.shape[0]
     own_rows = master.shape[0]
     position = lax.axis_index("fsdp")
-    unrotated = unrotate(key_cotangents[0], position * tok_rows)
-    gradient = lax.psum_scatter(
-        lax.dot_general(
-            tokens, unrotated, (((0,), (0,)), ((), ())), preferred_element_type=jnp.float32
-        ),
-        "fsdp",
-        scatter_dimension=0,
-        tiled=True,
+    columns = lax.all_to_all(activations[0], "fsdp", 1, 0, tiled=True)
+    tok_rows = key_cotangents.shape[1]
+    unrotated = lax.all_gather(
+        unrotate(key_cotangents[0], position * tok_rows), "fsdp", axis=0, tiled=True
+    )
+    gradient = lax.dot_general(
+        columns, unrotated, (((0,), (0,)), ((), ())), preferred_element_type=jnp.float32
     )
     squares = lax.psum(jnp.sum(gradient * gradient), "fsdp")
     factor = 1.0 / jnp.sqrt(squares + norm_epsilon)
@@ -84,9 +81,7 @@
     momentum_out = outer_moment * momentum + drift
     master_out = master - outer_rate * (drift + outer_moment * momentum_out)
     first_row = position * own_rows
-    totals = (
-        lax.psum(local_tiles(island_drift, tile_rows, first_row), ("island", "fsdp")) / replicas
-    )
+    totals = lax.psum(local_tiles(drift, tile_rows, first_row), "fsdp")
     tile_sums = totals / jnp.sqrt(tile_rows.astype(jnp.float32) * master.shape[1])
     return (master_out, momentum_out, tile_sums)
 

time: 273 us -> 298 us (1.092)
  waiting for transfers between devices: 152 us -> 182 us
  blocking collectives: 55.5 us -> 26.2 us
  local copies, waits for them, and re-layouts: 20.4 us -> 43 us
  starting transfers between devices: 0.08 us -> 5.38 us
    reduce_scatter x1 -> x0, waiting for transfers between devices: 111 us -> none  [body(): lax.psum_scatter(lax.dot_general(tokens, unrotated, (((0,), (0,)), ((), (...]
    all_to_all x0 -> x1, waiting for transfers between devices: none -> 96.8 us  [body(): columns = lax.all_to_all(activations[0], 'fsdp', 1, 0, tiled=True)]
    psum x1, waiting for transfers between devices: 40.7 us -> 84.7 us  [body(): drift = lax.psum(island_drift, 'island') / replicas]
    psum x1, blocking collectives: 42.2 us -> 13.6 us  [body(): totals = lax.psum(local_tiles(drift, tile_rows, first_row), 'fsdp')]
    unnamed x11 -> x15, local copies, waits for them, and re-layouts: 18.9 us -> 31.2 us
    all_to_all x0 -> x1, local copies, waits for them, and re-layouts: none -> 11.4 us  [body(): columns = lax.all_to_all(activations[0], 'fsdp', 1, 0, tiled=True)]
    reduce_sum x2 -> x0, other arithmetic: 9.3 us -> none  [the longest x1 6.56 us: local_tiles(): jnp.sum(drift_rows, axis=1)]
    sub x0 -> x1, other arithmetic: none -> 6.49 us  [body(): island_drift = master - inner]
  transfers between devices with their start and end apart: 2 -> 3, of which waited for: 2 -> 2; matrix products, arithmetic and copies ran while one was open for 4% -> 10% of each run, Pallas kernels for 0% -> 0%
where the time goes in v1:
time: 298 us; the launch traced here: 297 us
  waiting for transfers between devices  182 us (61%)
  local copies, waits for them, and re-layouts  43 us (14%)
  blocking collectives  26.2 us (9%)
  other arithmetic  15 us (5%)
  between operations  14.8 us (5%)
  matrix products  11.5 us (4%)
  starting transfers between devices  5.38 us (2%)
    all_to_all x1, waiting for transfers between devices, body(): columns = lax.all_to_all(activations[0], 'fsdp', 1, 0, tiled=True)  96.8 us
    psum x1, waiting for transfers between devices, body(): drift = lax.psum(island_drift, 'island') / replicas  84.7 us
    unnamed x15, local copies, waits for them, and re-layouts  31.2 us
    psum x1, blocking collectives, body(): totals = lax.psum(local_tiles(drift, tile_rows, first_row), 'fsdp')  13.6 us
    psum x1, blocking collectives, body(): squares = lax.psum(jnp.sum(gradient * gradient), 'fsdp')  12.6 us
    all_to_all x1, local copies, waits for them, and re-layouts, body(): columns = lax.all_to_all(activations[0], 'fsdp', 1, 0, tiled=True)  11.4 us
    dot_general x1, matrix products, body(): lax.dot_general(columns, unrotated, (((0,), (0,)), ((), ())), preferred_e...  11.1 us
    sub x1, other arithmetic, body(): island_drift = master - inner  6.49 us
  transfers between devices with their start and end apart: 3, of which 2 were waited for; matrix products, arithmetic and copies ran while one was open for 10% of the time, Pallas kernels for 0%

profile of v1, /device:TPU:0, one launch (start us, length us, event | category | flops | bytes accessed | tf_op | source)
XLA Modules:
  0.0 297.4 jit_solution(9480182531813186173)
XLA Ops:
  7.2 11.9 %copy.31 = bf16[1,512,8192]{1,2,0:T(8,128)(2,1)} copy(bf16[1,512,8192]{2,1,0:T(8,128)(2,1)} %param.8) | data formatting | bytes 16777216 | tf_op args[0]
  19.1 0.0 copy-start.1
  19.1 5.3 %all-to-all-start = ((bf16[512,8,1024]{0,2,1:T(8,128)(2,1)}), bf16[512,8,1024]{0,2,1:T(8,128)(2,1)}, u32[]{:S(2)}, u32[]{:S(2)}) async-start(bf16[512,8,1024]{0,2,1:T(8,128)(2,1)} %bitcast.42), calls=%async_computation | async-start | bytes 16777216 | tf_op jit(solution)/shard_map/all_to_all | solution.py:67
  24.4 0.0 all-gather.2.cloned.1.call-start
  24.5 0.0 copy-done.1
  24.5 0.3 reshape.119
  24.8 1.0 multiply_cosine_fusion
  25.8 0.9 add_convert_fusion
  26.7 0.7 pad_maximum_fusion
  27.4 0.9 copy.42
  28.3 0.0 all-gather.2.cloned.1.call-update
  28.3 0.0 all-reduce.2.cloned.1.call-start
  28.4 1.9 copy.36
  30.3 2.9 copy.29
  33.2 2.9 copy.30
  36.1 2.9 copy.33
  39.0 96.8 %all-to-all-done = bf16[512,8,1024]{0,2,1:T(8,128)(2,1)} async-done(((bf16[512,8,1024]{0,2,1:T(8,128)(2,1)}), bf16[512,8,1024]{0,2,1:T(8,128)(2,1)}, u32[]{:S(2)}, u32[]{:S(2)}) %all-to-all-start) | async-done | bytes 8388640 | tf_op jit(solution)/shard_map/all_to_all | solution.py:67
  135.7 11.4 %copy.32 = bf16[8,512,1024]{2,1,0:T(8,128)(2,1)} copy(bf16[8,512,1024]{1,2,0:T(8,128)(2,1)} %bitcast.3) | data formatting | bytes 16777216 | tf_op jit(solution)/shard_map/all_to_all | solution.py:67
  147.2 0.0 all-gather.2.cloned.1.call-done
  147.2 11.1 %multiply_reduce_fusion = (f32[]{:T(128)}, f32[512,1024]{1,0:T(8,128)}) fusion(bf16[4096,512]{1,0:T(8,128)(2,1)} %all-gather.2.cloned.1.call-done, bf16[4096,1024]{1,0:T(8,128)(2,1)} %bitcast.43), kind=kOutput, calls=%fused_computation.15 | convolution fusion | flops 4296015872 | bytes 14680068 | tf_op jit(solution)/shard_map/dot_general | solution.py:72
  158.3 12.6 %psum.21 = f32[]{:T(128)} all-reduce(f32[]{:T(128)} %get-tuple-element.19), channel_id=1, replica_groups=mesh['island'=4,'fsdp'=8] {'fsdp'}, use_global_device_ids=true, to_apply=%region_1.2 | all-reduce | flops 1 | bytes 8 | tf_op jit(solution)/shard_map/psum | solution.py:75
  171.6 6.5 %fusion.8 = f32[1024,512]{0,1:T(8,128)} fusion(f32[1024,512]{0,1:T(8,128)S(1)} %copy.36, f32[1,1024,512]{1,2,0:T(8,128)} %copy.29, f32[1,1024,512]{1,2,0:T(8,128)} %copy.33, f32[512,1024]{1,0:T(8,128)} %get-tuple-element.20, f32[1,1024,512]{1,2,0:T(8,128)} %copy.30, f32[]{:T(128)S(6)} %sqrt.9), kind=kLoop, calls=%fused_computation.12 | loop fusion | flops 8912896 | bytes 12582916 | tf_op jit(solution)/shard_map/sub | solution.py:78
  178.1 0.0 all-reduce.2.cloned.1.call-update
  178.1 0.0 copy-start.2
  178.1 2.9 copy.35
  181.0 0.0 copy-done.2
  181.0 0.1 copy.37
  181.1 0.1 reduce-window.8
  181.2 0.1 reduce.1
  181.3 84.7 %all-reduce.2.cloned.1.call-done = f32[1024,512]{0,1:T(8,128)} async-done(((f32[1024,512]{0,1:T(8,128)}), f32[1024,512]{0,1:T(8,128)}) %all-reduce.2.cloned.1.call-update) | async-done | bytes 2097168 | tf_op jit(solution)/shard_map/psum | solution.py:80
  266.0 5.2 %multiply_add_fusion = (f32[1024,512]{0,1:T(8,128)}, f32[1024,512]{0,1:T(8,128)}, f32[1024]{0:T(1024)S(1)}) fusion(f32[1024,512]{0,1:T(8,128)} %copy.35, f32[1024,512]{0,1:T(8,128)} %all-reduce.2.cloned.1.call-done, f32[1024,512]{0,1:T(8,128)S(1)} %copy.36), kind=kLoop, calls=%fused_computation.14 | loop fusion | flops 4193280 | bytes 10489856 | tf_op jit(solution)/shard_map/add | solution.py:81
  271.2 0.4 convolution_bitcast_fusion
  271.6 13.6 %psum.23 = f32[48]{0:T(128)S(1)} all-reduce(f32[48]{0:T(128)S(1)} %convolution_bitcast_fusion), channel_id=1, replica_groups=mesh['island'=4,'fsdp'=8] {'fsdp'}, use_global_device_ids=true, to_apply=%region_5.6 | all-reduce | flops 48 | bytes 384 | tf_op jit(solution)/shard_map/psum | solution.py:84
  285.2 0.5 rsqrt_multiply_fusion
  285.7 0.0 copy-start
  285.7 3.0 %copy.38 = f32[1024,512]{1,0:T(8,128)} copy(f32[1024,512]{0,1:T(8,128)} %get-tuple-element.13) | data formatting | bytes 4194304
  288.8 0.0 copy-done
  288.8 1.8 copy.39
  (4 shorter events, 0.0 us)
Async XLA Ops:
  19.1 5.4 %copy-start.1 = (bf16[1,512,512]{2,1,0:T(8,128)(2,1)S(1)}, bf16[1,512,512]{2,1,0:T(8,128)(2,1)}, u32[]{:S(2)}) copy-start(bf16[1,512,512]{2,1,0:T(8,128)(2,1)} %param.9) | copy-start | bytes 1572868
  19.1 116.7 %all-to-all-start = ((bf16[512,8,1024]{0,2,1:T(8,128)(2,1)}), bf16[512,8,1024]{0,2,1:T(8,128)(2,1)}, u32[]{:S(2)}, u32[]{:S(2)}) async-start(bf16[512,8,1024]{0,2,1:T(8,128)(2,1)} %bitcast.42), calls=%async_computation | async-start | bytes 16777216 | tf_op jit(solution)/shard_map/all_to_all | solution.py:67
  24.4 122.8 %all-gather.2.cloned.1.call-start = ((), (), s32[]{:S(2)}) async-start(), calls=%async_computation.1 | async-start | bytes 4718592 | tf_op jit(solution)/shard_map/all_gather | solution.py:69
  28.3 237.7 %all-reduce.2.cloned.1.call-start = ((), (), s32[]{:S(2)}) async-start(), calls=%async_computation.2 | async-start | bytes 4194304 | tf_op jit(solution)/shard_map/psum | solution.py:80
  178.1 2.9 copy-start.2
  285.7 3.0 %copy-start = (f32[1024,512]{0,1:T(8,128)S(1)}, f32[1024,512]{0,1:T(8,128)}, u32[]{:S(2)}) copy-start(f32[1024,512]{0,1:T(8,128)} %get-tuple-element.12) | copy-start | bytes 6291460
Sparse Core Ops, SparseCore 0:
  28.4 75.3 all-gather.1
  178.2 87.7 all-reduce.1

commit v2 on v1

--- a/solution.py
+++ b/solution.py
@@ -63,16 +63,27 @@
     tile_rows,
 ):
     own_rows = master.shape[0]
-    position = lax.axis_index("fsdp")
-    columns = lax.all_to_all(activations[0], "fsdp", 1, 0, tiled=True)
     tok_rows = key_cotangents.shape[1]
-    unrotated = lax.all_gather(
-        unrotate(key_cotangents[0], position * tok_rows), "fsdp", axis=0, tiled=True
+    chips = lax.axis_size("chip")
+    core = lax.axis_index("core")
+    position = lax.axis_index("chip") * 2 + core
+    swap = [(0, 1), (1, 0)]
+    unrotated = unrotate(key_cotangents[0], position * tok_rows)
+    blocks = activations[0].reshape(tok_rows, chips, 2, own_rows)
+    mine = lax.dynamic_index_in_dim(blocks, core, axis=2, keepdims=False)
+    other = lax.dynamic_index_in_dim(blocks, 1 - core, axis=2, keepdims=False)
+    their_tokens = lax.ppermute(other, "core", swap)
+    their_unrotated = lax.ppermute(unrotated, "core", swap)
+    contract = (((0,), (0,)), ((), ()))
+    partial = lax.dot_general(
+        mine.reshape(tok_rows, chips * own_rows), unrotated, contract,
+        preferred_element_type=jnp.float32,
+    ) + lax.dot_general(
+        their_tokens.reshape(tok_rows, chips * own_rows), their_unrotated, contract,
+        preferred_element_type=jnp.float32,
     )
-    gradient = lax.dot_general(
-        columns, unrotated, (((0,), (0,)), ((), ())), preferred_element_type=jnp.float32
-    )
-    squares = lax.psum(jnp.sum(gradient * gradient), "fsdp")
+    gradient = lax.psum_scatter(partial, "chip", scatter_dimension=0, tiled=True)
+    squares = lax.psum(jnp.sum(gradient * gradient), ("chip", "core"))
     factor = 1.0 / jnp.sqrt(squares + norm_epsilon)
     inner = adam_update(gradient * factor, island_weights[0], first_moment[0], second_moment[0])
     island_drift = master - inner
@@ -81,26 +92,34 @@
     momentum_out = outer_moment * momentum + drift
     master_out = master - outer_rate * (drift + outer_moment * momentum_out)
     first_row = position * own_rows
-    totals = lax.psum(local_tiles(drift, tile_rows, first_row), "fsdp")
+    totals = (
+        lax.psum(local_tiles(island_drift, tile_rows, first_row), ("island", "chip", "core"))
+        / replicas
+    )
     tile_sums = totals / jnp.sqrt(tile_rows.astype(jnp.float32) * master.shape[1])
     return (master_out, momentum_out, tile_sums)
 
 
 def solution(mesh):
+    islands, fsdp = mesh.devices.shape
+    cores = jax.sharding.Mesh(
+        mesh.devices.reshape(islands, fsdp // 2, 2), ("island", "chip", "core")
+    )
+    rows = ("chip", "core")
     placed = (
-        P("island", "fsdp", None),
-        P("island", "fsdp", None),
-        P("fsdp", None),
-        P("fsdp", None),
-        P("island", "fsdp", None),
-        P("island", "fsdp", None),
-        P("island", "fsdp", None),
+        P("island", rows, None),
+        P("island", rows, None),
+        P(rows, None),
+        P(rows, None),
+        P("island", rows, None),
+        P("island", rows, None),
+        P("island", rows, None),
         P(),
     )
     return jax.shard_map(
         body,
-        mesh=mesh,
+        mesh=cores,
         in_specs=placed,
-        out_specs=(P("fsdp", None), P("fsdp", None), P()),
+        out_specs=(P(rows, None), P(rows, None), P()),
         check_vma=False,
     )

time: 298 us -> 272 us (0.913)
  waiting for transfers between devices: 182 us -> 132 us
  blocking collectives: 26.2 us -> 55.7 us
  local copies, waits for them, and re-layouts: 43 us -> 33.3 us
  matrix products: 11.5 us -> 16.4 us
  starting transfers between devices: 5.38 us -> 0.66 us
    all_to_all x1 -> x0, waiting for transfers between devices: 96.8 us -> none  [body(): columns = lax.all_to_all(activations[0], 'fsdp', 1, 0, tiled=True)]
    reduce_scatter x0 -> x1, waiting for transfers between devices: none -> 88.9 us  [body(): lax.psum_scatter(partial, 'chip', scatter_dimension=0, tiled=True)]
    psum x1, waiting for transfers between devices: 84.7 us -> 43.5 us  [body(): drift = lax.psum(island_drift, 'island') / replicas]
    psum x2, blocking collectives: 26.2 us -> 55.7 us  [the longest x1 42.3 us: body(): lax.psum(local_tiles(island_drift, tile_rows, first_row), ('island', 'chi...]
    unnamed x15 -> x10, local copies, waits for them, and re-layouts: 31.2 us -> 13 us
    dynamic_slice x0 -> x2, local copies, waits for them, and re-layouts: none -> 13.6 us  [body(): other = lax.dynamic_index_in_dim(blocks, 1 - core, axis=2, keepdims=False)]
    all_to_all x1 -> x0, local copies, waits for them, and re-layouts: 11.4 us -> none  [body(): columns = lax.all_to_all(activations[0], 'fsdp', 1, 0, tiled=True)]
    reduce_sum x0 -> x2, other arithmetic: none -> 9.38 us  [the longest x1 6.65 us: local_tiles(): jnp.sum(drift_rows, axis=1)]
  transfers between devices with their start and end apart: 3 -> 4, of which waited for: 2 -> 2; matrix products, arithmetic and copies ran while one was open for 10% -> 6% of each run, Pallas kernels for 0% -> 0%
where the time goes in v2:
time: 272 us; the launch traced here: 271 us
  waiting for transfers between devices  132 us (49%)
  blocking collectives  55.7 us (20%)
  local copies, waits for them, and re-layouts  33.3 us (12%)
  other arithmetic  17.7 us (7%)
  matrix products  16.4 us (6%)
  between operations  14.8 us (5%)
    reduce_scatter x1, waiting for transfers between devices, body(): lax.psum_scatter(partial, 'chip', scatter_dimension=0, tiled=True)  88.9 us
    psum x1, waiting for transfers between devices, body(): drift = lax.psum(island_drift, 'island') / replicas  43.5 us
    psum x1, blocking collectives, body(): lax.psum(local_tiles(island_drift, tile_rows, first_row), ('island', 'chi...  42.3 us
    dynamic_slice x2, local copies, waits for them, and re-layouts, body(): other = lax.dynamic_index_in_dim(blocks, 1 - core, axis=2, keepdims=False)  13.6 us
    psum x1, blocking collectives, body(): squares = lax.psum(jnp.sum(gradient * gradient), ('chip', 'core'))  13.5 us
    unnamed x10, local copies, waits for them, and re-layouts  13 us
    dot_general x1, matrix products, body(): lax.dot_general(their_tokens.reshape(tok_rows, chips * own_rows), their_u...  10.2 us
    reduce_sum x1, other arithmetic, local_tiles(): jnp.sum(drift_rows, axis=1)  6.65 us
  transfers between devices with their start and end apart: 4, of which 2 were waited for; matrix products, arithmetic and copies ran while one was open for 6% of the time, Pallas kernels for 0%

profile of v2, /device:TPU:0, one launch (start us, length us, event | category | flops | bytes accessed | tf_op | source)
XLA Modules:
  0.0 271.0 jit_solution(1579005775285741684)
XLA Ops:
  7.2 0.0 reduce-scatter.2.cloned.1.call-start
  7.2 11.9 %copy.14 = bf16[1,512,8192]{1,2,0:T(8,128)(2,1)} copy(bf16[1,512,8192]{2,1,0:T(8,128)(2,1)} %param.8) | data formatting | bytes 16777216 | tf_op args[0]
  19.1 7.2 %constant_dynamic-slice_fusion = (bf16[512,4,1,1024]{0,3,2,1:T(8,128)(2,1)}, bf16[512,4,1,1024]{0,3,2,1:T(8,128)(2,1)}) fusion(bf16[512,4,2,1024]{0,3,2,1:T(8,128)(2,1)} %bitcast.41, s32[]{:T(128)S(6)} %select_n.20, s32[]{:T(128)S(6)} %select_n.18), kind=kLoop, calls=%fused_computation.36 | loop fusion | bytes 16777224 | tf_op jit(solution)/shard_map/jit(dynamic_index_in_dim)/dynamic_slice | solution.py:74
  26.3 0.0 copy-start.2
  26.3 6.4 %copy.15 = bf16[512,4,1,1024]{3,0,2,1:T(8,128)(2,1)} copy(bf16[512,4,1,1024]{0,3,2,1:T(8,128)(2,1)} %get-tuple-element.7) | data formatting | bytes 8388608 | tf_op jit(solution)/shard_map/jit(dynamic_index_in_dim)/dynamic_slice | solution.py:74
  32.8 0.5 collective-permute-start
  33.2 0.0 copy-done.2
  33.2 0.3 reshape.131
  33.6 1.0 multiply_cosine_fusion
  34.6 0.0 copy-start
  34.6 0.9 multiply_add_fusion.1
  35.4 0.7 maximum_convert_fusion
  36.2 0.1 copy.21
  36.2 0.1 collective-permute-start.1
  36.4 0.4 copy-done
  36.8 5.8 %fusion.14 = f32[4096,512]{1,0:T(8,128)} fusion(bf16[512,4096]{0,1:T(8,128)(2,1)S(1)} %bitcast.43, bf16[64,8,4,128]{3,2,1,0:T(4,128)(2,1)S(1)} %bitcast.45), kind=kOutput, calls=%fused_computation.38 | convolution fusion | flops 2147483648 | bytes 13107200 | tf_op jit(solution)/shard_map/dot_general | solution.py:78
  42.5 0.0 collective-permute-done
  42.5 6.2 %copy.16 = bf16[512,4,1024]{0,2,1:T(8,128)(2,1)} copy(bf16[512,4,1024]{2,0,1:T(8,128)(2,1)} %collective-permute-done) | data formatting | bytes 8388608 | tf_op jit(solution)/shard_map/ppermute | solution.py:75
  48.7 0.0 collective-permute-done.1
  48.7 10.2 %convolution_add_fusion = f32[4096,512]{1,0:T(8,128)} fusion(f32[4096,512]{1,0:T(8,128)} %fusion.14, bf16[512,4096]{0,1:T(8,128)(2,1)} %bitcast.42, bf16[512,512]{1,0:T(8,128)(2,1)S(1)} %collective-permute-done.1), kind=kOutput, calls=%fused_computation | convolution fusion | flops 2149580800 | bytes 21495808 | tf_op jit(solution)/shard_map/dot_general | solution.py:81
  59.0 0.0 reduce-scatter.2.cloned.1.call-update
  59.0 0.0 copy-start.1
  59.0 0.0 all-reduce.2.cloned.1.call-start
  59.0 88.9 %reduce-scatter.2.cloned.1.call-done = f32[1024,512]{1,0:T(8,128)} async-done(((f32[4096,512]{1,0:T(8,128)}), f32[1024,512]{1,0:T(8,128)}) %reduce-scatter.2.cloned.1.call-update) | async-done | bytes 2097168 | tf_op jit(solution)/shard_map/reduce_scatter | solution.py:85
  147.9 2.7 %multiply_reduce_fusion = f32[]{:T(128)} fusion(f32[1024,512]{1,0:T(8,128)} %reduce-scatter.2.cloned.1.call-done), kind=kLoop, calls=%fused_computation.15 | loop fusion | flops 1048575 | bytes 2097156 | tf_op jit(solution)/shard_map/reduce_sum | solution.py:86
  150.7 13.5 %psum.21 = f32[]{:T(128)} all-reduce(f32[]{:T(128)} %multiply_reduce_fusion), channel_id=1, replica_groups=mesh['island'=4,'chip'=4,'core'=2] {'chip','core'}, use_global_device_ids=true, to_apply=%region_2.3 | all-reduce | flops 1 | bytes 8 | tf_op jit(solution)/shard_map/psum | solution.py:86
  164.8 0.0 copy-done.1
  164.8 6.6 %fusion.15 = (f32[1024]{0:T(1024)S(1)}, f32[1024,512]{1,0:T(8,128)}) fusion(f32[1024,512]{1,0:T(8,128)S(1)} %copy-done.1, f32[1,1024,512]{2,1,0:T(8,128)} %param.14, f32[1024,512]{1,0:T(8,128)} %reduce-scatter.2.cloned.1.call-done, f32[]{:T(128)S(6)} %sqrt.9, f32[1,1024,512]{2,1,0:T(8,128)} %param.13, f32[1,1024,512]{2,1,0:T(8,128)} %param.12), kind=kLoop, calls=%fused_computation.39 | loop fusion | flops 9436160 | bytes 12587012 | tf_op jit(solution)/shard_map/reduce_sum | solution.py:52
  171.5 0.0 copy-start.3
  171.5 0.0 all-reduce.2.cloned.1.call-update
  171.5 0.6 copy-done.3
  172.2 0.1 copy.17
  172.2 0.1 reduce-window.8
  172.3 0.1 reduce
  172.5 0.4 convolution_bitcast_fusion
  172.8 42.3 %psum.23 = f32[48]{0:T(128)S(1)} all-reduce(f32[48]{0:T(128)S(1)} %convolution_bitcast_fusion), channel_id=1, replica_groups=mesh['island'=4,'chip'=4,'core'=2] {'island','chip','core'}, use_global_device_ids=true, to_apply=%region_6.7 | all-reduce | flops 48 | bytes 384 | tf_op jit(solution)/shard_map/psum | solution.py:96
  215.1 0.5 rsqrt_multiply_fusion
  215.6 43.5 %all-reduce.2.cloned.1.call-done = f32[1024,512]{1,0:T(8,128)} async-done(((f32[1024,512]{1,0:T(8,128)}), f32[1024,512]{1,0:T(8,128)}) %all-reduce.2.cloned.1.call-update) | async-done | bytes 2097168 | tf_op jit(solution)/shard_map/psum | solution.py:91
  259.1 5.0 %multiply_subtract_fusion = (f32[1024,512]{1,0:T(8,128)}, f32[1024,512]{1,0:T(8,128)}) fusion(f32[1024,512]{1,0:T(8,128)S(1)} %copy-done.1, f32[1024,512]{1,0:T(8,128)} %all-reduce.2.cloned.1.call-done, f32[1024,512]{1,0:T(8,128)} %param.11), kind=kLoop, calls=%fused_computation.13 | loop fusion | flops 3670016 | bytes 10485760 | tf_op jit(solution)/shard_map/sub | solution.py:93
  (4 shorter events, 0.0 us)
Async XLA Ops:
  7.2 140.8 %reduce-scatter.2.cloned.1.call-start = ((), (), s32[]{:S(2)}) async-start(), calls=%async_computation.1 | async-start | bytes 10485760 | tf_op jit(solution)/shard_map/reduce_scatter | solution.py:85
  26.3 6.9 %copy-start.2 = (bf16[1,512,512]{2,1,0:T(8,128)(2,1)S(1)}, bf16[1,512,512]{2,1,0:T(8,128)(2,1)}, u32[]{:S(2)}) copy-start(bf16[1,512,512]{2,1,0:T(8,128)(2,1)} %param.9) | copy-start | bytes 1572868
  32.8 9.8 %collective-permute-start = (bf16[512,4,1024]{2,0,1:T(8,128)(2,1)}, bf16[512,4,1024]{2,0,1:T(8,128)(2,1)}, u32[]{:S(2)}, u32[]{:S(2)}) collective-permute-start(bf16[512,4,1024]{2,0,1:T(8,128)(2,1)} %bitcast.46), channel_id=1, source_target_pairs={{0,1},{1,0},{2,3},{3,2},{4,5},{5,4},{6,7},{7,6},{8,9},{9,8},{10,11... | collective-permute-start | bytes 12582920 | tf_op jit(solution)/shard_map/ppermute | solution.py:75
  34.6 2.2 copy-start
  36.2 12.5 %collective-permute-start.1 = (bf16[512,512]{1,0:T(8,128)(2,1)S(1)}, bf16[512,512]{1,0:T(8,128)(2,1)S(1)}, u32[]{:S(2)}, u32[]{:S(2)}) collective-permute-start(bf16[512,512]{1,0:T(8,128)(2,1)S(1)} %bitcast.47), channel_id=1, source_target_pairs={{0,1},{1,0},{2,3},{3,2},{4,5},{5,4},{6,7},{7,6},{8,9},{9,8},{10,11... | collective-permute-start | bytes 1572872 | tf_op jit(solution)/shard_map/ppermute | solution.py:76
  59.0 105.9 %copy-start.1 = (f32[1024,512]{1,0:T(8,128)S(1)}, f32[1024,512]{1,0:T(8,128)}, u32[]{:S(2)}) copy-start(f32[1024,512]{1,0:T(8,128)} %param.10) | copy-start | bytes 6291460
  59.0 200.1 %all-reduce.2.cloned.1.call-start = ((), (), s32[]{:S(2)}) async-start(), calls=%async_computation.2 | async-start | bytes 4194304 | tf_op jit(solution)/shard_map/psum | solution.py:91
  171.5 0.7 copy-start.3
Sparse Core Ops, SparseCore 0:
  59.1 88.7 reduce-scatter.1
  171.6 87.4 all-reduce.1

commit v3 on v2

--- a/solution.py
+++ b/solution.py
@@ -69,20 +69,27 @@
     position = lax.axis_index("chip") * 2 + core
     swap = [(0, 1), (1, 0)]
     unrotated = unrotate(key_cotangents[0], position * tok_rows)
-    blocks = activations[0].reshape(tok_rows, chips, 2, own_rows)
-    mine = lax.dynamic_index_in_dim(blocks, core, axis=2, keepdims=False)
-    other = lax.dynamic_index_in_dim(blocks, 1 - core, axis=2, keepdims=False)
-    their_tokens = lax.ppermute(other, "core", swap)
+    tokens = activations[0]
+
+    def parity(side):
+        return jnp.stack(
+            [
+                lax.dynamic_slice_in_dim(tokens, (2 * k + side) * own_rows, own_rows, axis=1)
+                for k in range(chips)
+            ],
+            axis=1,
+        )
+
+    their_tokens = lax.ppermute(parity(1 - core), "core", swap)
     their_unrotated = lax.ppermute(unrotated, "core", swap)
     contract = (((0,), (0,)), ((), ()))
     partial = lax.dot_general(
-        mine.reshape(tok_rows, chips * own_rows), unrotated, contract,
-        preferred_element_type=jnp.float32,
+        unrotated, parity(core), contract, preferred_element_type=jnp.float32
     ) + lax.dot_general(
-        their_tokens.reshape(tok_rows, chips * own_rows), their_unrotated, contract,
-        preferred_element_type=jnp.float32,
+        their_unrotated, their_tokens, contract, preferred_element_type=jnp.float32
     )
-    gradient = lax.psum_scatter(partial, "chip", scatter_dimension=0, tiled=True)
+    gradient = lax.psum_scatter(partial, "chip", scatter_dimension=1, tiled=True)
+    gradient = gradient.reshape(gradient.shape[0], own_rows).T
     squares = lax.psum(jnp.sum(gradient * gradient), ("chip", "core"))
     factor = 1.0 / jnp.sqrt(squares + norm_epsilon)
     inner = adam_update(gradient * factor, island_weights[0], first_moment[0], second_moment[0])

time: 272 us -> 251 us (0.923)
  local copies, waits for them, and re-layouts: 33.3 us -> 26 us
  waiting for transfers between devices: 132 us -> 125 us
  matrix products: 16.4 us -> 10.8 us
    reduce_scatter x1 -> x0, waiting for transfers between devices: 88.9 us -> none  [body(): lax.psum_scatter(partial, 'chip', scatter_dimension=0, tiled=True)]
    unnamed x2 -> x3, waiting for transfers between devices: 0.03 us -> 81.5 us
    dynamic_slice x2 -> x0, local copies, waits for them, and re-layouts: 13.6 us -> none  [body(): other = lax.dynamic_index_in_dim(blocks, 1 - core, axis=2, keepdims=False)]
    ppermute x1 -> x0, local copies, waits for them, and re-layouts: 6.21 us -> none  [body(): their_tokens = lax.ppermute(other, 'core', swap)]
    unnamed x10 -> x15, local copies, waits for them, and re-layouts: 13 us -> 18.9 us
    another operation x1 -> x2, local copies, waits for them, and re-layouts: 0.09 us -> 5.84 us  [the longest x1 5.74 us: parity(): jnp.stack([lax.dynamic_slice_in_dim(tokens, (2 * k + side) * own_rows, ow...]
    dot_general x2, matrix products: 16 us -> 10.4 us  [the longest x1 7.86 us: body(): lax.dot_general(their_unrotated, their_tokens, contract, preferred_elemen...]
    sub x1 -> x0, other arithmetic: 5.02 us -> none  [body(): master_out = master - outer_rate * (drift + outer_moment * momentum_out)]
  transfers between devices with their start and end apart: 4 -> 4, of which waited for: 2 -> 3; matrix products, arithmetic and copies ran while one was open for 6% -> 6% of each run, Pallas kernels for 0% -> 0%
where the time goes in v3:
time: 251 us
  waiting for transfers between devices  125 us (50%)
  blocking collectives  55.7 us (22%)
  local copies, waits for them, and re-layouts  26 us (10%)
  other arithmetic  18.2 us (7%)
  between operations  14.8 us (6%)
  matrix products  10.8 us (4%)
    unnamed x3, waiting for transfers between devices  81.5 us
    psum x1, blocking collectives, body(): lax.psum(local_tiles(island_drift, tile_rows, first_row), ('island', 'chi...  42.5 us
    psum x1, waiting for transfers between devices, body(): drift = lax.psum(island_drift, 'island') / replicas  41 us
    unnamed x15, local copies, waits for them, and re-layouts  18.9 us
    psum x1, blocking collectives, body(): squares = lax.psum(jnp.sum(gradient * gradient), ('chip', 'core'))  13.3 us
    dot_general x1, matrix products, body(): lax.dot_general(their_unrotated, their_tokens, contract, preferred_elemen...  7.86 us
    reduce_sum x1, other arithmetic, local_tiles(): jnp.sum(drift_rows, axis=1)  6.56 us
    another operation x1, local copies, waits for them, and re-layouts, parity(): jnp.stack([lax.dynamic_slice_in_dim(tokens, (2 * k + side) * own_rows, ow...  5.74 us
  transfers between devices with their start and end apart: 4, of which 3 were waited for; matrix products, arithmetic and copies ran while one was open for 6% of the time, Pallas kernels for 0%

profile of v3, /device:TPU:0, one launch (start us, length us, event | category | flops | bytes accessed | tf_op | source)
XLA Modules:
  0.0 250.9 jit_solution(4024872703927389999)
XLA Ops:
  7.2 0.0 reduce-scatter.4.cloned.1.call-start
  7.2 5.7 %dynamic-slice_bitcast_fusion.3 = (bf16[512,1,1024]{2,0,1:T(8,128)(2,1)S(1)}, bf16[512,1,1024]{2,0,1:T(8,128)(2,1)S(1)}, bf16[512,1,1024]{2,0,1:T(8,128)(2,1)S(1...) fusion(bf16[1,512,8192]{2,1,0:T(8,128)(2,1)} %param.8, ...), kind=kLoop, calls=%fused_computation.30 | loop fusion | bytes 16777248 | tf_op jit(solution)/shard_map/stack | solution.py:75
  13.0 2.2 pad_maximum_fusion
  15.2 0.5 collective-permute-start.1
  15.6 1.3 copy.44
  16.9 0.0 copy-start.1
  16.9 0.0 copy-start.2
  17.0 0.5 multiply_cosine_fusion
  17.5 0.2 add_convert_fusion
  17.7 0.1 collective-permute-start
  17.8 0.3 copy-done.1
  18.1 0.3 copy-done.2
  18.4 2.5 %fusion = f32[512,4,1024]{2,0,1:T(8,128)S(1)} fusion(bf16[512,512,1]{0,1,2:T(8,128)(2,1)S(1)} %bitcast.67, bf16[512,1,1024]{2,0,1:T(8,128)(2,1)S(1)} %get-tuple-element.16, bf16[512,1,1024]{2,0,1:T(8,128)(2,1)S(1)} %get-tuple-element.17, bf16[512,1,1024]{2,0,1:T(8,128)(2,1)S(1)} %copy-done.1, bf16[512,1,1024]{2,0,1:T(8,128)(2,1)S(1)} %copy-done.2), kind=kOutput, calls=%fused_computation | convolution fusion | flops 2164260864 | bytes 13107200 | tf_op jit(solution)/shard_map/dot_general | solution.py:86
  21.0 2.2 collective-permute-done
  23.2 0.0 collective-permute-done.1
  23.2 7.9 %convolution_add_fusion = f32[512,4,1024]{2,0,1:T(8,128)} fusion(f32[512,4,1024]{2,0,1:T(8,128)S(1)} %fusion, bf16[512,4,1024]{2,0,1:T(8,128)(2,1)} %collective-permute-done.1, bf16[512,512]{0,1:T(8,128)(2,1)S(1)} %collective-permute-done), kind=kOutput, calls=%fused_computation.10 | convolution fusion | flops 2149580800 | bytes 21495808 | tf_op jit(solution)/shard_map/dot_general | solution.py:88
  31.0 0.0 reduce-scatter.4.cloned.1.call-update
  31.1 0.0 all-reduce.3.cloned.1.call-start
  31.1 1.9 copy.40
  33.1 2.9 %copy.33 = f32[1,1024,512]{1,2,0:T(8,128)} copy(f32[1,1024,512]{2,1,0:T(8,128)} %param.12) | data formatting | bytes 4194304 | tf_op args[4]
  35.9 2.9 %copy.34 = f32[1,1024,512]{1,2,0:T(8,128)} copy(f32[1,1024,512]{2,1,0:T(8,128)} %param.13) | data formatting | bytes 4194304 | tf_op args[5]
  38.8 81.4 %reduce-scatter.4.cloned.1.call-done = f32[512,1,1024]{2,0,1:T(8,128)} async-done(((f32[512,4,1024]{2,0,1:T(8,128)}), f32[512,1,1024]{2,0,1:T(8,128)}) %reduce-scatter.4.cloned.1.call-update) | async-done | bytes 2097168
  120.3 2.7 %multiply_reduce_fusion = f32[]{:T(128)} fusion(f32[512,1,1024]{2,0,1:T(8,128)} %reduce-scatter.4.cloned.1.call-done), kind=kLoop, calls=%fused_computation.25 | loop fusion | flops 1048575 | bytes 2097156 | tf_op jit(solution)/shard_map/reduce_sum | solution.py:93
  123.0 2.9 %copy.37 = f32[1,1024,512]{1,2,0:T(8,128)} copy(f32[1,1024,512]{2,1,0:T(8,128)} %param.14) | data formatting | bytes 4194304 | tf_op args[6]
  125.9 13.3 %psum.21 = f32[]{:T(128)} all-reduce(f32[]{:T(128)} %multiply_reduce_fusion), channel_id=1, replica_groups=mesh['island'=4,'chip'=4,'core'=2] {'chip','core'}, use_global_device_ids=true, to_apply=%region_2.3 | all-reduce | flops 1 | bytes 8 | tf_op jit(solution)/shard_map/psum | solution.py:93
  139.8 6.6 %fusion.25 = (f32[1024]{0:T(1024)S(1)}, f32[1024,512]{0,1:T(8,128)}) fusion(f32[1024,512]{0,1:T(8,128)S(1)} %copy.40, f32[1,1024,512]{1,2,0:T(8,128)} %copy.37, f32[512,1,1024]{2,0,1:T(8,128)} %reduce-scatter.4.cloned.1.call-done, f32[]{:T(128)S(6)} %sqrt.9, f32[1,1024,512]{1,2,0:T(8,128)} %copy.34, f32[1,1024,512]{1,2,0:T(8,128)} %copy.33), kind=kLoop, calls=%fused_computation.55 | loop fusion | flops 9436160 | bytes 12587012 | tf_op jit(solution)/shard_map/reduce_sum | solution.py:52
  146.4 0.0 all-reduce.3.cloned.1.call-update
  146.4 0.0 copy-start.3
  146.4 2.9 %copy.39 = f32[1024,512]{0,1:T(8,128)} copy(f32[1024,512]{1,0:T(8,128)} %param.11) | data formatting | bytes 4194304 | tf_op args[3]
  149.3 0.0 copy-done.3
  149.3 0.1 copy.41
  149.4 0.1 reduce-window.8
  149.5 0.1 reduce.2
  149.6 0.4 convolution_bitcast_fusion
  150.0 42.5 %psum.23 = f32[48]{0:T(128)S(1)} all-reduce(f32[48]{0:T(128)S(1)} %convolution_bitcast_fusion), channel_id=1, replica_groups=mesh['island'=4,'chip'=4,'core'=2] {'island','chip','core'}, use_global_device_ids=true, to_apply=%region_6.7 | all-reduce | flops 48 | bytes 384 | tf_op jit(solution)/shard_map/psum | solution.py:103
  192.5 0.5 rsqrt_multiply_fusion
  193.0 41.0 %all-reduce.3.cloned.1.call-done = f32[1024,512]{0,1:T(8,128)} async-done(((f32[1024,512]{0,1:T(8,128)}), f32[1024,512]{0,1:T(8,128)}) %all-reduce.3.cloned.1.call-update) | async-done | bytes 2097168 | tf_op jit(solution)/shard_map/psum | solution.py:98
  234.0 5.2 %multiply_add_fusion = (f32[1024,512]{0,1:T(8,128)}, f32[1024,512]{0,1:T(8,128)}) fusion(f32[1024,512]{0,1:T(8,128)} %copy.39, f32[1024,512]{0,1:T(8,128)} %all-reduce.3.cloned.1.call-done, f32[1024,512]{0,1:T(8,128)S(1)} %copy.40), kind=kLoop, calls=%fused_computation.24 | loop fusion | flops 3670016 | bytes 10485760 | tf_op jit(solution)/shard_map/add | solution.py:99
  239.2 0.0 copy-start
  239.2 3.0 %copy.42 = f32[1024,512]{1,0:T(8,128)} copy(f32[1024,512]{0,1:T(8,128)} %get-tuple-element.23) | data formatting | bytes 4194304
  242.2 0.0 copy-done
  242.2 1.8 copy.43
  (5 shorter events, 0.1 us)
Async XLA Ops:
  7.2 113.1 %reduce-scatter.4.cloned.1.call-start = ((), (), s32[]{:S(2)}) async-start(), calls=%async_computation.2 | async-start | bytes 10485760
  15.2 8.0 %collective-permute-start.1 = (bf16[512,4,1024]{2,0,1:T(8,128)(2,1)}, bf16[512,4,1024]{2,0,1:T(8,128)(2,1)}, u32[]{:S(2)}, u32[]{:S(2)}) collective-permute-start(bf16[512,4,1024]{2,0,1:T(8,128)(2,1)} %pad_maximum_fusion), channel_id=1, source_target_pairs={{0,1},{1,0},{2,3},{3,2},{4,5},{5,4},{6,7},{7,6},{8,9},{9,8},{10,11... | collective-permute-start | bytes 12582920 | tf_op jit(solution)/shard_map/ppermute | solution.py:83
  16.9 1.2 copy-start.1
  16.9 1.5 copy-start.2
  17.7 5.5 %collective-permute-start = (bf16[512,512]{0,1:T(8,128)(2,1)S(1)}, bf16[512,512]{0,1:T(8,128)(2,1)S(1)}, u32[]{:S(2)}, u32[]{:S(2)}) collective-permute-start(bf16[512,512]{0,1:T(8,128)(2,1)S(1)} %bitcast.66), channel_id=1, source_target_pairs={{0,1},{1,0},{2,3},{3,2},{4,5},{5,4},{6,7},{7,6},{8,9},{9,8},{10,11... | collective-permute-start | bytes 1572872 | tf_op jit(solution)/shard_map/ppermute | solution.py:84
  31.1 202.9 %all-reduce.3.cloned.1.call-start = ((), (), s32[]{:S(2)}) async-start(), calls=%async_computation.1 | async-start | bytes 4194304 | tf_op jit(solution)/shard_map/psum | solution.py:98
  146.4 2.9 %copy-start.3 = (s32[48]{0:T(128)S(1)}, s32[48]{0:T(128)}, u32[]{:S(2)}) copy-start(s32[48]{0:T(128)} %param.15) | copy-start | bytes 580
  239.2 3.0 %copy-start = (f32[1024,512]{0,1:T(8,128)S(1)}, f32[1024,512]{0,1:T(8,128)}, u32[]{:S(2)}) copy-start(f32[1024,512]{0,1:T(8,128)} %get-tuple-element.22) | copy-start | bytes 6291460
Sparse Core Ops, SparseCore 0:
  31.2 89.0 reduce-scatter.3
  146.5 87.4 all-reduce.2

commit v4 on v3

--- a/solution.py
+++ b/solution.py
@@ -1,6 +1,7 @@
 import jax
 import jax.numpy as jnp
 from jax import lax
+from jax.experimental.layout import Layout, with_layout_constraint
 from jax.sharding import PartitionSpec as P
 
 HEAD = 128
@@ -88,8 +89,11 @@
     ) + lax.dot_general(
         their_unrotated, their_tokens, contract, preferred_element_type=jnp.float32
     )
+    partial = with_layout_constraint(partial, Layout((1, 2, 0)))
     gradient = lax.psum_scatter(partial, "chip", scatter_dimension=1, tiled=True)
-    gradient = gradient.reshape(gradient.shape[0], own_rows).T
+    gradient = with_layout_constraint(
+        gradient.reshape(gradient.shape[0], own_rows).T, Layout((0, 1))
+    )
     squares = lax.psum(jnp.sum(gradient * gradient), ("chip", "core"))
     factor = 1.0 / jnp.sqrt(squares + norm_epsilon)
     inner = adam_update(gradient * factor, island_weights[0], first_moment[0], second_moment[0])

time: 251 us -> 263 us (1.048)
  waiting for transfers between devices: 125 us -> 133 us
  other arithmetic: 18.2 us -> 21.4 us
    dynamic_slice x0 -> x9, local copies, waits for them, and re-layouts: none -> 20.9 us  [parity(): lax.dynamic_slice_in_dim(tokens, (2 * k + side) * own_rows, own_rows, axi...]
    unnamed x15 -> x11, local copies, waits for them, and re-layouts: 18.9 us -> 1.58 us
    unnamed x3, waiting for transfers between devices: 81.5 us -> 89.2 us
    another operation x2 -> x1, local copies, waits for them, and re-layouts: 5.84 us -> 0.09 us  [the longest x1 5.74 us: parity(): jnp.stack([lax.dynamic_slice_in_dim(tokens, (2 * k + side) * own_rows, ow...]
    add x1 -> x0, other arithmetic: 5.19 us -> none  [body(): momentum_out = outer_moment * momentum + drift]
    sub x0 -> x1, other arithmetic: none -> 5.02 us  [body(): master_out = master - outer_rate * (drift + outer_moment * momentum_out)]
  transfers between devices with their start and end apart: 4 -> 4, of which waited for: 3 -> 2; matrix products, arithmetic and copies ran while one was open for 6% -> 7% of each run, Pallas kernels for 0% -> 0%
where the time goes in v4:
time: 263 us; the launch traced here: 262 us
  waiting for transfers between devices  133 us (51%)
  blocking collectives  55.8 us (21%)
  local copies, waits for them, and re-layouts  24.9 us (9%)
  other arithmetic  21.4 us (8%)
  between operations  14.8 us (6%)
  matrix products  12.2 us (5%)
    unnamed x3, waiting for transfers between devices  89.2 us
    psum x1, waiting for transfers between devices, body(): drift = lax.psum(island_drift, 'island') / replicas  43.5 us
    psum x1, blocking collectives, body(): lax.psum(local_tiles(island_drift, tile_rows, first_row), ('island', 'chi...  42.3 us
    dynamic_slice x9, local copies, waits for them, and re-layouts, parity(): lax.dynamic_slice_in_dim(tokens, (2 * k + side) * own_rows, own_rows, axi...  20.9 us
    psum x1, blocking collectives, body(): squares = lax.psum(jnp.sum(gradient * gradient), ('chip', 'core'))  13.5 us
    dot_general x1, matrix products, body(): lax.dot_general(their_unrotated, their_tokens, contract, preferred_elemen...  7.91 us
    reduce_sum x1, other arithmetic, local_tiles(): jnp.sum(drift_rows, axis=1)  6.65 us
  transfers between devices with their start and end apart: 4, of which 2 were waited for; matrix products, arithmetic and copies ran while one was open for 7% of the time, Pallas kernels for 0%

profile of v4, /device:TPU:0, one launch (start us, length us, event | category | flops | bytes accessed | tf_op | source)
XLA Modules:
  0.0 262.5 jit_solution(13055974338753780336)
XLA Ops:
  7.2 0.0 reduce-scatter.4.cloned.1.call-start
  7.2 6.3 %constant_dynamic-slice_fusion.3 = (bf16[1,512,1024]{2,1,0:T(8,128)(2,1)}, bf16[1,512,1024]{2,1,0:T(8,128)(2,1)}, bf16[1,512,1024]{2,1,0:T(8,128)(2,1)S(1)}, bf1...) fusion(bf16[1,512,8192]{2,1,0:T(8,128)(2,1)} %param.8, ...), kind=kLoop, calls=%fused_computation.49 | loop fusion | bytes 16777248 | tf_op jit(solution)/shard_map/dynamic_slice | solution.py:78
  13.5 2.3 copy.36
  15.8 2.4 copy.33
  18.2 2.3 copy.34
  20.5 1.3 copy.35
  21.8 3.7 %pad_maximum_fusion = bf16[512,4,1024]{0,2,1:T(8,128)(2,1)} fusion(bf16[512,1,1024]{0,2,1:T(8,128)(2,1)} %bitcast.58, bf16[512,1,1024]{0,2,1:T(8,128)(2,1)} %bitcast.61, bf16[512,1,1024]{0,2,1:T(8,128)(2,1)} %bitcast.60, bf16[512,1,1024]{0,2,1:T(8,128)(2,1)} %bitcast.59), kind=kLoop, calls=%fused_computation.8 | loop fusion | flops 6291456 | bytes 8388608 | tf_op jit(solution)/shard_map/stack | solution.py:76
  25.5 0.5 collective-permute-start.1
  26.0 1.4 reshape.135
  27.4 1.0 multiply_cosine_fusion
  28.4 0.9 add_convert_fusion
  29.3 0.7 pad_maximum_fusion.1
  30.0 0.9 copy.40
  30.9 0.1 collective-permute-start
  31.0 1.0 reshape.136
  31.9 0.0 copy-start.1
  31.9 2.4 copy.29
  34.3 0.0 copy-done.1
  34.3 1.3 copy.30
  35.7 0.0 copy-start.2
  35.7 1.3 copy.31
  37.0 0.0 copy-start.3
  37.0 1.3 copy.32
  38.3 0.0 copy-done.2
  38.3 0.0 copy-done.3
  38.3 3.9 %fusion = f32[512,4,1024]{0,2,1:T(8,128)S(1)} fusion(bf16[512,512,1]{1,0,2:T(8,128)(2,1)} %reshape.136, bf16[512,1,1024]{0,2,1:T(8,128)(2,1)} %bitcast.65, bf16[512,1,1024]{0,2,1:T(8,128)(2,1)} %bitcast.64, bf16[512,1,1024]{0,2,1:T(8,128)(2,1)S(1)} %bitcast.63, bf16[512,1,1024]{0,2,1:T(8,128)(2,1)S(1)} %bitcast.62), kind=kOutput, calls=%fused_computation | convolution fusion | flops 2164260864 | bytes 13107200 | tf_op jit(solution)/shard_map/dot_general | solution.py:87
  42.2 0.0 collective-permute-done
  42.2 0.0 collective-permute-done.1
  42.2 7.9 %convolution_add_fusion = f32[512,4,1024]{0,2,1:T(8,128)} fusion(f32[512,4,1024]{0,2,1:T(8,128)S(1)} %fusion, bf16[512,4,1024]{0,2,1:T(8,128)(2,1)} %collective-permute-done.1, bf16[512,512]{1,0:T(8,128)(2,1)} %collective-permute-done), kind=kOutput, calls=%fused_computation.10 | convolution fusion | flops 2149580800 | bytes 21495808 | tf_op jit(solution)/shard_map/dot_general | solution.py:89
  50.2 0.0 reduce-scatter.4.cloned.1.call-update
  50.2 0.0 copy-start
  50.2 0.0 all-reduce.3.cloned.1.call-start
  50.2 89.2 %reduce-scatter.4.cloned.1.call-done = f32[512,1,1024]{0,2,1:T(8,128)} async-done(((f32[512,4,1024]{0,2,1:T(8,128)}), f32[512,1,1024]{0,2,1:T(8,128)}) %reduce-scatter.4.cloned.1.call-update) | async-done | bytes 2097168
  139.4 2.7 %fusion.14 = f32[]{:T(128)} fusion(f32[512,1,1024]{0,2,1:T(8,128)} %reduce-scatter.4.cloned.1.call-done), kind=kLoop, calls=%fused_computation.19 | loop fusion | flops 1048575 | bytes 2097156 | tf_op jit(solution)/shard_map/reduce_sum | solution.py:97
  142.2 13.5 %psum.21 = f32[]{:T(128)} all-reduce(f32[]{:T(128)} %fusion.14), channel_id=1, replica_groups=mesh['island'=4,'chip'=4,'core'=2] {'chip','core'}, use_global_device_ids=true, to_apply=%region_2.3 | all-reduce | flops 1 | bytes 8 | tf_op jit(solution)/shard_map/psum | solution.py:97
  156.3 0.0 copy-done
  156.3 6.6 %fusion.25 = (f32[1024]{0:T(1024)S(1)}, f32[1024,512]{1,0:T(8,128)}) fusion(f32[1024,512]{1,0:T(8,128)S(1)} %copy-done, f32[1,1024,512]{2,1,0:T(8,128)} %param.14, f32[]{:T(128)S(6)} %sqrt.9, f32[512,1,1024]{0,2,1:T(8,128)} %reduce-scatter.4.cloned.1.call-done, f32[1,1024,512]{2,1,0:T(8,128)} %param.13, f32[1,1024,512]{2,1,0:T(8,128)} %param.12), kind=kLoop, calls=%fused_computation.57 | loop fusion | flops 9436160 | bytes 12587012 | tf_op jit(solution)/shard_map/reduce_sum | solution.py:53
  163.0 0.0 copy-start.4
  163.0 0.0 all-reduce.3.cloned.1.call-update
  163.0 0.6 copy-done.4
  163.6 0.1 copy.37
  163.7 0.1 reduce-window.8
  163.8 0.1 reduce
  163.9 0.4 convolution_bitcast_fusion
  164.3 42.3 %psum.23 = f32[48]{0:T(128)S(1)} all-reduce(f32[48]{0:T(128)S(1)} %convolution_bitcast_fusion), channel_id=1, replica_groups=mesh['island'=4,'chip'=4,'core'=2] {'island','chip','core'}, use_global_device_ids=true, to_apply=%region_6.7 | all-reduce | flops 48 | bytes 384 | tf_op jit(solution)/shard_map/psum | solution.py:107
  206.6 0.5 rsqrt_multiply_fusion
  207.1 43.5 %all-reduce.3.cloned.1.call-done = f32[1024,512]{1,0:T(8,128)} async-done(((f32[1024,512]{1,0:T(8,128)}), f32[1024,512]{1,0:T(8,128)}) %all-reduce.3.cloned.1.call-update) | async-done | bytes 2097168 | tf_op jit(solution)/shard_map/psum | solution.py:102
  250.6 5.0 %multiply_subtract_fusion = (f32[1024,512]{1,0:T(8,128)}, f32[1024,512]{1,0:T(8,128)}) fusion(f32[1024,512]{1,0:T(8,128)S(1)} %copy-done, f32[1024,512]{1,0:T(8,128)} %all-reduce.3.cloned.1.call-done, f32[1024,512]{1,0:T(8,128)} %param.11), kind=kLoop, calls=%fused_computation.25 | loop fusion | flops 3670016 | bytes 10485760 | tf_op jit(solution)/shard_map/sub | solution.py:104
  (4 shorter events, 0.0 us)
Async XLA Ops:
  7.2 132.3 %reduce-scatter.4.cloned.1.call-start = ((), (), s32[]{:S(2)}) async-start(), calls=%async_computation.2 | async-start | bytes 10485760
  25.5 16.7 %collective-permute-start.1 = (bf16[512,4,1024]{0,2,1:T(8,128)(2,1)}, bf16[512,4,1024]{0,2,1:T(8,128)(2,1)}, u32[]{:S(2)}, u32[]{:S(2)}) collective-permute-start(bf16[512,4,1024]{0,2,1:T(8,128)(2,1)} %pad_maximum_fusion), channel_id=1, source_target_pairs={{0,1},{1,0},{2,3},{3,2},{4,5},{5,4},{6,7},{7,6},{8,9},{9,8},{10,11... | collective-permute-start | bytes 12582920 | tf_op jit(solution)/shard_map/ppermute | solution.py:84
  30.9 11.3 %collective-permute-start = (bf16[512,512]{1,0:T(8,128)(2,1)}, bf16[512,512]{1,0:T(8,128)(2,1)}, u32[]{:S(2)}, u32[]{:S(2)}) collective-permute-start(bf16[512,512]{1,0:T(8,128)(2,1)} %bitcast.56), channel_id=1, source_target_pairs={{0,1},{1,0},{2,3},{3,2},{4,5},{5,4},{6,7},{7,6},{8,9},{9,8},{10,11... | collective-permute-start | bytes 1572872 | tf_op jit(solution)/shard_map/ppermute | solution.py:85
  31.9 2.4 copy-start.1
  35.7 2.6 %copy-start.2 = (bf16[1,512,1024]{1,2,0:T(8,128)(2,1)S(1)}, bf16[1,512,1024]{1,2,0:T(8,128)(2,1)}, u32[]{:S(2)}) copy-start(bf16[1,512,1024]{1,2,0:T(8,128)(2,1)} %copy.29) | copy-start | bytes 3145732
  37.0 1.3 copy-start.3
  50.2 106.2 %copy-start = (f32[1024,512]{1,0:T(8,128)S(1)}, f32[1024,512]{1,0:T(8,128)}, u32[]{:S(2)}) copy-start(f32[1024,512]{1,0:T(8,128)} %param.10) | copy-start | bytes 6291460
  50.2 200.4 %all-reduce.3.cloned.1.call-start = ((), (), s32[]{:S(2)}) async-start(), calls=%async_computation.1 | async-start | bytes 4194304 | tf_op jit(solution)/shard_map/psum | solution.py:102
  163.0 0.7 copy-start.4
Sparse Core Ops, SparseCore 0:
  50.3 89.0 reduce-scatter.3
  163.1 87.4 all-reduce.2

commit v5 on v4

--- a/solution.py
+++ b/solution.py
@@ -89,8 +89,8 @@
     ) + lax.dot_general(
         their_unrotated, their_tokens, contract, preferred_element_type=jnp.float32
     )
-    partial = with_layout_constraint(partial, Layout((1, 2, 0)))
     gradient = lax.psum_scatter(partial, "chip", scatter_dimension=1, tiled=True)
+    gradient = with_layout_constraint(gradient, Layout((0, 1, 2)))
     gradient = with_layout_constraint(
         gradient.reshape(gradient.shape[0], own_rows).T, Layout((0, 1))
     )

time: 263 us -> 244 us (0.928)
  local copies, waits for them, and re-layouts: 24.9 us -> 10.2 us
  other arithmetic: 21.4 us -> 16.5 us
    dynamic_slice x9 -> x0, local copies, waits for them, and re-layouts: 20.9 us -> none  [parity(): lax.dynamic_slice_in_dim(tokens, (2 * k + side) * own_rows, own_rows, axi...]
    another operation x1 -> x3, local copies, waits for them, and re-layouts: 0.09 us -> 7.75 us  [the longest x1 5.74 us: parity(): jnp.stack([lax.dynamic_slice_in_dim(tokens, (2 * k + side) * own_rows, ow...]
  transfers between devices with their start and end apart: 4 -> 4, of which waited for: 2 -> 3; matrix products, arithmetic and copies ran while one was open for 7% -> 2% of each run, Pallas kernels for 0% -> 0%
where the time goes in v5:
time: 244 us; the launch traced here: 243 us
  waiting for transfers between devices  135 us (55%)
  blocking collectives  55.6 us (23%)
  other arithmetic  16.5 us (7%)
  between operations  14.8 us (6%)
  matrix products  10.8 us (4%)
  local copies, waits for them, and re-layouts  10.2 us (4%)
    unnamed x3, waiting for transfers between devices  89.2 us
    psum x1, waiting for transfers between devices, body(): drift = lax.psum(island_drift, 'island') / replicas  43.5 us
    psum x1, blocking collectives, body(): lax.psum(local_tiles(island_drift, tile_rows, first_row), ('island', 'chi...  42.3 us
    psum x1, blocking collectives, body(): squares = lax.psum(jnp.sum(gradient * gradient), ('chip', 'core'))  13.3 us
    dot_general x1, matrix products, body(): lax.dot_general(their_unrotated, their_tokens, contract, preferred_elemen...  7.86 us
    reduce_sum x1, other arithmetic, local_tiles(): jnp.sum(drift_rows, axis=1)  6.65 us
    another operation x1, local copies, waits for them, and re-layouts, parity(): jnp.stack([lax.dynamic_slice_in_dim(tokens, (2 * k + side) * own_rows, ow...  5.74 us
    sub x1, other arithmetic, body(): master_out = master - outer_rate * (drift + outer_moment * momentum_out)  5.02 us
  transfers between devices with their start and end apart: 4, of which 3 were waited for; matrix products, arithmetic and copies ran while one was open for 2% of the time, Pallas kernels for 0%

profile of v5, /device:TPU:0, one launch (start us, length us, event | category | flops | bytes accessed | tf_op | source)
XLA Modules:
  0.0 243.4 jit_solution(14641525735417198936)
XLA Ops:
  7.2 0.0 reduce-scatter.4.cloned.1.call-start
  7.2 5.7 %dynamic-slice_bitcast_fusion.3 = (bf16[512,1,1024]{2,0,1:T(8,128)(2,1)S(1)}, bf16[512,1,1024]{2,0,1:T(8,128)(2,1)S(1)}, bf16[512,1,1024]{2,0,1:T(8,128)(2,1)S(1...) fusion(bf16[1,512,8192]{2,1,0:T(8,128)(2,1)} %param.8, ...), kind=kLoop, calls=%fused_computation.31 | loop fusion | bytes 16777248 | tf_op jit(solution)/shard_map/stack | solution.py:76
  13.0 2.2 pad_maximum_fusion
  15.2 0.5 collective-permute-start.1
  15.6 1.3 copy.29
  16.9 0.0 copy-start.1
  16.9 0.0 copy-start.2
  17.0 0.5 multiply_cosine_fusion
  17.5 0.2 add_convert_fusion
  17.7 0.1 collective-permute-start
  17.8 0.3 copy-done.1
  18.1 0.3 copy-done.2
  18.4 2.5 %fusion = f32[512,4,1024]{2,0,1:T(8,128)S(1)} fusion(bf16[512,512,1]{0,1,2:T(8,128)(2,1)S(1)} %bitcast.67, bf16[512,1,1024]{2,0,1:T(8,128)(2,1)S(1)} %get-tuple-element.9, bf16[512,1,1024]{2,0,1:T(8,128)(2,1)S(1)} %get-tuple-element.10, bf16[512,1,1024]{2,0,1:T(8,128)(2,1)S(1)} %copy-done.1, bf16[512,1,1024]{2,0,1:T(8,128)(2,1)S(1)} %copy-done.2), kind=kOutput, calls=%fused_computation | convolution fusion | flops 2164260864 | bytes 13107200 | tf_op jit(solution)/shard_map/dot_general | solution.py:87
  21.0 2.2 collective-permute-done
  23.2 0.0 collective-permute-done.1
  23.2 7.9 %convolution_add_fusion = f32[512,4,1024]{2,0,1:T(8,128)} fusion(f32[512,4,1024]{2,0,1:T(8,128)S(1)} %fusion, bf16[512,4,1024]{2,0,1:T(8,128)(2,1)} %collective-permute-done.1, bf16[512,512]{0,1:T(8,128)(2,1)S(1)} %collective-permute-done), kind=kOutput, calls=%fused_computation.10 | convolution fusion | flops 2149580800 | bytes 21495808 | tf_op jit(solution)/shard_map/dot_general | solution.py:89
  31.0 0.0 reduce-scatter.4.cloned.1.call-update
  31.1 0.0 all-reduce.3.cloned.1.call-start
  31.1 89.1 %reduce-scatter.4.cloned.1.call-done = f32[512,1,1024]{2,0,1:T(8,128)} async-done(((f32[512,4,1024]{2,0,1:T(8,128)}), f32[512,1,1024]{2,0,1:T(8,128)}) %reduce-scatter.4.cloned.1.call-update) | async-done | bytes 2097168
  120.3 1.9 copy.26
  122.2 1.1 fusion.14
  123.3 13.3 %psum.21 = f32[]{:T(128)} all-reduce(f32[]{:T(128)} %fusion.14), channel_id=1, replica_groups=mesh['island'=4,'chip'=4,'core'=2] {'chip','core'}, use_global_device_ids=true, to_apply=%region_2.3 | all-reduce | flops 1 | bytes 8 | tf_op jit(solution)/shard_map/psum | solution.py:97
  137.3 6.6 %fusion.25 = (f32[1024]{0:T(1024)S(1)}, f32[1024,512]{1,0:T(8,128)}) fusion(f32[1024,512]{1,0:T(8,128)} %param.10, f32[1,1024,512]{2,1,0:T(8,128)} %param.14, f32[]{:T(128)S(6)} %sqrt.9, f32[512,1,1024]{0,2,1:T(8,128)S(1)} %copy.26, f32[1,1024,512]{2,1,0:T(8,128)} %param.13, f32[1,1024,512]{2,1,0:T(8,128)} %param.12), kind=kLoop, calls=%fused_computation.56 | loop fusion | flops 9436160 | bytes 12587012 | tf_op jit(solution)/shard_map/reduce_sum | solution.py:53
  143.9 0.0 copy-start.3
  143.9 0.0 copy-start
  143.9 0.0 all-reduce.3.cloned.1.call-update
  144.0 0.6 copy-done.3
  144.6 0.1 copy.27
  144.7 0.1 reduce-window.8
  144.8 0.1 reduce
  144.9 0.4 convolution_bitcast_fusion
  145.3 42.3 %psum.23 = f32[48]{0:T(128)S(1)} all-reduce(f32[48]{0:T(128)S(1)} %convolution_bitcast_fusion), channel_id=1, replica_groups=mesh['island'=4,'chip'=4,'core'=2] {'island','chip','core'}, use_global_device_ids=true, to_apply=%region_6.7 | all-reduce | flops 48 | bytes 384 | tf_op jit(solution)/shard_map/psum | solution.py:107
  187.6 0.5 rsqrt_multiply_fusion
  188.1 43.5 %all-reduce.3.cloned.1.call-done = f32[1024,512]{1,0:T(8,128)} async-done(((f32[1024,512]{1,0:T(8,128)}), f32[1024,512]{1,0:T(8,128)}) %all-reduce.3.cloned.1.call-update) | async-done | bytes 2097168 | tf_op jit(solution)/shard_map/psum | solution.py:102
  231.6 0.0 copy-done
  231.6 5.0 %multiply_subtract_fusion = (f32[1024,512]{1,0:T(8,128)}, f32[1024,512]{1,0:T(8,128)}) fusion(f32[1024,512]{1,0:T(8,128)S(1)} %copy-done, f32[1024,512]{1,0:T(8,128)} %all-reduce.3.cloned.1.call-done, f32[1024,512]{1,0:T(8,128)} %param.11), kind=kLoop, calls=%fused_computation.25 | loop fusion | flops 3670016 | bytes 10485760 | tf_op jit(solution)/shard_map/sub | solution.py:104
  (5 shorter events, 0.1 us)
Async XLA Ops:
  7.2 113.1 %reduce-scatter.4.cloned.1.call-start = ((), (), s32[]{:S(2)}) async-start(), calls=%async_computation.2 | async-start | bytes 10485760
  15.2 8.0 %collective-permute-start.1 = (bf16[512,4,1024]{2,0,1:T(8,128)(2,1)}, bf16[512,4,1024]{2,0,1:T(8,128)(2,1)}, u32[]{:S(2)}, u32[]{:S(2)}) collective-permute-start(bf16[512,4,1024]{2,0,1:T(8,128)(2,1)} %pad_maximum_fusion), channel_id=1, source_target_pairs={{0,1},{1,0},{2,3},{3,2},{4,5},{5,4},{6,7},{7,6},{8,9},{9,8},{10,11... | collective-permute-start | bytes 12582920 | tf_op jit(solution)/shard_map/ppermute | solution.py:84
  16.9 1.2 copy-start.1
  16.9 1.5 copy-start.2
  17.7 5.5 %collective-permute-start = (bf16[512,512]{0,1:T(8,128)(2,1)S(1)}, bf16[512,512]{0,1:T(8,128)(2,1)S(1)}, u32[]{:S(2)}, u32[]{:S(2)}) collective-permute-start(bf16[512,512]{0,1:T(8,128)(2,1)S(1)} %bitcast.66), channel_id=1, source_target_pairs={{0,1},{1,0},{2,3},{3,2},{4,5},{5,4},{6,7},{7,6},{8,9},{9,8},{10,11... | collective-permute-start | bytes 1572872 | tf_op jit(solution)/shard_map/ppermute | solution.py:85
  31.1 200.5 %all-reduce.3.cloned.1.call-start = ((), (), s32[]{:S(2)}) async-start(), calls=%async_computation.1 | async-start | bytes 4194304 | tf_op jit(solution)/shard_map/psum | solution.py:102
  143.9 0.7 copy-start.3
  143.9 87.6 %copy-start = (f32[1024,512]{1,0:T(8,128)S(1)}, f32[1024,512]{1,0:T(8,128)}, u32[]{:S(2)}) copy-start(f32[1024,512]{1,0:T(8,128)} %param.10) | copy-start | bytes 6291460
Sparse Core Ops, SparseCore 0:
  31.2 89.0 reduce-scatter.3
  144.1 87.4 all-reduce.2

commit v6 on v5

--- a/solution.py
+++ b/solution.py
@@ -94,7 +94,7 @@
     gradient = with_layout_constraint(
         gradient.reshape(gradient.shape[0], own_rows).T, Layout((0, 1))
     )
-    squares = lax.psum(jnp.sum(gradient * gradient), ("chip", "core"))
+    squares = lax.psum(lax.psum(jnp.sum(gradient * gradient), "core"), "chip")
     factor = 1.0 / jnp.sqrt(squares + norm_epsilon)
     inner = adam_update(gradient * factor, island_weights[0], first_moment[0], second_moment[0])
     island_drift = master - inner

time: 244 us -> 243 us (level)
    psum x1 -> x2, blocking collectives: 13.3 us -> 12.6 us  [body(): squares = lax.psum(lax.psum(jnp.sum(gradient * gradient), 'core'), 'chip')]
where the time goes in v6:
time: 243 us
  waiting for transfers between devices  135 us (56%)
  blocking collectives  54.9 us (23%)
  other arithmetic  16.5 us (7%)
  between operations  14.8 us (6%)
  matrix products  10.8 us (4%)
  local copies, waits for them, and re-layouts  10.2 us (4%)
    unnamed x3, waiting for transfers between devices  89.2 us
    psum x1, waiting for transfers between devices, body(): drift = lax.psum(island_drift, 'island') / replicas  43.5 us
    psum x1, blocking collectives, body(): lax.psum(local_tiles(island_drift, tile_rows, first_row), ('island', 'chi...  42.3 us
    psum x2, blocking collectives, body(): squares = lax.psum(lax.psum(jnp.sum(gradient * gradient), 'core'), 'chip')  12.6 us
    dot_general x1, matrix products, body(): lax.dot_general(their_unrotated, their_tokens, contract, preferred_elemen...  7.86 us
    reduce_sum x1, other arithmetic, local_tiles(): jnp.sum(drift_rows, axis=1)  6.65 us
    another operation x1, local copies, waits for them, and re-layouts, parity(): jnp.stack([lax.dynamic_slice_in_dim(tokens, (2 * k + side) * own_rows, ow...  5.74 us
    sub x1, other arithmetic, body(): master_out = master - outer_rate * (drift + outer_moment * momentum_out)  5.02 us
  transfers between devices with their start and end apart: 4, of which 3 were waited for; matrix products, arithmetic and copies ran while one was open for 2% of the time, Pallas kernels for 0%

profile of v6, /device:TPU:0, one launch (start us, length us, event | category | flops | bytes accessed | tf_op | source)
XLA Modules:
  0.0 242.7 jit_solution(495265386519610267)
XLA Ops:
  7.2 0.0 reduce-scatter.4.cloned.1.call-start
  7.2 5.7 %dynamic-slice_bitcast_fusion.3 = (bf16[512,1,1024]{2,0,1:T(8,128)(2,1)S(1)}, bf16[512,1,1024]{2,0,1:T(8,128)(2,1)S(1)}, bf16[512,1,1024]{2,0,1:T(8,128)(2,1)S(1...) fusion(bf16[1,512,8192]{2,1,0:T(8,128)(2,1)} %param.8, ...), kind=kLoop, calls=%fused_computation.31 | loop fusion | bytes 16777248 | tf_op jit(solution)/shard_map/stack | solution.py:76
  13.0 2.2 pad_maximum_fusion
  15.2 0.5 collective-permute-start.1
  15.6 1.3 copy.29
  16.9 0.0 copy-start.1
  16.9 0.0 copy-start.2
  17.0 0.5 multiply_cosine_fusion
  17.5 0.2 add_convert_fusion
  17.7 0.1 collective-permute-start
  17.8 0.3 copy-done.1
  18.1 0.3 copy-done.2
  18.4 2.5 %fusion = f32[512,4,1024]{2,0,1:T(8,128)S(1)} fusion(bf16[512,512,1]{0,1,2:T(8,128)(2,1)S(1)} %bitcast.67, bf16[512,1,1024]{2,0,1:T(8,128)(2,1)S(1)} %get-tuple-element.9, bf16[512,1,1024]{2,0,1:T(8,128)(2,1)S(1)} %get-tuple-element.10, bf16[512,1,1024]{2,0,1:T(8,128)(2,1)S(1)} %copy-done.1, bf16[512,1,1024]{2,0,1:T(8,128)(2,1)S(1)} %copy-done.2), kind=kOutput, calls=%fused_computation | convolution fusion | flops 2164260864 | bytes 13107200 | tf_op jit(solution)/shard_map/dot_general | solution.py:87
  21.0 2.2 collective-permute-done
  23.2 0.0 collective-permute-done.1
  23.2 7.9 %convolution_add_fusion = f32[512,4,1024]{2,0,1:T(8,128)} fusion(f32[512,4,1024]{2,0,1:T(8,128)S(1)} %fusion, bf16[512,4,1024]{2,0,1:T(8,128)(2,1)} %collective-permute-done.1, bf16[512,512]{0,1:T(8,128)(2,1)S(1)} %collective-permute-done), kind=kOutput, calls=%fused_computation.10 | convolution fusion | flops 2149580800 | bytes 21495808 | tf_op jit(solution)/shard_map/dot_general | solution.py:89
  31.0 0.0 reduce-scatter.4.cloned.1.call-update
  31.1 0.0 all-reduce.3.cloned.1.call-start
  31.1 89.1 %reduce-scatter.4.cloned.1.call-done = f32[512,1,1024]{2,0,1:T(8,128)} async-done(((f32[512,4,1024]{2,0,1:T(8,128)}), f32[512,1,1024]{2,0,1:T(8,128)}) %reduce-scatter.4.cloned.1.call-update) | async-done | bytes 2097168
  120.3 1.9 copy.26
  122.2 1.1 fusion.14
  123.3 3.1 %psum.28 = f32[]{:T(128)} all-reduce(f32[]{:T(128)} %fusion.14), channel_id=1, replica_groups=mesh['island'=4,'chip'=4,'core'=2] {'core'}, use_global_device_ids=true, to_apply=%region_2.3 | all-reduce | flops 1 | bytes 8 | tf_op jit(solution)/shard_map/psum | solution.py:97
  126.4 9.5 %psum.29 = f32[]{:T(128)} all-reduce(f32[]{:T(128)} %psum.28), channel_id=1, replica_groups=mesh['island'=4,'chip'=4,'core'=2] {'chip'}, use_global_device_ids=true, to_apply=%region_3.4 | all-reduce | flops 1 | bytes 8 | tf_op jit(solution)/shard_map/psum | solution.py:97
  136.6 6.6 %fusion.25 = (f32[1024]{0:T(1024)S(1)}, f32[1024,512]{1,0:T(8,128)}) fusion(f32[1024,512]{1,0:T(8,128)} %param.10, f32[1,1024,512]{2,1,0:T(8,128)} %param.14, f32[]{:T(128)S(6)} %sqrt.9, f32[512,1,1024]{0,2,1:T(8,128)S(1)} %copy.26, f32[1,1024,512]{2,1,0:T(8,128)} %param.13, f32[1,1024,512]{2,1,0:T(8,128)} %param.12), kind=kLoop, calls=%fused_computation.56 | loop fusion | flops 9436160 | bytes 12587012 | tf_op jit(solution)/shard_map/reduce_sum | solution.py:53
  143.3 0.0 copy-start.3
  143.3 0.0 copy-start
  143.3 0.0 all-reduce.3.cloned.1.call-update
  143.3 0.6 copy-done.3
  143.9 0.1 copy.27
  144.0 0.1 reduce-window.8
  144.1 0.1 reduce
  144.2 0.4 convolution_bitcast_fusion
  144.6 42.3 %psum.31 = f32[48]{0:T(128)S(1)} all-reduce(f32[48]{0:T(128)S(1)} %convolution_bitcast_fusion), channel_id=1, replica_groups=mesh['island'=4,'chip'=4,'core'=2] {'island','chip','core'}, use_global_device_ids=true, to_apply=%region_7.8 | all-reduce | flops 48 | bytes 384 | tf_op jit(solution)/shard_map/psum | solution.py:107
  186.9 0.5 rsqrt_multiply_fusion
  187.4 43.5 %all-reduce.3.cloned.1.call-done = f32[1024,512]{1,0:T(8,128)} async-done(((f32[1024,512]{1,0:T(8,128)}), f32[1024,512]{1,0:T(8,128)}) %all-reduce.3.cloned.1.call-update) | async-done | bytes 2097168 | tf_op jit(solution)/shard_map/psum | solution.py:102
  230.9 0.0 copy-done
  230.9 5.0 %multiply_subtract_fusion = (f32[1024,512]{1,0:T(8,128)}, f32[1024,512]{1,0:T(8,128)}) fusion(f32[1024,512]{1,0:T(8,128)S(1)} %copy-done, f32[1024,512]{1,0:T(8,128)} %all-reduce.3.cloned.1.call-done, f32[1024,512]{1,0:T(8,128)} %param.11), kind=kLoop, calls=%fused_computation.25 | loop fusion | flops 3670016 | bytes 10485760 | tf_op jit(solution)/shard_map/sub | solution.py:104
  (5 shorter events, 0.1 us)
Async XLA Ops:
  7.2 113.1 %reduce-scatter.4.cloned.1.call-start = ((), (), s32[]{:S(2)}) async-start(), calls=%async_computation.2 | async-start | bytes 10485760
  15.2 8.0 %collective-permute-start.1 = (bf16[512,4,1024]{2,0,1:T(8,128)(2,1)}, bf16[512,4,1024]{2,0,1:T(8,128)(2,1)}, u32[]{:S(2)}, u32[]{:S(2)}) collective-permute-start(bf16[512,4,1024]{2,0,1:T(8,128)(2,1)} %pad_maximum_fusion), channel_id=1, source_target_pairs={{0,1},{1,0},{2,3},{3,2},{4,5},{5,4},{6,7},{7,6},{8,9},{9,8},{10,11... | collective-permute-start | bytes 12582920 | tf_op jit(solution)/shard_map/ppermute | solution.py:84
  16.9 1.2 copy-start.1
  16.9 1.5 copy-start.2
  17.7 5.5 %collective-permute-start = (bf16[512,512]{0,1:T(8,128)(2,1)S(1)}, bf16[512,512]{0,1:T(8,128)(2,1)S(1)}, u32[]{:S(2)}, u32[]{:S(2)}) collective-permute-start(bf16[512,512]{0,1:T(8,128)(2,1)S(1)} %bitcast.66), channel_id=1, source_target_pairs={{0,1},{1,0},{2,3},{3,2},{4,5},{5,4},{6,7},{7,6},{8,9},{9,8},{10,11... | collective-permute-start | bytes 1572872 | tf_op jit(solution)/shard_map/ppermute | solution.py:85
  31.1 199.8 %all-reduce.3.cloned.1.call-start = ((), (), s32[]{:S(2)}) async-start(), calls=%async_computation.1 | async-start | bytes 4194304 | tf_op jit(solution)/shard_map/psum | solution.py:102
  143.3 0.7 copy-start.3
  143.3 87.6 %copy-start = (f32[1024,512]{1,0:T(8,128)S(1)}, f32[1024,512]{1,0:T(8,128)}, u32[]{:S(2)}) copy-start(f32[1024,512]{1,0:T(8,128)} %param.10) | copy-start | bytes 6291460
Sparse Core Ops, SparseCore 0:
  31.2 89.0 reduce-scatter.3
  143.4 87.4 all-reduce.2

commit v7 on v5

--- a/solution.py
+++ b/solution.py
@@ -53,6 +53,25 @@
     return jnp.dot(jnp.sum(drift_rows, axis=1), member, precision=lax.Precision.HIGHEST)
 
 
+def island_sum(values, replicas, pieces=4):
+    if replicas != 4:
+        return lax.psum(values, "island")
+    island = lax.axis_index("island")
+    middle = (island == 1) | (island == 2)
+    rows = values.shape[0] // pieces
+    sums, arrived = [], None
+    for piece in range(pieces):
+        part = values[piece * rows : (piece + 1) * rows]
+        if arrived is not None:
+            part, _ = lax.optimization_barrier((part, arrived))
+        arrived = lax.ppermute(part, "island", [(0, 1), (3, 2)])
+        pair = part + arrived
+        whole = pair + lax.ppermute(pair, "island", [(1, 2), (2, 1)])
+        back = lax.ppermute(whole, "island", [(1, 0), (2, 3)])
+        sums.append(jnp.where(middle, whole, back))
+    return jnp.concatenate(sums, axis=0)
+
+
 def body(
     activations,
     key_cotangents,
@@ -99,14 +118,14 @@
     inner = adam_update(gradient * factor, island_weights[0], first_moment[0], second_moment[0])
     island_drift = master - inner
     replicas = lax.axis_size("island")
-    drift = lax.psum(island_drift, "island") / replicas
+    first_row = position * own_rows
+    everyone = ("island", "chip", "core")
+    partials = local_tiles(island_drift, tile_rows, first_row)
+    padded = jnp.zeros((65536,), jnp.float32).at[: partials.shape[0]].set(partials)
+    totals = lax.psum(padded, everyone)[: partials.shape[0]] / replicas
+    drift = island_sum(island_drift, replicas) / replicas
     momentum_out = outer_moment * momentum + drift
     master_out = master - outer_rate * (drift + outer_moment * momentum_out)
-    first_row = position * own_rows
-    totals = (
-        lax.psum(local_tiles(island_drift, tile_rows, first_row), ("island", "chip", "core"))
-        / replicas
-    )
     tile_sums = totals / jnp.sqrt(tile_rows.astype(jnp.float32) * master.shape[1])
     return (master_out, momentum_out, tile_sums)
 

time: 244 us -> 365 us (1.50)
  waiting for transfers between devices: 135 us -> 265 us
  blocking collectives: 55.6 us -> 13.3 us
  starting transfers between devices: 0.66 us -> 28.8 us
  other arithmetic: 16.5 us -> 21.1 us
    psum x1, waiting for transfers between devices: 43.5 us -> 126 us  [body(): totals = lax.psum(padded, everyone)[:partials.shape[0]] / replicas]
    ppermute x0 -> x12, waiting for transfers between devices: none -> 46.9 us  [the longest x4 27.2 us: island_sum(): arrived = lax.ppermute(part, 'island', [(0, 1), (3, 2)])]
    psum x1 -> x0, blocking collectives: 42.3 us -> none  [body(): lax.psum(local_tiles(island_drift, tile_rows, first_row), ('island', 'chi...]
    ppermute x0 -> x12, starting transfers between devices: none -> 28.2 us  [the longest x4 17.6 us: island_sum(): arrived = lax.ppermute(part, 'island', [(0, 1), (3, 2)])]
    add x0 -> x8, other arithmetic: none -> 5 us  [the longest x4 3.44 us: island_sum(): whole = pair + lax.ppermute(pair, 'island', [(1, 2), (2, 1)])]
  transfers between devices with their start and end apart: 4 -> 16, of which waited for: 3 -> 9; matrix products, arithmetic and copies ran while one was open for 2% -> 4% of each run, Pallas kernels for 0% -> 0%
where the time goes in v7:
time: 365 us; the launch traced here: 364 us
  waiting for transfers between devices  265 us (73%)
  starting transfers between devices  28.8 us (8%)
  other arithmetic  21.1 us (6%)
  between operations  15 us (4%)
  blocking collectives  13.3 us (4%)
  matrix products  10.8 us (3%)
  local copies, waits for them, and re-layouts  10.4 us (3%)
    psum x1, waiting for transfers between devices, body(): totals = lax.psum(padded, everyone)[:partials.shape[0]] / replicas  126 us
    unnamed x3, waiting for transfers between devices  89.2 us
    ppermute x4, waiting for transfers between devices, island_sum(): arrived = lax.ppermute(part, 'island', [(0, 1), (3, 2)])  27.2 us
    ppermute x4, waiting for transfers between devices, island_sum(): back = lax.ppermute(whole, 'island', [(1, 0), (2, 3)])  19.6 us
    ppermute x4, starting transfers between devices, island_sum(): arrived = lax.ppermute(part, 'island', [(0, 1), (3, 2)])  17.6 us
    psum x1, blocking collectives, body(): squares = lax.psum(jnp.sum(gradient * gradient), ('chip', 'core'))  13.3 us
    dot_general x1, matrix products, body(): lax.dot_general(their_unrotated, their_tokens, contract, preferred_elemen...  7.87 us
  transfers between devices with their start and end apart: 16, of which 9 were waited for; matrix products, arithmetic and copies ran while one was open for 4% of the time, Pallas kernels for 0%

profile of v7, /device:TPU:0, one launch (start us, length us, event | category | flops | bytes accessed | tf_op | source)
XLA Modules:
  0.0 363.9 jit_solution(9505688208822841466)
XLA Ops:
  7.2 0.0 reduce-scatter.4.cloned.1.call-start
  7.2 5.7 %dynamic-slice_bitcast_fusion.3 = (bf16[512,1,1024]{2,0,1:T(8,128)(2,1)S(1)}, bf16[512,1,1024]{2,0,1:T(8,128)(2,1)S(1)}, bf16[512,1,1024]{2,0,1:T(8,128)(2,1)S(1...) fusion(bf16[1,512,8192]{2,1,0:T(8,128)(2,1)} %param.10, ...), kind=kLoop, calls=%fused_computation.32 | loop fusion | bytes 16777248 | tf_op jit(solution)/shard_map/stack | solution.py:95
  13.0 2.2 pad_maximum_fusion
  15.2 0.5 collective-permute-start.1
  15.6 1.3 copy.29
  16.9 0.0 copy-start.2
  16.9 0.0 copy-start.3
  16.9 0.5 multiply_cosine_fusion
  17.5 0.2 add_convert_fusion
  17.7 0.1 collective-permute-start
  17.8 0.3 copy-done.2
  18.1 0.3 copy-done.3
  18.4 2.5 fusion
  20.9 2.2 collective-permute-done
  23.1 0.0 collective-permute-done.1
  23.1 7.9 %convolution_add_fusion = f32[512,4,1024]{2,0,1:T(8,128)} fusion(f32[512,4,1024]{2,0,1:T(8,128)S(1)} %fusion, bf16[512,4,1024]{2,0,1:T(8,128)(2,1)} %collective-permute-done.1, bf16[512,512]{0,1:T(8,128)(2,1)S(1)} %collective-permute-done), kind=kOutput, calls=%fused_computation.10 | convolution fusion | flops 2149580800 | bytes 21495808 | tf_op jit(solution)/shard_map/dot_general | solution.py:108
  31.0 0.0 reduce-scatter.4.cloned.1.call-update
  31.0 0.0 all-reduce.4.cloned.1.call-start
  31.1 89.1 %reduce-scatter.4.cloned.1.call-done = f32[512,1,1024]{2,0,1:T(8,128)} async-done(((f32[512,4,1024]{2,0,1:T(8,128)}), f32[512,1,1024]{2,0,1:T(8,128)}) %reduce-scatter.4.cloned.1.call-update) | async-done | bytes 2097168
  120.2 1.9 copy.26
  122.1 1.1 fusion.14
  123.3 13.3 %psum.14 = f32[]{:T(128)} all-reduce(f32[]{:T(128)} %fusion.14), channel_id=1, replica_groups=mesh['island'=4,'chip'=4,'core'=2] {'chip','core'}, use_global_device_ids=true, to_apply=%region_2.3 | all-reduce | flops 1 | bytes 8 | tf_op jit(solution)/shard_map/psum | solution.py:116
  137.2 5.4 %fusion.26 = (f32[1024]{0:T(1024)S(1)}, f32[1024,512]{1,0:T(8,128)S(1)}) fusion(f32[1024,512]{1,0:T(8,128)} %param.12, f32[1,1024,512]{2,1,0:T(8,128)} %param.16, f32[]{:T(128)S(6)} %sqrt.9, f32[512,1,1024]{0,2,1:T(8,128)S(1)} %copy.26, f32[1,1024,512]{2,1,0:T(8,128)} %param.15, f32[1,1024,512]{2,1,0:T(8,128)} %param.14), kind=kLoop, calls=%fused_computation.63 | loop fusion | flops 9436160 | bytes 12587012 | tf_op jit(solution)/shard_map/reduce_sum | solution.py:53
  142.7 3.4 collective-permute-start.2
  146.1 10.3 %collective-permute-done.2 = f32[256,512]{1,0:T(8,128)S(1)} collective-permute-done((f32[256,512]{1,0:T(8,128)S(1)}, f32[256,512]{1,0:T(8,128)S(1)}, u32[]{:S(2)}, u32[]{:S(2)}) %collective-permute-start.2) | collective-permute-done | bytes 524320 | tf_op jit(solution)/shard_map/ppermute | solution.py:67
  156.4 0.3 slice_add_fusion
  156.7 4.4 %collective-permute-start.5 = (f32[256,512]{1,0:T(8,128)S(1)}, f32[256,512]{1,0:T(8,128)S(1)}, u32[]{:S(2)}, u32[]{:S(2)}) collective-permute-start(f32[256,512]{1,0:T(8,128)S(1)} %get-tuple-element.18), channel_id=1, source_target_pairs={{0,8},{24,16},{1,9},{25,17},{2,10},{26,18},{3,11},{27,19},{4,12},{... | collective-permute-start | bytes 1572872 | tf_op jit(solution)/shard_map/ppermute | solution.py:67
  161.1 9.4 %collective-permute-done.5 = f32[256,512]{1,0:T(8,128)S(1)} collective-permute-done((f32[256,512]{1,0:T(8,128)S(1)}, f32[256,512]{1,0:T(8,128)S(1)}, u32[]{:S(2)}, u32[]{:S(2)}) %collective-permute-start.5) | collective-permute-done | bytes 524320 | tf_op jit(solution)/shard_map/ppermute | solution.py:67
  170.5 4.4 %collective-permute-start.8 = (f32[256,512]{1,0:T(8,128)S(1)}, f32[256,512]{1,0:T(8,128)S(1)}, u32[]{:S(2)}, u32[]{:S(2)}) collective-permute-start(f32[256,512]{1,0:T(8,128)S(1)} %get-tuple-element.19), channel_id=1, source_target_pairs={{0,8},{24,16},{1,9},{25,17},{2,10},{26,18},{3,11},{27,19},{4,12},{... | collective-permute-start | bytes 1572872 | tf_op jit(solution)/shard_map/ppermute | solution.py:67
  174.9 1.5 collective-permute-start.3
  176.4 7.0 %collective-permute-done.8 = f32[256,512]{1,0:T(8,128)S(1)} collective-permute-done((f32[256,512]{1,0:T(8,128)S(1)}, f32[256,512]{1,0:T(8,128)S(1)}, u32[]{:S(2)}, u32[]{:S(2)}) %collective-permute-start.8) | collective-permute-done | bytes 524320 | tf_op jit(solution)/shard_map/ppermute | solution.py:67
  183.4 5.4 %collective-permute-start.11 = (f32[256,512]{1,0:T(8,128)S(1)}, f32[256,512]{1,0:T(8,128)}, u32[]{:S(2)}, u32[]{:S(2)}) collective-permute-start(f32[256,512]{1,0:T(8,128)S(1)} %get-tuple-element.20), channel_id=1, source_target_pairs={{0,8},{24,16},{1,9},{25,17},{2,10},{26,18},{3,11},{27,19},{4,12},{... | collective-permute-start | bytes 1572872 | tf_op jit(solution)/shard_map/ppermute | solution.py:67
  188.7 0.1 add.170
  188.8 1.4 collective-permute-start.6
  190.2 1.1 add.169
  191.4 1.3 collective-permute-start.4
  192.7 0.1 add.172
  192.8 0.7 collective-permute-start.9
  193.5 0.1 copy.27
  193.6 0.1 reduce-window.8
  193.7 0.1 reduce.2
  193.8 0.4 convolution_bitcast_fusion
  194.2 0.7 scatter.4
  194.9 0.0 all-reduce.4.cloned.1.call-update
  194.9 0.6 collective-permute-done.11
  195.5 1.1 add.174
  196.7 1.5 collective-permute-start.12
  198.2 1.1 add.171
  199.3 1.3 collective-permute-start.7
  200.6 126.3 %all-reduce.4.cloned.1.call-done = f32[65536]{0:T(1024)} async-done(((f32[65536]{0:T(1024)}), f32[65536]{0:T(1024)}) %all-reduce.4.cloned.1.call-update) | async-done | bytes 262160 | tf_op jit(solution)/shard_map/psum | solution.py:125
  326.9 1.2 fusion.24
  328.1 0.1 add.173
  328.2 1.3 collective-permute-start.10
  329.5 1.1 broadcast_select_fusion.3
  330.6 1.1 add.175
  331.7 0.0 copy-start
  331.8 0.0 copy-start.1
  331.8 1.6 collective-permute-start.13
  333.3 1.1 broadcast_select_fusion.2
  334.5 10.4 %collective-permute-done.10 = f32[256,512]{1,0:T(8,128)S(1)} collective-permute-done((f32[256,512]{1,0:T(8,128)S(1)}, f32[256,512]{1,0:T(8,128)S(1)}, u32[]{:S(2)}, u32[]{:S(2)}) %collective-permute-start.10) | collective-permute-done | bytes 524320 | tf_op jit(solution)/shard_map/ppermute | solution.py:70
  344.9 0.1 broadcast_select_fusion.1
  345.0 9.2 %collective-permute-done.13 = f32[256,512]{1,0:T(8,128)S(1)} collective-permute-done((f32[256,512]{1,0:T(8,128)S(1)}, f32[256,512]{1,0:T(8,128)S(1)}, u32[]{:S(2)}, u32[]{:S(2)}) %collective-permute-start.13) | collective-permute-done | bytes 524320 | tf_op jit(solution)/shard_map/ppermute | solution.py:70
  354.2 0.1 broadcast_select_fusion
  354.3 2.8 multiply_subtract_fusion
  (16 shorter events, 0.1 us)
Async XLA Ops:
  7.2 113.1 %reduce-scatter.4.cloned.1.call-start = ((), (), s32[]{:S(2)}) async-start(), calls=%async_computation.2 | async-start | bytes 10485760
  15.2 8.0 %collective-permute-start.1 = (bf16[512,4,1024]{2,0,1:T(8,128)(2,1)}, bf16[512,4,1024]{2,0,1:T(8,128)(2,1)}, u32[]{:S(2)}, u32[]{:S(2)}) collective-permute-start(bf16[512,4,1024]{2,0,1:T(8,128)(2,1)} %pad_maximum_fusion), channel_id=1, source_target_pairs={{0,1},{1,0},{2,3},{3,2},{4,5},{5,4},{6,7},{7,6},{8,9},{9,8},{10,11... | collective-permute-start | bytes 12582920 | tf_op jit(solution)/shard_map/ppermute | solution.py:103
  16.9 1.2 copy-start.2
  16.9 1.5 copy-start.3
  17.7 5.5 %collective-permute-start = (bf16[512,512]{0,1:T(8,128)(2,1)S(1)}, bf16[512,512]{0,1:T(8,128)(2,1)S(1)}, u32[]{:S(2)}, u32[]{:S(2)}) collective-permute-start(bf16[512,512]{0,1:T(8,128)(2,1)S(1)} %bitcast.66), channel_id=1, source_target_pairs={{0,1},{1,0},{2,3},{3,2},{4,5},{5,4},{6,7},{7,6},{8,9},{9,8},{10,11... | collective-permute-start | bytes 1572872 | tf_op jit(solution)/shard_map/ppermute | solution.py:104
  31.0 295.9 %all-reduce.4.cloned.1.call-start = ((), (), s32[]{:S(2)}) async-start(), calls=%async_computation.1 | async-start | bytes 524288 | tf_op jit(solution)/shard_map/psum | solution.py:125
  142.7 13.7 %collective-permute-start.2 = (f32[256,512]{1,0:T(8,128)S(1)}, f32[256,512]{1,0:T(8,128)S(1)}, u32[]{:S(2)}, u32[]{:S(2)}) collective-permute-start(f32[256,512]{1,0:T(8,128)S(1)} %slice.41), channel_id=1, source_target_pairs={{0,8},{24,16},{1,9},{25,17},{2,10},{26,18},{3,11},{27,19},{4,12},{... | collective-permute-start | bytes 1572872 | tf_op jit(solution)/shard_map/ppermute | solution.py:67
  156.7 13.8 %collective-permute-start.5 = (f32[256,512]{1,0:T(8,128)S(1)}, f32[256,512]{1,0:T(8,128)S(1)}, u32[]{:S(2)}, u32[]{:S(2)}) collective-permute-start(f32[256,512]{1,0:T(8,128)S(1)} %get-tuple-element.18), channel_id=1, source_target_pairs={{0,8},{24,16},{1,9},{25,17},{2,10},{26,18},{3,11},{27,19},{4,12},{... | collective-permute-start | bytes 1572872 | tf_op jit(solution)/shard_map/ppermute | solution.py:67
  170.5 12.9 %collective-permute-start.8 = (f32[256,512]{1,0:T(8,128)S(1)}, f32[256,512]{1,0:T(8,128)S(1)}, u32[]{:S(2)}, u32[]{:S(2)}) collective-permute-start(f32[256,512]{1,0:T(8,128)S(1)} %get-tuple-element.19), channel_id=1, source_target_pairs={{0,8},{24,16},{1,9},{25,17},{2,10},{26,18},{3,11},{27,19},{4,12},{... | collective-permute-start | bytes 1572872 | tf_op jit(solution)/shard_map/ppermute | solution.py:67
  174.9 15.3 %collective-permute-start.3 = (f32[256,512]{1,0:T(8,128)S(1)}, f32[256,512]{1,0:T(8,128)}, u32[]{:S(2)}, u32[]{:S(2)}) collective-permute-start(f32[256,512]{1,0:T(8,128)S(1)} %get-tuple-element.33), channel_id=1, source_target_pairs={{8,16},{16,8},{9,17},{17,9},{10,18},{18,10},{11,19},{19,11},{12,20... | collective-permute-start | bytes 1572872 | tf_op jit(solution)/shard_map/ppermute | solution.py:69
  183.4 10.1 %copy-start.4 = (s32[48]{0:T(128)S(1)}, s32[48]{0:T(128)}, u32[]{:S(2)}) copy-start(s32[48]{0:T(128)} %param.17) | copy-start | bytes 580
  183.4 12.2 %collective-permute-start.11 = (f32[256,512]{1,0:T(8,128)S(1)}, f32[256,512]{1,0:T(8,128)}, u32[]{:S(2)}, u32[]{:S(2)}) collective-permute-start(f32[256,512]{1,0:T(8,128)S(1)} %get-tuple-element.20), channel_id=1, source_target_pairs={{0,8},{24,16},{1,9},{25,17},{2,10},{26,18},{3,11},{27,19},{4,12},{... | collective-permute-start | bytes 1572872 | tf_op jit(solution)/shard_map/ppermute | solution.py:67
  188.8 9.4 %collective-permute-start.6 = (f32[256,512]{1,0:T(8,128)S(1)}, f32[256,512]{1,0:T(8,128)}, u32[]{:S(2)}, u32[]{:S(2)}) collective-permute-start(f32[256,512]{1,0:T(8,128)S(1)} %add.170), channel_id=1, source_target_pairs={{8,16},{16,8},{9,17},{17,9},{10,18},{18,10},{11,19},{19,11},{12,20... | collective-permute-start | bytes 1572872 | tf_op jit(solution)/shard_map/ppermute | solution.py:69
  191.4 138.1 %collective-permute-start.4 = (f32[256,512]{1,0:T(8,128)S(1)}, f32[256,512]{1,0:T(8,128)}, u32[]{:S(2)}, u32[]{:S(2)}) collective-permute-start(f32[256,512]{1,0:T(8,128)S(1)} %add.169), channel_id=1, source_target_pairs={{8,0},{16,24},{9,1},{17,25},{10,2},{18,26},{11,3},{19,27},{12,4},{... | collective-permute-start | bytes 1572872 | tf_op jit(solution)/shard_map/ppermute | solution.py:70
  192.8 135.3 %collective-permute-start.9 = (f32[256,512]{1,0:T(8,128)S(1)}, f32[256,512]{1,0:T(8,128)S(1)}, u32[]{:S(2)}, u32[]{:S(2)}) collective-permute-start(f32[256,512]{1,0:T(8,128)S(1)} %add.172), channel_id=1, source_target_pairs={{8,16},{16,8},{9,17},{17,9},{10,18},{18,10},{11,19},{19,11},{12,20... | collective-permute-start | bytes 1572872 | tf_op jit(solution)/shard_map/ppermute | solution.py:69
  196.7 134.0 %collective-permute-start.12 = (f32[256,512]{1,0:T(8,128)S(1)}, f32[256,512]{1,0:T(8,128)}, u32[]{:S(2)}, u32[]{:S(2)}) collective-permute-start(f32[256,512]{1,0:T(8,128)S(1)} %add.174), channel_id=1, source_target_pairs={{8,16},{16,8},{9,17},{17,9},{10,18},{18,10},{11,19},{19,11},{12,20... | collective-permute-start | bytes 1572872 | tf_op jit(solution)/shard_map/ppermute | solution.py:69
  199.3 134.1 %collective-permute-start.7 = (f32[256,512]{1,0:T(8,128)S(1)}, f32[256,512]{1,0:T(8,128)}, u32[]{:S(2)}, u32[]{:S(2)}) collective-permute-start(f32[256,512]{1,0:T(8,128)S(1)} %add.171), channel_id=1, source_target_pairs={{8,0},{16,24},{9,1},{17,25},{10,2},{18,26},{11,3},{19,27},{12,4},{... | collective-permute-start | bytes 1572872 | tf_op jit(solution)/shard_map/ppermute | solution.py:70
  328.2 16.8 %collective-permute-start.10 = (f32[256,512]{1,0:T(8,128)S(1)}, f32[256,512]{1,0:T(8,128)S(1)}, u32[]{:S(2)}, u32[]{:S(2)}) collective-permute-start(f32[256,512]{1,0:T(8,128)S(1)} %add.173), channel_id=1, source_target_pairs={{8,0},{16,24},{9,1},{17,25},{10,2},{18,26},{11,3},{19,27},{12,4},{... | collective-permute-start | bytes 1572872 | tf_op jit(solution)/shard_map/ppermute | solution.py:70
  331.7 22.5 %copy-start = (f32[1024,512]{1,0:T(8,128)S(1)}, f32[1024,512]{1,0:T(8,128)}, u32[]{:S(2)}) copy-start(f32[1024,512]{1,0:T(8,128)} %param.12) | copy-start | bytes 6291460
  331.8 22.5 %copy-start.1 = (f32[1024,512]{1,0:T(8,128)S(1)}, f32[1024,512]{1,0:T(8,128)}, u32[]{:S(2)}) copy-start(f32[1024,512]{1,0:T(8,128)} %param.13) | copy-start | bytes 6291460
  331.8 22.4 %collective-permute-start.13 = (f32[256,512]{1,0:T(8,128)S(1)}, f32[256,512]{1,0:T(8,128)S(1)}, u32[]{:S(2)}, u32[]{:S(2)}) collective-permute-start(f32[256,512]{1,0:T(8,128)S(1)} %add.175), channel_id=1, source_target_pairs={{8,0},{16,24},{9,1},{17,25},{10,2},{18,26},{11,3},{19,27},{12,4},{... | collective-permute-start | bytes 1572872 | tf_op jit(solution)/shard_map/ppermute | solution.py:70
Sparse Core Ops, SparseCore 0:
  31.2 89.0 reduce-scatter.3
  195.0 131.8 all-reduce.3

commit v8 on v5

--- a/solution.py
+++ b/solution.py
@@ -73,21 +73,19 @@
     tokens = activations[0]
 
     def parity(side):
-        return jnp.stack(
-            [
-                lax.dynamic_slice_in_dim(tokens, (2 * k + side) * own_rows, own_rows, axis=1)
-                for k in range(chips)
-            ],
-            axis=1,
-        )
+        return [
+            lax.dynamic_slice_in_dim(tokens, (2 * k + side) * own_rows, own_rows, axis=1)
+            for k in range(chips)
+        ]
 
-    their_tokens = lax.ppermute(parity(1 - core), "core", swap)
+    their_tokens = [lax.ppermute(block, "core", swap) for block in parity(1 - core)]
     their_unrotated = lax.ppermute(unrotated, "core", swap)
     contract = (((0,), (0,)), ((), ()))
     partial = lax.dot_general(
-        unrotated, parity(core), contract, preferred_element_type=jnp.float32
+        unrotated, jnp.stack(parity(core), axis=1), contract, preferred_element_type=jnp.float32
     ) + lax.dot_general(
-        their_unrotated, their_tokens, contract, preferred_element_type=jnp.float32
+        their_unrotated, jnp.stack(their_tokens, axis=1), contract,
+        preferred_element_type=jnp.float32,
     )
     gradient = lax.psum_scatter(partial, "chip", scatter_dimension=1, tiled=True)
     gradient = with_layout_constraint(gradient, Layout((0, 1, 2)))

time: 244 us -> 242 us (level)
    dynamic_slice x0 -> x1, local copies, waits for them, and re-layouts: none -> 6.32 us  [parity(): lax.dynamic_slice_in_dim(tokens, (2 * k + side) * own_rows, own_rows, axi...]
    another operation x2 -> x1, local copies, waits for them, and re-layouts: 5.84 us -> 0.09 us  [the longest x1 5.74 us: parity(): jnp.stack([lax.dynamic_slice_in_dim(tokens, (2 * k + side) * own_rows, ow...]
  transfers between devices with their start and end apart: 4 -> 7, of which waited for: 3 -> 2; matrix products, arithmetic and copies ran while one was open for 2% -> 3% of each run, Pallas kernels for 0% -> 0%
where the time goes in v8:
time: 242 us
  waiting for transfers between devices  133 us (55%)
  blocking collectives  55.6 us (23%)
  between operations  14.9 us (6%)
  other arithmetic  14.3 us (6%)
  matrix products  12 us (5%)
  local copies, waits for them, and re-layouts  11 us (5%)
    unnamed x3, waiting for transfers between devices  89.2 us
    psum x1, waiting for transfers between devices, body(): drift = lax.psum(island_drift, 'island') / replicas  43.5 us
    psum x1, blocking collectives, body(): lax.psum(local_tiles(island_drift, tile_rows, first_row), ('island', 'chi...  42.3 us
    psum x1, blocking collectives, body(): squares = lax.psum(jnp.sum(gradient * gradient), ('chip', 'core'))  13.3 us
    dot_general x1, matrix products, body(): lax.dot_general(their_unrotated, jnp.stack(their_tokens, axis=1), contrac...  7.92 us
    reduce_sum x1, other arithmetic, local_tiles(): jnp.sum(drift_rows, axis=1)  6.65 us
    dynamic_slice x1, local copies, waits for them, and re-layouts, parity(): lax.dynamic_slice_in_dim(tokens, (2 * k + side) * own_rows, own_rows, axi...  6.32 us
    sub x1, other arithmetic, body(): master_out = master - outer_rate * (drift + outer_moment * momentum_out)  5.02 us
  transfers between devices with their start and end apart: 7, of which 2 were waited for; matrix products, arithmetic and copies ran while one was open for 3% of the time, Pallas kernels for 0%

profile of v8, /device:TPU:0, one launch (start us, length us, event | category | flops | bytes accessed | tf_op | source)
XLA Modules:
  0.0 242.1 jit_solution(17847055473372867821)
XLA Ops:
  7.2 0.0 reduce-scatter.4.cloned.1.call-start
  7.2 6.3 %dynamic-slice_bitcast_fusion.3 = (bf16[512,1024]{1,0:T(8,128)(2,1)}, bf16[512,1024]{1,0:T(8,128)(2,1)}, bf16[512,1,1024]{2,0,1:T(8,128)(2,1)}, bf16[512,1,1024]...) fusion(bf16[1,512,8192]{2,1,0:T(8,128)(2,1)} %param.8, ...), kind=kLoop, calls=%fused_computation.38 | loop fusion | bytes 16777248 | tf_op jit(solution)/shard_map/dynamic_slice | solution.py:77
  13.5 0.5 collective-permute-start.1
  14.0 0.1 collective-permute-start.2
  14.1 0.5 collective-permute-start.3
  14.5 0.1 collective-permute-start.4
  14.6 0.5 multiply_cosine_fusion
  15.1 1.3 copy.29
  16.4 0.0 copy-start.1
  16.4 0.0 copy-start.2
  16.4 0.2 add_convert_fusion
  16.6 0.5 collective-permute-start
  17.2 0.5 copy-done.1
  17.6 0.3 copy-done.2
  17.9 3.7 %fusion = f32[512,4,1024]{2,0,1:T(8,128)S(1)} fusion(bf16[512,512,1]{0,1,2:T(8,128)(2,1)S(1)} %bitcast.70, bf16[512,1,1024]{2,0,1:T(8,128)(2,1)S(1)} %copy-done.1, bf16[512,1,1024]{2,0,1:T(8,128)(2,1)S(1)} %copy-done.2, bf16[512,1,1024]{2,0,1:T(8,128)(2,1)} %get-tuple-element.11, bf16[512,1,1024]{2,0,1:T(8,128)(2,1)} %get-tuple-element.12), kind=kOutput, calls=%fused_computation | convolution fusion | flops 2164260864 | bytes 13107200 | tf_op jit(solution)/shard_map/dot_general | solution.py:84
  21.7 0.0 collective-permute-done
  21.7 0.0 collective-permute-done.1
  21.7 0.0 collective-permute-done.2
  21.7 0.0 collective-permute-done.3
  21.7 0.0 collective-permute-done.4
  21.7 7.9 %fusion.16 = f32[512,4,1024]{2,0,1:T(8,128)} fusion(f32[512,4,1024]{2,0,1:T(8,128)S(1)} %fusion, bf16[512,1,1024]{2,0,1:T(8,128)(2,1)} %bitcast.16, bf16[512,1,1024]{2,0,1:T(8,128)(2,1)} %bitcast.14, bf16[512,1,1024]{2,0,1:T(8,128)(2,1)} %bitcast.12, bf16[512,1,1024]{2,0,1:T(8,128)(2,1)} %bitcast.10, bf16[512,512]{0,1:T(8,128)(2,1)S(1)} %collective-permute-done), kind=kOutput, calls=%fused_computation.17 | convolution fusion | flops 2166358016 | bytes 21495808 | tf_op jit(solution)/shard_map/dot_general | solution.py:86
  29.7 0.0 reduce-scatter.4.cloned.1.call-update
  29.7 0.0 all-reduce.3.cloned.1.call-start
  29.7 89.2 %reduce-scatter.4.cloned.1.call-done = f32[512,1,1024]{2,0,1:T(8,128)} async-done(((f32[512,4,1024]{2,0,1:T(8,128)}), f32[512,1,1024]{2,0,1:T(8,128)}) %reduce-scatter.4.cloned.1.call-update) | async-done | bytes 2097168
  118.9 1.9 copy.26
  120.9 1.1 fusion.25
  122.0 13.3 %psum.21 = f32[]{:T(128)} all-reduce(f32[]{:T(128)} %fusion.25), channel_id=1, replica_groups=mesh['island'=4,'chip'=4,'core'=2] {'chip','core'}, use_global_device_ids=true, to_apply=%region_2.3 | all-reduce | flops 1 | bytes 8 | tf_op jit(solution)/shard_map/psum | solution.py:95
  136.0 6.6 %fusion.37 = (f32[1024]{0:T(1024)S(1)}, f32[1024,512]{1,0:T(8,128)}) fusion(f32[1024,512]{1,0:T(8,128)} %param.10, f32[1,1024,512]{2,1,0:T(8,128)} %param.14, f32[]{:T(128)S(6)} %sqrt.9, f32[512,1,1024]{0,2,1:T(8,128)S(1)} %copy.26, f32[1,1024,512]{2,1,0:T(8,128)} %param.13, f32[1,1024,512]{2,1,0:T(8,128)} %param.12), kind=kLoop, calls=%fused_computation.64 | loop fusion | flops 9436160 | bytes 12587012 | tf_op jit(solution)/shard_map/reduce_sum | solution.py:53
  142.6 0.0 copy-start.3
  142.6 0.0 copy-start
  142.6 0.0 all-reduce.3.cloned.1.call-update
  142.7 0.6 copy-done.3
  143.3 0.1 copy.27
  143.4 0.1 reduce-window.8
  143.5 0.1 reduce
  143.6 0.4 convolution_bitcast_fusion
  144.0 42.3 %psum.23 = f32[48]{0:T(128)S(1)} all-reduce(f32[48]{0:T(128)S(1)} %convolution_bitcast_fusion), channel_id=1, replica_groups=mesh['island'=4,'chip'=4,'core'=2] {'island','chip','core'}, use_global_device_ids=true, to_apply=%region_6.7 | all-reduce | flops 48 | bytes 384 | tf_op jit(solution)/shard_map/psum | solution.py:105
  186.2 0.5 rsqrt_multiply_fusion
  186.8 43.5 %all-reduce.3.cloned.1.call-done = f32[1024,512]{1,0:T(8,128)} async-done(((f32[1024,512]{1,0:T(8,128)}), f32[1024,512]{1,0:T(8,128)}) %all-reduce.3.cloned.1.call-update) | async-done | bytes 2097168 | tf_op jit(solution)/shard_map/psum | solution.py:100
  230.2 0.0 copy-done
  230.2 5.0 %multiply_subtract_fusion = (f32[1024,512]{1,0:T(8,128)}, f32[1024,512]{1,0:T(8,128)}) fusion(f32[1024,512]{1,0:T(8,128)S(1)} %copy-done, f32[1024,512]{1,0:T(8,128)} %all-reduce.3.cloned.1.call-done, f32[1024,512]{1,0:T(8,128)} %param.11), kind=kLoop, calls=%fused_computation.32 | loop fusion | flops 3670016 | bytes 10485760 | tf_op jit(solution)/shard_map/sub | solution.py:102
  (5 shorter events, 0.1 us)
Async XLA Ops:
  7.2 111.8 %reduce-scatter.4.cloned.1.call-start = ((), (), s32[]{:S(2)}) async-start(), calls=%async_computation.2 | async-start | bytes 10485760
  13.5 8.1 %collective-permute-start.1 = (bf16[512,1024]{1,0:T(8,128)(2,1)}, bf16[512,1024]{1,0:T(8,128)(2,1)}, u32[]{:S(2)}, u32[]{:S(2)}) collective-permute-start(bf16[512,1024]{1,0:T(8,128)(2,1)} %get-tuple-element.7), channel_id=1, source_target_pairs={{0,1},{1,0},{2,3},{3,2},{4,5},{5,4},{6,7},{7,6},{8,9},{9,8},{10,11... | collective-permute-start | bytes 3145736 | tf_op jit(solution)/shard_map/ppermute | solution.py:81
  14.0 7.7 %collective-permute-start.2 = (bf16[512,1024]{1,0:T(8,128)(2,1)}, bf16[512,1024]{1,0:T(8,128)(2,1)}, u32[]{:S(2)}, u32[]{:S(2)}) collective-permute-start(bf16[512,1024]{1,0:T(8,128)(2,1)} %get-tuple-element.8), channel_id=1, source_target_pairs={{0,1},{1,0},{2,3},{3,2},{4,5},{5,4},{6,7},{7,6},{8,9},{9,8},{10,11... | collective-permute-start | bytes 3145736 | tf_op jit(solution)/shard_map/ppermute | solution.py:81
  14.1 7.7 %collective-permute-start.3 = (bf16[512,1024]{1,0:T(8,128)(2,1)S(1)}, bf16[512,1024]{1,0:T(8,128)(2,1)}, u32[]{:S(2)}, u32[]{:S(2)}) collective-permute-start(bf16[512,1024]{1,0:T(8,128)(2,1)S(1)} %get-tuple-element.14), channel_id=1, source_target_pairs={{0,1},{1,0},{2,3},{3,2},{4,5},{5,4},{6,7},{7,6},{8,9},{9,8},{10,11... | collective-permute-start | bytes 3145736 | tf_op jit(solution)/shard_map/ppermute | solution.py:81
  14.5 7.2 %collective-permute-start.4 = (bf16[512,1024]{1,0:T(8,128)(2,1)S(1)}, bf16[512,1024]{1,0:T(8,128)(2,1)}, u32[]{:S(2)}, u32[]{:S(2)}) collective-permute-start(bf16[512,1024]{1,0:T(8,128)(2,1)S(1)} %get-tuple-element.13), channel_id=1, source_target_pairs={{0,1},{1,0},{2,3},{3,2},{4,5},{5,4},{6,7},{7,6},{8,9},{9,8},{10,11... | collective-permute-start | bytes 3145736 | tf_op jit(solution)/shard_map/ppermute | solution.py:81
  16.4 1.2 copy-start.1
  16.4 1.5 copy-start.2
  16.6 5.0 %collective-permute-start = (bf16[512,512]{0,1:T(8,128)(2,1)S(1)}, bf16[512,512]{0,1:T(8,128)(2,1)S(1)}, u32[]{:S(2)}, u32[]{:S(2)}) collective-permute-start(bf16[512,512]{0,1:T(8,128)(2,1)S(1)} %bitcast.69), channel_id=1, source_target_pairs={{0,1},{1,0},{2,3},{3,2},{4,5},{5,4},{6,7},{7,6},{8,9},{9,8},{10,11... | collective-permute-start | bytes 1572872 | tf_op jit(solution)/shard_map/ppermute | solution.py:82
  29.7 200.6 %all-reduce.3.cloned.1.call-start = ((), (), s32[]{:S(2)}) async-start(), calls=%async_computation.1 | async-start | bytes 4194304 | tf_op jit(solution)/shard_map/psum | solution.py:100
  142.6 0.7 copy-start.3
  142.6 87.6 %copy-start = (f32[1024,512]{1,0:T(8,128)S(1)}, f32[1024,512]{1,0:T(8,128)}, u32[]{:S(2)}) copy-start(f32[1024,512]{1,0:T(8,128)} %param.10) | copy-start | bytes 6291460
Sparse Core Ops, SparseCore 0:
  29.8 89.0 reduce-scatter.3
  142.8 87.4 all-reduce.2

commit v9 on v8

--- a/solution.py
+++ b/solution.py
@@ -53,6 +53,28 @@
     return jnp.dot(jnp.sum(drift_rows, axis=1), member, precision=lax.Precision.HIGHEST)
 
 
+def chip_scatter(partial, chips):
+    core = lax.axis_index("core")
+    chip = lax.axis_index("chip")
+    along_x, along_y = chip % 2, chip // 2
+    first = jnp.where(core == 0, along_x, along_y)
+    second = jnp.where(core == 0, along_y, along_x)
+    lanes = ("chip", "core")
+    cross_first = [(f, f ^ 2) if f % 2 == 0 else (f, f ^ 4) for f in range(2 * chips)]
+    cross_second = [(f, f ^ 4) if f % 2 == 0 else (f, f ^ 2) for f in range(2 * chips)]
+    grid = partial.reshape(partial.shape[0], 2, 2, partial.shape[2])
+    by_x = [grid[:, :, 0], grid[:, :, 1]]
+    by_y = [grid[:, 0], grid[:, 1]]
+    lower = jnp.where(core == 0, by_x[0], by_y[0])
+    upper = jnp.where(core == 0, by_x[1], by_y[1])
+    keep = jnp.where(first == 0, lower, upper)
+    send = jnp.where(first == 0, upper, lower)
+    held = keep + lax.ppermute(send, lanes, cross_first)
+    keep = jnp.where(second == 0, held[:, 0], held[:, 1])
+    send = jnp.where(second == 0, held[:, 1], held[:, 0])
+    return (keep + lax.ppermute(send, lanes, cross_second))[:, None]
+
+
 def body(
     activations,
     key_cotangents,
@@ -87,7 +109,17 @@
         their_unrotated, jnp.stack(their_tokens, axis=1), contract,
         preferred_element_type=jnp.float32,
     )
-    gradient = lax.psum_scatter(partial, "chip", scatter_dimension=1, tiled=True)
+    if chips == 4:
+        split = partial.shape[0] // 2
+        gradient = jnp.concatenate(
+            [
+                lax.psum_scatter(partial[:split], "chip", scatter_dimension=1, tiled=True),
+                chip_scatter(partial[split:], chips),
+            ],
+            axis=0,
+        )
+    else:
+        gradient = lax.psum_scatter(partial, "chip", scatter_dimension=1, tiled=True)
     gradient = with_layout_constraint(gradient, Layout((0, 1, 2)))
     gradient = with_layout_constraint(
         gradient.reshape(gradient.shape[0], own_rows).T, Layout((0, 1))

time: 242 us -> 243 us (level)
  waiting for transfers between devices: 133 us -> 106 us
  other arithmetic: 14.3 us -> 28.6 us
  local copies, waits for them, and re-layouts: 11 us -> 20.7 us
  starting transfers between devices: 1.62 us -> 7.8 us
  matrix products: 12 us -> 8.3 us
    unnamed x3, waiting for transfers between devices: 89.2 us -> 0.05 us
    ppermute x0 -> x2, waiting for transfers between devices: none -> 63.2 us  [the longest x1 50.5 us: chip_scatter(): held = keep + lax.ppermute(send, lanes, cross_first)]
    select_n x0 -> x2, other arithmetic: none -> 6.13 us  [the longest x1 5.96 us: chip_scatter(): send = jnp.where(first == 0, upper, lower)]
    ppermute x0 -> x2, starting transfers between devices: none -> 6 us  [the longest x1 3.06 us: chip_scatter(): return (keep + lax.ppermute(send, lanes, cross_second))[:, None]]
    add x0 -> x2, other arithmetic: none -> 5.03 us  [the longest x1 4.72 us: chip_scatter(): held = keep + lax.ppermute(send, lanes, cross_first)]
    slice x0 -> x1, local copies, waits for them, and re-layouts: none -> 4.07 us  [body(): partial[:split]]
    dot_general x1, matrix products: 7.92 us -> 4.19 us  [body(): lax.dot_general(their_unrotated, jnp.stack(their_tokens, axis=1), contrac...]
    concatenate x0 -> x1, other arithmetic: none -> 3.12 us  [body(): jnp.concatenate([lax.psum_scatter(partial[:split], 'chip', scatter_dimens...]
  transfers between devices with their start and end apart: 7 -> 9, of which waited for: 2 -> 3; matrix products, arithmetic and copies ran while one was open for 3% -> 8% of each run, Pallas kernels for 0% -> 0%
where the time goes in v9:
time: 243 us
  waiting for transfers between devices  106 us (44%)
  blocking collectives  55.7 us (23%)
  other arithmetic  28.6 us (12%)
  local copies, waits for them, and re-layouts  20.7 us (9%)
  between operations  14.9 us (6%)
  matrix products  8.3 us (3%)
  starting transfers between devices  7.8 us (3%)
    ppermute x1, waiting for transfers between devices, chip_scatter(): held = keep + lax.ppermute(send, lanes, cross_first)  50.5 us
    psum x1, waiting for transfers between devices, body(): drift = lax.psum(island_drift, 'island') / replicas  43.2 us
    psum x1, blocking collectives, body(): lax.psum(local_tiles(island_drift, tile_rows, first_row), ('island', 'chi...  42.3 us
    psum x1, blocking collectives, body(): squares = lax.psum(jnp.sum(gradient * gradient), ('chip', 'core'))  13.4 us
    ppermute x1, waiting for transfers between devices, chip_scatter(): return (keep + lax.ppermute(send, lanes, cross_second))[:, None]  12.8 us
    reduce_sum x1, other arithmetic, local_tiles(): jnp.sum(drift_rows, axis=1)  6.65 us
    dynamic_slice x1, local copies, waits for them, and re-layouts, parity(): lax.dynamic_slice_in_dim(tokens, (2 * k + side) * own_rows, own_rows, axi...  6.32 us
    select_n x1, other arithmetic, chip_scatter(): send = jnp.where(first == 0, upper, lower)  5.96 us
  transfers between devices with their start and end apart: 9, of which 3 were waited for; matrix products, arithmetic and copies ran while one was open for 8% of the time, Pallas kernels for 0%

profile of v9, /device:TPU:0, one launch (start us, length us, event | category | flops | bytes accessed | tf_op | source)
XLA Modules:
  0.0 242.5 jit_solution(14045545278529696532)
XLA Ops:
  7.2 0.0 reduce-scatter.4.cloned.1.call-start
  7.2 6.3 %dynamic-slice_bitcast_fusion.3 = (bf16[512,1024]{1,0:T(8,128)(2,1)}, bf16[512,1024]{1,0:T(8,128)(2,1)}, bf16[512,1,1024]{2,0,1:T(8,128)(2,1)}, bf16[512,1,1024]...) fusion(bf16[1,512,8192]{2,1,0:T(8,128)(2,1)} %param.8, ...), kind=kLoop, calls=%fused_computation.48 | loop fusion | bytes 16777248 | tf_op jit(solution)/shard_map/dynamic_slice | solution.py:99
  13.5 0.5 collective-permute-start.1
  14.0 0.1 collective-permute-start.2
  14.1 0.5 collective-permute-start.3
  14.5 0.1 collective-permute-start.4
  14.6 0.5 multiply_cosine_fusion
  15.1 1.3 copy.30
  16.4 0.0 copy-start.1
  16.4 0.0 copy-start.2
  16.4 0.2 add_convert_fusion
  16.6 0.5 collective-permute-start
  17.2 0.5 copy-done.1
  17.6 0.3 copy-done.2
  17.9 3.7 %fusion = f32[512,4,1024]{2,0,1:T(8,128)S(1)} fusion(bf16[512,512,1]{0,1,2:T(8,128)(2,1)S(1)} %bitcast.109, bf16[512,1,1024]{2,0,1:T(8,128)(2,1)S(1)} %copy-done.1, bf16[512,1,1024]{2,0,1:T(8,128)(2,1)S(1)} %copy-done.2, bf16[512,1,1024]{2,0,1:T(8,128)(2,1)} %get-tuple-element.13, bf16[512,1,1024]{2,0,1:T(8,128)(2,1)} %get-tuple-element.14), kind=kOutput, calls=%fused_computation | convolution fusion | flops 2164260864 | bytes 13107200 | tf_op jit(solution)/shard_map/dot_general | solution.py:106
  21.7 0.0 collective-permute-done
  21.7 0.0 collective-permute-done.1
  21.7 0.0 collective-permute-done.2
  21.7 0.0 collective-permute-done.3
  21.7 0.0 collective-permute-done.4
  21.7 4.2 %fusion.16 = f32[512,4,1024]{2,0,1:T(8,128)S(1)} fusion(f32[512,4,1024]{2,0,1:T(8,128)S(1)} %fusion, bf16[512,1,1024]{2,0,1:T(8,128)(2,1)} %bitcast.16, bf16[512,1,1024]{2,0,1:T(8,128)(2,1)} %bitcast.14, bf16[512,1,1024]{2,0,1:T(8,128)(2,1)} %bitcast.12, bf16[512,1,1024]{2,0,1:T(8,128)(2,1)} %bitcast.10, bf16[512,512]{0,1:T(8,128)(2,1)S(1)} %collective-permute-done), kind=kOutput, calls=%fused_computation.17 | convolution fusion | flops 2166358016 | bytes 21495808 | tf_op jit(solution)/shard_map/dot_general | solution.py:108
  25.9 4.1 %fusion.41 = (f32[256,4,1024]{2,0,1:T(8,128)}, f32[256,4,1024]{2,0,1:T(8,128)}) fusion(f32[512,4,1024]{2,0,1:T(8,128)S(1)} %fusion.16), kind=kLoop, calls=%fused_computation.76 | loop fusion | bytes 16777216 | tf_op jit(solution)/shard_map/slice | solution.py:116
  30.0 0.0 reduce-scatter.4.cloned.1.call-update
  30.0 0.2 all-reduce.3.cloned.1.call-start
  30.3 6.0 %broadcast_select_fusion = f32[256,2,1024]{2,0,1:T(8,128)} fusion(pred[]{:T(512)S(6)} %eq.20, f32[256,2,2,1024]{3,0,2,1:T(8,128)} %bitcast.105, pred[]{:T(512)S(6)} %eq.10), kind=kLoop, calls=%fused_computation.53 | loop fusion | flops 1572864 | bytes 10485762 | tf_op jit(solution)/shard_map/jit(_where)/select_n | solution.py:71
  36.3 2.9 %collective-permute-start.5 = (f32[256,2,1024]{2,0,1:T(8,128)}, f32[256,2,1024]{2,0,1:T(8,128)S(1)}, u32[]{:S(2)}, u32[]{:S(2)}) collective-permute-start(f32[256,2,1024]{2,0,1:T(8,128)} %broadcast_select_fusion), channel_id=1, source_target_pairs={{0,2},{1,5},{2,0},{3,7},{4,6},{5,1},{6,4},{7,3},{8,10},{9,13},{10,... | collective-permute-start | bytes 6291464 | tf_op jit(solution)/shard_map/ppermute | solution.py:72
  39.2 50.5 %collective-permute-done.5 = f32[256,2,1024]{2,0,1:T(8,128)S(1)} collective-permute-done((f32[256,2,1024]{2,0,1:T(8,128)}, f32[256,2,1024]{2,0,1:T(8,128)S(1)}, u32[]{:S(2)}, u32[]{:S(2)}) %collective-permute-start.5) | collective-permute-done | bytes 2097184 | tf_op jit(solution)/shard_map/ppermute | solution.py:72
  89.6 4.7 %select_add_fusion = f32[256,2,1024]{2,0,1:T(8,128)S(1)} fusion(f32[256,2,1024]{2,0,1:T(8,128)S(1)} %collective-permute-done.5, pred[]{:T(512)S(6)} %eq.20, f32[256,2,2,1024]{3,0,2,1:T(8,128)} %bitcast.106, pred[]{:T(512)S(6)} %eq.10), kind=kLoop, calls=%fused_computation.41 | loop fusion | flops 2097152 | bytes 12582914 | tf_op jit(solution)/shard_map/add | solution.py:72
  94.4 0.2 select_bitcast_fusion
  94.5 3.1 %collective-permute-start.6 = (f32[256,1024]{1,0:T(8,128)S(1)}, f32[256,1024]{1,0:T(8,128)S(1)}, u32[]{:S(2)}, u32[]{:S(2)}) collective-permute-start(f32[256,1024]{1,0:T(8,128)S(1)} %select_bitcast_fusion), channel_id=1, source_target_pairs={{0,4},{1,3},{2,6},{3,1},{4,0},{5,7},{6,2},{7,5},{8,12},{9,11},{10,... | collective-permute-start | bytes 3145736 | tf_op jit(solution)/shard_map/ppermute | solution.py:75
  97.6 12.8 %collective-permute-done.6 = f32[256,1024]{1,0:T(8,128)S(1)} collective-permute-done((f32[256,1024]{1,0:T(8,128)S(1)}, f32[256,1024]{1,0:T(8,128)S(1)}, u32[]{:S(2)}, u32[]{:S(2)}) %collective-permute-start.6) | collective-permute-done | bytes 1048608 | tf_op jit(solution)/shard_map/ppermute | solution.py:75
  110.4 0.3 bitcast_add_fusion.1
  110.7 0.7 broadcast_in_dim.2
  111.4 0.0 reduce-scatter.4.cloned.1.call-done
  111.5 2.3 copy.27
  113.8 3.1 %pad_maximum_fusion = f32[512,1,1024]{2,1,0:T(1,128)} fusion(f32[256,1,1024]{2,1,0:T(1,128)S(1)} %broadcast_in_dim.2, f32[256,1,1024]{2,1,0:T(1,128)S(1)} %copy.27), kind=kLoop, calls=%fused_computation.30 | loop fusion | flops 524288 | bytes 4194304 | tf_op jit(solution)/shard_map/concatenate | solution.py:114
  116.9 4.6 %copy.28 = f32[512,1,1024]{0,2,1:T(8,128)S(1)} copy(f32[512,1,1024]{2,1,0:T(1,128)} %pad_maximum_fusion) | data formatting | bytes 4194304 | tf_op jit(solution)/shard_map/layout_constraint | solution.py:123
  121.4 1.1 fusion.27
  122.6 13.4 %psum.21 = f32[]{:T(128)} all-reduce(f32[]{:T(128)} %fusion.27), channel_id=1, replica_groups=mesh['island'=4,'chip'=4,'core'=2] {'chip','core'}, use_global_device_ids=true, to_apply=%region_2.3 | all-reduce | flops 1 | bytes 8 | tf_op jit(solution)/shard_map/psum | solution.py:127
  136.7 6.6 %fusion.39 = (f32[1024]{0:T(1024)S(1)}, f32[1024,512]{1,0:T(8,128)}) fusion(f32[1024,512]{1,0:T(8,128)} %param.10, f32[1,1024,512]{2,1,0:T(8,128)} %param.14, f32[]{:T(128)S(6)} %sqrt.9, f32[512,1,1024]{0,2,1:T(8,128)S(1)} %copy.28, f32[1,1024,512]{2,1,0:T(8,128)} %param.13, f32[1,1024,512]{2,1,0:T(8,128)} %param.12), kind=kLoop, calls=%fused_computation.75 | loop fusion | flops 9436160 | bytes 12587012 | tf_op jit(solution)/shard_map/reduce_sum | solution.py:53
  143.4 0.0 copy-start.3
  143.4 0.0 copy-start
  143.4 0.0 all-reduce.3.cloned.1.call-update
  143.4 0.6 copy-done.3
  144.0 0.1 copy.29
  144.1 0.1 reduce-window.8
  144.2 0.1 reduce
  144.3 0.4 convolution_bitcast_fusion
  144.7 42.3 %psum.23 = f32[48]{0:T(128)S(1)} all-reduce(f32[48]{0:T(128)S(1)} %convolution_bitcast_fusion), channel_id=1, replica_groups=mesh['island'=4,'chip'=4,'core'=2] {'island','chip','core'}, use_global_device_ids=true, to_apply=%region_6.7 | all-reduce | flops 48 | bytes 384 | tf_op jit(solution)/shard_map/psum | solution.py:137
  187.0 0.5 rsqrt_multiply_fusion
  187.5 43.2 %all-reduce.3.cloned.1.call-done = f32[1024,512]{1,0:T(8,128)} async-done(((f32[1024,512]{1,0:T(8,128)}), f32[1024,512]{1,0:T(8,128)}) %all-reduce.3.cloned.1.call-update) | async-done | bytes 2097168 | tf_op jit(solution)/shard_map/psum | solution.py:132
  230.7 0.0 copy-done
  230.7 5.0 %multiply_subtract_fusion = (f32[1024,512]{1,0:T(8,128)}, f32[1024,512]{1,0:T(8,128)}) fusion(f32[1024,512]{1,0:T(8,128)S(1)} %copy-done, f32[1024,512]{1,0:T(8,128)} %all-reduce.3.cloned.1.call-done, f32[1024,512]{1,0:T(8,128)} %param.11), kind=kLoop, calls=%fused_computation.39 | loop fusion | flops 3670016 | bytes 10485760 | tf_op jit(solution)/shard_map/sub | solution.py:134
  (5 shorter events, 0.1 us)
Async XLA Ops:
  7.2 104.3 %reduce-scatter.4.cloned.1.call-start = ((), (), s32[]{:S(2)}) async-start(), calls=%async_computation.2 | async-start | bytes 5242880
  13.5 8.1 %collective-permute-start.1 = (bf16[512,1024]{1,0:T(8,128)(2,1)}, bf16[512,1024]{1,0:T(8,128)(2,1)}, u32[]{:S(2)}, u32[]{:S(2)}) collective-permute-start(bf16[512,1024]{1,0:T(8,128)(2,1)} %get-tuple-element.9), channel_id=1, source_target_pairs={{0,1},{1,0},{2,3},{3,2},{4,5},{5,4},{6,7},{7,6},{8,9},{9,8},{10,11... | collective-permute-start | bytes 3145736 | tf_op jit(solution)/shard_map/ppermute | solution.py:103
  14.0 7.7 %collective-permute-start.2 = (bf16[512,1024]{1,0:T(8,128)(2,1)}, bf16[512,1024]{1,0:T(8,128)(2,1)}, u32[]{:S(2)}, u32[]{:S(2)}) collective-permute-start(bf16[512,1024]{1,0:T(8,128)(2,1)} %get-tuple-element.10), channel_id=1, source_target_pairs={{0,1},{1,0},{2,3},{3,2},{4,5},{5,4},{6,7},{7,6},{8,9},{9,8},{10,11... | collective-permute-start | bytes 3145736 | tf_op jit(solution)/shard_map/ppermute | solution.py:103
  14.1 7.7 %collective-permute-start.3 = (bf16[512,1024]{1,0:T(8,128)(2,1)S(1)}, bf16[512,1024]{1,0:T(8,128)(2,1)}, u32[]{:S(2)}, u32[]{:S(2)}) collective-permute-start(bf16[512,1024]{1,0:T(8,128)(2,1)S(1)} %get-tuple-element.16), channel_id=1, source_target_pairs={{0,1},{1,0},{2,3},{3,2},{4,5},{5,4},{6,7},{7,6},{8,9},{9,8},{10,11... | collective-permute-start | bytes 3145736 | tf_op jit(solution)/shard_map/ppermute | solution.py:103
  14.5 7.2 %collective-permute-start.4 = (bf16[512,1024]{1,0:T(8,128)(2,1)S(1)}, bf16[512,1024]{1,0:T(8,128)(2,1)}, u32[]{:S(2)}, u32[]{:S(2)}) collective-permute-start(bf16[512,1024]{1,0:T(8,128)(2,1)S(1)} %get-tuple-element.15), channel_id=1, source_target_pairs={{0,1},{1,0},{2,3},{3,2},{4,5},{5,4},{6,7},{7,6},{8,9},{9,8},{10,11... | collective-permute-start | bytes 3145736 | tf_op jit(solution)/shard_map/ppermute | solution.py:103
  16.4 1.2 copy-start.1
  16.4 1.5 copy-start.2
  16.6 5.1 %collective-permute-start = (bf16[512,512]{0,1:T(8,128)(2,1)S(1)}, bf16[512,512]{0,1:T(8,128)(2,1)S(1)}, u32[]{:S(2)}, u32[]{:S(2)}) collective-permute-start(bf16[512,512]{0,1:T(8,128)(2,1)S(1)} %bitcast.108), channel_id=1, source_target_pairs={{0,1},{1,0},{2,3},{3,2},{4,5},{5,4},{6,7},{7,6},{8,9},{9,8},{10,11... | collective-permute-start | bytes 1572872 | tf_op jit(solution)/shard_map/ppermute | solution.py:104
  30.0 200.7 %all-reduce.3.cloned.1.call-start = ((), (), s32[]{:S(2)}) async-start(), calls=%async_computation.1 | async-start | bytes 4194304 | tf_op jit(solution)/shard_map/psum | solution.py:132
  36.3 53.4 %collective-permute-start.5 = (f32[256,2,1024]{2,0,1:T(8,128)}, f32[256,2,1024]{2,0,1:T(8,128)S(1)}, u32[]{:S(2)}, u32[]{:S(2)}) collective-permute-start(f32[256,2,1024]{2,0,1:T(8,128)} %broadcast_select_fusion), channel_id=1, source_target_pairs={{0,2},{1,5},{2,0},{3,7},{4,6},{5,1},{6,4},{7,3},{8,10},{9,13},{10,... | collective-permute-start | bytes 6291464 | tf_op jit(solution)/shard_map/ppermute | solution.py:72
  94.5 15.8 %collective-permute-start.6 = (f32[256,1024]{1,0:T(8,128)S(1)}, f32[256,1024]{1,0:T(8,128)S(1)}, u32[]{:S(2)}, u32[]{:S(2)}) collective-permute-start(f32[256,1024]{1,0:T(8,128)S(1)} %select_bitcast_fusion), channel_id=1, source_target_pairs={{0,4},{1,3},{2,6},{3,1},{4,0},{5,7},{6,2},{7,5},{8,12},{9,11},{10,... | collective-permute-start | bytes 3145736 | tf_op jit(solution)/shard_map/ppermute | solution.py:75
  143.4 0.7 copy-start.3
  143.4 87.3 %copy-start = (f32[1024,512]{1,0:T(8,128)S(1)}, f32[1024,512]{1,0:T(8,128)}, u32[]{:S(2)}) copy-start(f32[1024,512]{1,0:T(8,128)} %param.10) | copy-start | bytes 6291460
Sparse Core Ops, SparseCore 0:
  30.1 68.5 reduce-scatter.3
  143.5 87.1 all-reduce.2

commit v10 on v9

--- a/solution.py
+++ b/solution.py
@@ -109,21 +109,23 @@
         their_unrotated, jnp.stack(their_tokens, axis=1), contract,
         preferred_element_type=jnp.float32,
     )
+    def rows_major(block):
+        block = with_layout_constraint(block, Layout((0, 1, 2)))
+        return with_layout_constraint(block.reshape(block.shape[0], own_rows).T, Layout((0, 1)))
+
     if chips == 4:
         split = partial.shape[0] // 2
         gradient = jnp.concatenate(
             [
-                lax.psum_scatter(partial[:split], "chip", scatter_dimension=1, tiled=True),
-                chip_scatter(partial[split:], chips),
+                rows_major(
+                    lax.psum_scatter(partial[:split], "chip", scatter_dimension=1, tiled=True)
+                ),
+                rows_major(chip_scatter(partial[split:], chips)),
             ],
-            axis=0,
+            axis=1,
         )
     else:
-        gradient = lax.psum_scatter(partial, "chip", scatter_dimension=1, tiled=True)
-    gradient = with_layout_constraint(gradient, Layout((0, 1, 2)))
-    gradient = with_layout_constraint(
-        gradient.reshape(gradient.shape[0], own_rows).T, Layout((0, 1))
-    )
+        gradient = rows_major(lax.psum_scatter(partial, "chip", scatter_dimension=1, tiled=True))
     squares = lax.psum(jnp.sum(gradient * gradient), ("chip", "core"))
     factor = 1.0 / jnp.sqrt(squares + norm_epsilon)
     inner = adam_update(gradient * factor, island_weights[0], first_moment[0], second_moment[0])

time: 243 us -> 234 us (0.963)
  local copies, waits for them, and re-layouts: 20.7 us -> 15 us
  other arithmetic: 28.6 us -> 25.4 us
    concatenate x1 -> x0, other arithmetic: 3.12 us -> none  [body(): jnp.concatenate([lax.psum_scatter(partial[:split], 'chip', scatter_dimens...]
    another operation x2 -> x3, local copies, waits for them, and re-layouts: 4.64 us -> 1.98 us  [the longest x2 1.89 us: rows_major(): block = with_layout_constraint(block, Layout((0, 1, 2)))]
where the time goes in v10:
time: 234 us
  waiting for transfers between devices  106 us (45%)
  blocking collectives  56 us (24%)
  other arithmetic  25.4 us (11%)
  local copies, waits for them, and re-layouts  15 us (6%)
  between operations  14.9 us (6%)
  matrix products  8.3 us (4%)
  starting transfers between devices  7.89 us (3%)
    ppermute x1, waiting for transfers between devices, chip_scatter(): held = keep + lax.ppermute(send, lanes, cross_first)  50.1 us
    psum x1, waiting for transfers between devices, body(): drift = lax.psum(island_drift, 'island') / replicas  43.2 us
    psum x1, blocking collectives, body(): lax.psum(local_tiles(island_drift, tile_rows, first_row), ('island', 'chi...  42.6 us
    psum x1, blocking collectives, body(): squares = lax.psum(jnp.sum(gradient * gradient), ('chip', 'core'))  13.3 us
    ppermute x1, waiting for transfers between devices, chip_scatter(): return (keep + lax.ppermute(send, lanes, cross_second))[:, None]  12.8 us
    reduce_sum x1, other arithmetic, local_tiles(): jnp.sum(drift_rows, axis=1)  6.65 us
    dynamic_slice x1, local copies, waits for them, and re-layouts, parity(): lax.dynamic_slice_in_dim(tokens, (2 * k + side) * own_rows, own_rows, axi...  6.32 us
    select_n x1, other arithmetic, chip_scatter(): send = jnp.where(first == 0, upper, lower)  5.96 us
  transfers between devices with their start and end apart: 9, of which 3 were waited for; matrix products, arithmetic and copies ran while one was open for 8% of the time, Pallas kernels for 0%

profile of v10, /device:TPU:0, one launch (start us, length us, event | category | flops | bytes accessed | tf_op | source)
XLA Modules:
  0.0 233.7 jit_solution(10005027074528637392)
XLA Ops:
  7.2 0.0 reduce-scatter.4.cloned.1.call-start
  7.2 6.3 %dynamic-slice_bitcast_fusion.3 = (bf16[512,1024]{1,0:T(8,128)(2,1)}, bf16[512,1024]{1,0:T(8,128)(2,1)}, bf16[512,1,1024]{2,0,1:T(8,128)(2,1)}, bf16[512,1,1024]...) fusion(bf16[1,512,8192]{2,1,0:T(8,128)(2,1)} %param.8, ...), kind=kLoop, calls=%fused_computation.46 | loop fusion | bytes 16777248 | tf_op jit(solution)/shard_map/dynamic_slice | solution.py:99
  13.5 0.5 collective-permute-start.1
  14.0 0.1 collective-permute-start.2
  14.1 0.5 collective-permute-start.3
  14.5 0.1 collective-permute-start.4
  14.6 0.5 multiply_cosine_fusion
  15.1 1.3 copy.35
  16.4 0.0 copy-start.1
  16.4 0.0 copy-start.2
  16.4 0.2 add_convert_fusion
  16.6 0.5 collective-permute-start
  17.2 0.5 copy-done.1
  17.6 0.3 copy-done.2
  17.9 3.7 %fusion = f32[512,4,1024]{2,0,1:T(8,128)S(1)} fusion(bf16[512,512,1]{0,1,2:T(8,128)(2,1)S(1)} %bitcast.108, bf16[512,1,1024]{2,0,1:T(8,128)(2,1)S(1)} %copy-done.1, bf16[512,1,1024]{2,0,1:T(8,128)(2,1)S(1)} %copy-done.2, bf16[512,1,1024]{2,0,1:T(8,128)(2,1)} %get-tuple-element.13, bf16[512,1,1024]{2,0,1:T(8,128)(2,1)} %get-tuple-element.14), kind=kOutput, calls=%fused_computation | convolution fusion | flops 2164260864 | bytes 13107200 | tf_op jit(solution)/shard_map/dot_general | solution.py:106
  21.7 0.0 collective-permute-done
  21.7 0.0 collective-permute-done.1
  21.7 0.0 collective-permute-done.2
  21.7 0.0 collective-permute-done.3
  21.7 0.0 collective-permute-done.4
  21.7 4.2 %fusion.16 = f32[512,4,1024]{2,0,1:T(8,128)S(1)} fusion(f32[512,4,1024]{2,0,1:T(8,128)S(1)} %fusion, bf16[512,1,1024]{2,0,1:T(8,128)(2,1)} %bitcast.16, bf16[512,1,1024]{2,0,1:T(8,128)(2,1)} %bitcast.14, bf16[512,1,1024]{2,0,1:T(8,128)(2,1)} %bitcast.12, bf16[512,1,1024]{2,0,1:T(8,128)(2,1)} %bitcast.10, bf16[512,512]{0,1:T(8,128)(2,1)S(1)} %collective-permute-done), kind=kOutput, calls=%fused_computation.17 | convolution fusion | flops 2166358016 | bytes 21495808 | tf_op jit(solution)/shard_map/dot_general | solution.py:108
  25.9 4.1 %fusion.40 = (f32[256,4,1024]{2,0,1:T(8,128)}, f32[256,4,1024]{2,0,1:T(8,128)}) fusion(f32[512,4,1024]{2,0,1:T(8,128)S(1)} %fusion.16), kind=kLoop, calls=%fused_computation.74 | loop fusion | bytes 16777216 | tf_op jit(solution)/shard_map/slice | solution.py:121
  30.0 0.0 reduce-scatter.4.cloned.1.call-update
  30.0 0.0 all-reduce.3.cloned.1.call-start
  30.1 6.0 %broadcast_select_fusion = f32[256,2,1024]{2,0,1:T(8,128)} fusion(pred[]{:T(512)S(6)} %eq.20, f32[256,2,2,1024]{3,0,2,1:T(8,128)} %bitcast.100, pred[]{:T(512)S(6)} %eq.10), kind=kLoop, calls=%fused_computation.51 | loop fusion | flops 1572864 | bytes 10485762 | tf_op jit(solution)/shard_map/jit(_where)/select_n | solution.py:71
  36.1 2.9 %collective-permute-start.5 = (f32[256,2,1024]{2,0,1:T(8,128)}, f32[256,2,1024]{2,0,1:T(8,128)S(1)}, u32[]{:S(2)}, u32[]{:S(2)}) collective-permute-start(f32[256,2,1024]{2,0,1:T(8,128)} %broadcast_select_fusion), channel_id=1, source_target_pairs={{0,2},{1,5},{2,0},{3,7},{4,6},{5,1},{6,4},{7,3},{8,10},{9,13},{10,... | collective-permute-start | bytes 6291464 | tf_op jit(solution)/shard_map/ppermute | solution.py:72
  39.0 50.1 %collective-permute-done.5 = f32[256,2,1024]{2,0,1:T(8,128)S(1)} collective-permute-done((f32[256,2,1024]{2,0,1:T(8,128)}, f32[256,2,1024]{2,0,1:T(8,128)S(1)}, u32[]{:S(2)}, u32[]{:S(2)}) %collective-permute-start.5) | collective-permute-done | bytes 2097184 | tf_op jit(solution)/shard_map/ppermute | solution.py:72
  89.1 4.7 %select_add_fusion = f32[256,2,1024]{2,0,1:T(8,128)S(1)} fusion(f32[256,2,1024]{2,0,1:T(8,128)S(1)} %collective-permute-done.5, pred[]{:T(512)S(6)} %eq.20, f32[256,2,2,1024]{3,0,2,1:T(8,128)} %bitcast.101, pred[]{:T(512)S(6)} %eq.10), kind=kLoop, calls=%fused_computation.39 | loop fusion | flops 2097152 | bytes 12582914 | tf_op jit(solution)/shard_map/add | solution.py:72
  93.8 0.1 select_bitcast_fusion
  94.0 3.3 %collective-permute-start.6 = (f32[256,1024]{1,0:T(8,128)S(1)}, f32[256,1024]{1,0:T(8,128)S(1)}, u32[]{:S(2)}, u32[]{:S(2)}) collective-permute-start(f32[256,1024]{1,0:T(8,128)S(1)} %select_bitcast_fusion), channel_id=1, source_target_pairs={{0,4},{1,3},{2,6},{3,1},{4,0},{5,7},{6,2},{7,5},{8,12},{9,11},{10,... | collective-permute-start | bytes 3145736 | tf_op jit(solution)/shard_map/ppermute | solution.py:75
  97.3 12.8 %collective-permute-done.6 = f32[256,1024]{1,0:T(8,128)S(1)} collective-permute-done((f32[256,1024]{1,0:T(8,128)S(1)}, f32[256,1024]{1,0:T(8,128)S(1)}, u32[]{:S(2)}, u32[]{:S(2)}) %collective-permute-start.6) | collective-permute-done | bytes 1048608 | tf_op jit(solution)/shard_map/ppermute | solution.py:75
  110.1 0.3 bitcast_add_fusion.1
  110.4 0.3 copy.34
  110.8 0.0 reduce-scatter.4.cloned.1.call-done
  110.8 1.6 copy.30
  112.3 1.1 multiply_reduce_fusion
  113.5 13.3 %psum.21 = f32[]{:T(128)} all-reduce(f32[]{:T(128)} %multiply_reduce_fusion), channel_id=1, replica_groups=mesh['island'=4,'chip'=4,'core'=2] {'chip','core'}, use_global_device_ids=true, to_apply=%region_2.3 | all-reduce | flops 1 | bytes 8 | tf_op jit(solution)/shard_map/psum | solution.py:129
  127.5 6.6 %fusion.38 = (f32[1024]{0:T(1024)S(1)}, f32[1024,512]{1,0:T(8,128)}) fusion(f32[1024,512]{1,0:T(8,128)} %param.10, f32[1,1024,512]{2,1,0:T(8,128)} %param.14, f32[]{:T(128)S(6)} %sqrt.9, f32[1024,256]{1,0:T(8,128)S(1)} %bitcast.103, f32[1024,256]{1,0:T(8,128)S(1)} %bitcast.105, f32[1,1024,512]{2,1,0:T(8,128)} %param.13, f32[1,1024,512]{2,1,0:T(8,128)} %param.12), kind=kLoop, calls=%fused_computation.73 | loop fusion | flops 9960448 | bytes 12587012 | tf_op jit(solution)/shard_map/reduce_sum | solution.py:53
  134.2 0.0 copy-start.3
  134.2 0.0 copy-start
  134.2 0.0 all-reduce.3.cloned.1.call-update
  134.2 0.6 copy-done.3
  134.8 0.1 copy.32
  134.9 0.1 reduce-window.8
  135.0 0.1 reduce
  135.1 0.4 convolution_bitcast_fusion
  135.5 42.6 %psum.23 = f32[48]{0:T(128)S(1)} all-reduce(f32[48]{0:T(128)S(1)} %convolution_bitcast_fusion), channel_id=1, replica_groups=mesh['island'=4,'chip'=4,'core'=2] {'island','chip','core'}, use_global_device_ids=true, to_apply=%region_6.7 | all-reduce | flops 48 | bytes 384 | tf_op jit(solution)/shard_map/psum | solution.py:139
  178.1 0.5 rsqrt_multiply_fusion
  178.7 43.2 %all-reduce.3.cloned.1.call-done = f32[1024,512]{1,0:T(8,128)} async-done(((f32[1024,512]{1,0:T(8,128)}), f32[1024,512]{1,0:T(8,128)}) %all-reduce.3.cloned.1.call-update) | async-done | bytes 2097168 | tf_op jit(solution)/shard_map/psum | solution.py:134
  221.8 0.0 copy-done
  221.8 5.0 %multiply_subtract_fusion = (f32[1024,512]{1,0:T(8,128)}, f32[1024,512]{1,0:T(8,128)}) fusion(f32[1024,512]{1,0:T(8,128)S(1)} %copy-done, f32[1024,512]{1,0:T(8,128)} %all-reduce.3.cloned.1.call-done, f32[1024,512]{1,0:T(8,128)} %param.11), kind=kLoop, calls=%fused_computation.36 | loop fusion | flops 3670016 | bytes 10485760 | tf_op jit(solution)/shard_map/sub | solution.py:136
  (5 shorter events, 0.1 us)
Async XLA Ops:
  7.2 103.6 %reduce-scatter.4.cloned.1.call-start = ((), (), s32[]{:S(2)}) async-start(), calls=%async_computation.2 | async-start | bytes 5242880
  13.5 8.1 %collective-permute-start.1 = (bf16[512,1024]{1,0:T(8,128)(2,1)}, bf16[512,1024]{1,0:T(8,128)(2,1)}, u32[]{:S(2)}, u32[]{:S(2)}) collective-permute-start(bf16[512,1024]{1,0:T(8,128)(2,1)} %get-tuple-element.9), channel_id=1, source_target_pairs={{0,1},{1,0},{2,3},{3,2},{4,5},{5,4},{6,7},{7,6},{8,9},{9,8},{10,11... | collective-permute-start | bytes 3145736 | tf_op jit(solution)/shard_map/ppermute | solution.py:103
  14.0 7.7 %collective-permute-start.2 = (bf16[512,1024]{1,0:T(8,128)(2,1)}, bf16[512,1024]{1,0:T(8,128)(2,1)}, u32[]{:S(2)}, u32[]{:S(2)}) collective-permute-start(bf16[512,1024]{1,0:T(8,128)(2,1)} %get-tuple-element.10), channel_id=1, source_target_pairs={{0,1},{1,0},{2,3},{3,2},{4,5},{5,4},{6,7},{7,6},{8,9},{9,8},{10,11... | collective-permute-start | bytes 3145736 | tf_op jit(solution)/shard_map/ppermute | solution.py:103
  14.1 7.7 %collective-permute-start.3 = (bf16[512,1024]{1,0:T(8,128)(2,1)S(1)}, bf16[512,1024]{1,0:T(8,128)(2,1)}, u32[]{:S(2)}, u32[]{:S(2)}) collective-permute-start(bf16[512,1024]{1,0:T(8,128)(2,1)S(1)} %get-tuple-element.16), channel_id=1, source_target_pairs={{0,1},{1,0},{2,3},{3,2},{4,5},{5,4},{6,7},{7,6},{8,9},{9,8},{10,11... | collective-permute-start | bytes 3145736 | tf_op jit(solution)/shard_map/ppermute | solution.py:103
  14.5 7.2 %collective-permute-start.4 = (bf16[512,1024]{1,0:T(8,128)(2,1)S(1)}, bf16[512,1024]{1,0:T(8,128)(2,1)}, u32[]{:S(2)}, u32[]{:S(2)}) collective-permute-start(bf16[512,1024]{1,0:T(8,128)(2,1)S(1)} %get-tuple-element.15), channel_id=1, source_target_pairs={{0,1},{1,0},{2,3},{3,2},{4,5},{5,4},{6,7},{7,6},{8,9},{9,8},{10,11... | collective-permute-start | bytes 3145736 | tf_op jit(solution)/shard_map/ppermute | solution.py:103
  16.4 1.2 copy-start.1
  16.4 1.5 copy-start.2
  16.6 5.0 %collective-permute-start = (bf16[512,512]{0,1:T(8,128)(2,1)S(1)}, bf16[512,512]{0,1:T(8,128)(2,1)S(1)}, u32[]{:S(2)}, u32[]{:S(2)}) collective-permute-start(bf16[512,512]{0,1:T(8,128)(2,1)S(1)} %bitcast.107), channel_id=1, source_target_pairs={{0,1},{1,0},{2,3},{3,2},{4,5},{5,4},{6,7},{7,6},{8,9},{9,8},{10,11... | collective-permute-start | bytes 1572872 | tf_op jit(solution)/shard_map/ppermute | solution.py:104
  30.0 191.8 %all-reduce.3.cloned.1.call-start = ((), (), s32[]{:S(2)}) async-start(), calls=%async_computation.1 | async-start | bytes 4194304 | tf_op jit(solution)/shard_map/psum | solution.py:134
  36.1 53.0 %collective-permute-start.5 = (f32[256,2,1024]{2,0,1:T(8,128)}, f32[256,2,1024]{2,0,1:T(8,128)S(1)}, u32[]{:S(2)}, u32[]{:S(2)}) collective-permute-start(f32[256,2,1024]{2,0,1:T(8,128)} %broadcast_select_fusion), channel_id=1, source_target_pairs={{0,2},{1,5},{2,0},{3,7},{4,6},{5,1},{6,4},{7,3},{8,10},{9,13},{10,... | collective-permute-start | bytes 6291464 | tf_op jit(solution)/shard_map/ppermute | solution.py:72
  94.0 16.1 %collective-permute-start.6 = (f32[256,1024]{1,0:T(8,128)S(1)}, f32[256,1024]{1,0:T(8,128)S(1)}, u32[]{:S(2)}, u32[]{:S(2)}) collective-permute-start(f32[256,1024]{1,0:T(8,128)S(1)} %select_bitcast_fusion), channel_id=1, source_target_pairs={{0,4},{1,3},{2,6},{3,1},{4,0},{5,7},{6,2},{7,5},{8,12},{9,11},{10,... | collective-permute-start | bytes 3145736 | tf_op jit(solution)/shard_map/ppermute | solution.py:75
  134.2 0.7 copy-start.3
  134.2 87.7 %copy-start = (f32[1024,512]{1,0:T(8,128)S(1)}, f32[1024,512]{1,0:T(8,128)}, u32[]{:S(2)}) copy-start(f32[1024,512]{1,0:T(8,128)} %param.10) | copy-start | bytes 6291460
Sparse Core Ops, SparseCore 0:
  30.1 68.2 reduce-scatter.3
  134.3 87.4 all-reduce.2

commit v11 on v10

--- a/solution.py
+++ b/solution.py
@@ -75,6 +75,14 @@
     return (keep + lax.ppermute(send, lanes, cross_second))[:, None]
 
 
+def island_tree(values):
+    island = lax.axis_index("island")
+    pair = values + lax.ppermute(values, "island", [(0, 1), (3, 2)])
+    whole = pair + lax.ppermute(pair, "island", [(1, 2), (2, 1)])
+    back = lax.ppermute(whole, "island", [(1, 0), (2, 3)])
+    return jnp.where((island == 1) | (island == 2), whole, back)
+
+
 def body(
     activations,
     key_cotangents,
@@ -131,12 +139,21 @@
     inner = adam_update(gradient * factor, island_weights[0], first_moment[0], second_moment[0])
     island_drift = master - inner
     replicas = lax.axis_size("island")
-    drift = lax.psum(island_drift, "island") / replicas
+    if replicas == 4:
+        split = own_rows * 5 // 8
+        drift = jnp.concatenate(
+            [lax.psum(island_drift[:split], "island"), island_tree(island_drift[split:])], axis=0
+        ) / replicas
+    else:
+        drift = lax.psum(island_drift, "island") / replicas
     momentum_out = outer_moment * momentum + drift
     master_out = master - outer_rate * (drift + outer_moment * momentum_out)
     first_row = position * own_rows
     totals = (
-        lax.psum(local_tiles(island_drift, tile_rows, first_row), ("island", "chip", "core"))
+        lax.psum(
+            lax.psum(lax.psum(local_tiles(island_drift, tile_rows, first_row), "core"), "chip"),
+            "island",
+        )
         / replicas
     )
     tile_sums = totals / jnp.sqrt(tile_rows.astype(jnp.float32) * master.shape[1])

time: 234 us -> 252 us (1.077)
  blocking collectives: 56 us -> 90.3 us
  waiting for transfers between devices: 106 us -> 79.2 us
  starting transfers between devices: 7.89 us -> 14.5 us
    psum x1, waiting for transfers between devices: 43.2 us -> 0.02 us  [body(): lax.psum(island_drift[:split], 'island')]
    psum x1 -> x3, blocking collectives: 42.6 us -> 76.9 us  [the longest x1 66.5 us: body(): lax.psum(lax.psum(lax.psum(local_tiles(island_drift, tile_rows, first_row...]
    ppermute x0 -> x3, waiting for transfers between devices: none -> 16.3 us  [the longest x1 16.2 us: island_tree(): pair = values + lax.ppermute(values, 'island', [(0, 1), (3, 2)])]
    ppermute x0 -> x3, starting transfers between devices: none -> 6.61 us  [the longest x1 3.71 us: island_tree(): pair = values + lax.ppermute(values, 'island', [(0, 1), (3, 2)])]
  transfers between devices with their start and end apart: 9 -> 12, of which waited for: 3 -> 3; matrix products, arithmetic and copies ran while one was open for 8% -> 9% of each run, Pallas kernels for 0% -> 0%
where the time goes in v11:
time: 252 us; the launch traced here: 250 us
  blocking collectives  90.3 us (36%)
  waiting for transfers between devices  79.2 us (31%)
  other arithmetic  27.1 us (11%)
  local copies, waits for them, and re-layouts  15.6 us (6%)
  between operations  15 us (6%)
  starting transfers between devices  14.5 us (6%)
  matrix products  8.3 us (3%)
    psum x1, blocking collectives, body(): lax.psum(lax.psum(lax.psum(local_tiles(island_drift, tile_rows, first_row...  66.5 us
    ppermute x1, waiting for transfers between devices, chip_scatter(): held = keep + lax.ppermute(send, lanes, cross_first)  50.1 us
    ppermute x1, waiting for transfers between devices, island_tree(): pair = values + lax.ppermute(values, 'island', [(0, 1), (3, 2)])  16.2 us
    psum x1, blocking collectives, body(): squares = lax.psum(jnp.sum(gradient * gradient), ('chip', 'core'))  13.3 us
    ppermute x1, waiting for transfers between devices, chip_scatter(): return (keep + lax.ppermute(send, lanes, cross_second))[:, None]  12.8 us
    psum x1, blocking collectives, body(): lax.psum(lax.psum(local_tiles(island_drift, tile_rows, first_row), 'core'...  7.95 us
    dynamic_slice x1, local copies, waits for them, and re-layouts, parity(): lax.dynamic_slice_in_dim(tokens, (2 * k + side) * own_rows, own_rows, axi...  6.32 us
    select_n x1, other arithmetic, chip_scatter(): send = jnp.where(first == 0, upper, lower)  5.96 us
  transfers between devices with their start and end apart: 12, of which 3 were waited for; matrix products, arithmetic and copies ran while one was open for 9% of the time, Pallas kernels for 0%

profile of v11, /device:TPU:0, one launch (start us, length us, event | category | flops | bytes accessed | tf_op | source)
XLA Modules:
  0.0 250.0 jit_solution(5512764259260002944)
XLA Ops:
  7.2 0.0 reduce-scatter.4.cloned.1.call-start
  7.2 6.3 %dynamic-slice_bitcast_fusion.3 = (bf16[512,1024]{1,0:T(8,128)(2,1)}, bf16[512,1024]{1,0:T(8,128)(2,1)}, bf16[512,1,1024]{2,0,1:T(8,128)(2,1)}, bf16[512,1,1024]...) fusion(bf16[1,512,8192]{2,1,0:T(8,128)(2,1)} %param.8, ...), kind=kLoop, calls=%fused_computation.47 | loop fusion | bytes 16777248 | tf_op jit(solution)/shard_map/dynamic_slice | solution.py:107
  13.5 0.5 collective-permute-start.1
  14.0 0.1 collective-permute-start.2
  14.1 0.5 collective-permute-start.3
  14.5 0.1 collective-permute-start.4
  14.6 0.5 multiply_cosine_fusion
  15.1 1.3 copy.35
  16.4 0.0 copy-start.3
  16.4 0.0 copy-start.4
  16.4 0.2 add_convert_fusion
  16.6 0.5 collective-permute-start
  17.2 0.5 copy-done.3
  17.6 0.3 copy-done.4
  17.9 3.7 %fusion = f32[512,4,1024]{2,0,1:T(8,128)S(1)} fusion(bf16[512,512,1]{0,1,2:T(8,128)(2,1)S(1)} %bitcast.108, bf16[512,1,1024]{2,0,1:T(8,128)(2,1)S(1)} %copy-done.3, bf16[512,1,1024]{2,0,1:T(8,128)(2,1)S(1)} %copy-done.4, bf16[512,1,1024]{2,0,1:T(8,128)(2,1)} %get-tuple-element.13, bf16[512,1,1024]{2,0,1:T(8,128)(2,1)} %get-tuple-element.14), kind=kOutput, calls=%fused_computation | convolution fusion | flops 2164260864 | bytes 13107200 | tf_op jit(solution)/shard_map/dot_general | solution.py:114
  21.7 0.0 collective-permute-done
  21.7 0.0 collective-permute-done.1
  21.7 0.0 collective-permute-done.2
  21.7 0.0 collective-permute-done.3
  21.7 0.0 collective-permute-done.4
  21.7 4.2 %fusion.16 = f32[512,4,1024]{2,0,1:T(8,128)S(1)} fusion(f32[512,4,1024]{2,0,1:T(8,128)S(1)} %fusion, bf16[512,1,1024]{2,0,1:T(8,128)(2,1)} %bitcast.16, bf16[512,1,1024]{2,0,1:T(8,128)(2,1)} %bitcast.14, bf16[512,1,1024]{2,0,1:T(8,128)(2,1)} %bitcast.12, bf16[512,1,1024]{2,0,1:T(8,128)(2,1)} %bitcast.10, bf16[512,512]{0,1:T(8,128)(2,1)S(1)} %collective-permute-done), kind=kOutput, calls=%fused_computation.17 | convolution fusion | flops 2166358016 | bytes 21495808 | tf_op jit(solution)/shard_map/dot_general | solution.py:116
  25.9 4.1 %fusion.40 = (f32[256,4,1024]{2,0,1:T(8,128)}, f32[256,4,1024]{2,0,1:T(8,128)}) fusion(f32[512,4,1024]{2,0,1:T(8,128)S(1)} %fusion.16), kind=kLoop, calls=%fused_computation.77 | loop fusion | bytes 16777216 | tf_op jit(solution)/shard_map/slice | solution.py:129
  30.0 0.0 reduce-scatter.4.cloned.1.call-update
  30.0 0.0 all-reduce.3.cloned.1.call-start
  30.1 6.0 %broadcast_select_fusion = f32[256,2,1024]{2,0,1:T(8,128)} fusion(pred[]{:T(512)S(6)} %eq.26, f32[256,2,2,1024]{3,0,2,1:T(8,128)} %bitcast.100, pred[]{:T(512)S(6)} %eq.24), kind=kLoop, calls=%fused_computation.52 | loop fusion | flops 1572864 | bytes 10485762 | tf_op jit(solution)/shard_map/jit(_where)/select_n | solution.py:71
  36.1 2.9 %collective-permute-start.5 = (f32[256,2,1024]{2,0,1:T(8,128)}, f32[256,2,1024]{2,0,1:T(8,128)S(1)}, u32[]{:S(2)}, u32[]{:S(2)}) collective-permute-start(f32[256,2,1024]{2,0,1:T(8,128)} %broadcast_select_fusion), channel_id=1, source_target_pairs={{0,2},{1,5},{2,0},{3,7},{4,6},{5,1},{6,4},{7,3},{8,10},{9,13},{10,... | collective-permute-start | bytes 6291464 | tf_op jit(solution)/shard_map/ppermute | solution.py:72
  39.0 50.1 %collective-permute-done.5 = f32[256,2,1024]{2,0,1:T(8,128)S(1)} collective-permute-done((f32[256,2,1024]{2,0,1:T(8,128)}, f32[256,2,1024]{2,0,1:T(8,128)S(1)}, u32[]{:S(2)}, u32[]{:S(2)}) %collective-permute-start.5) | collective-permute-done | bytes 2097184 | tf_op jit(solution)/shard_map/ppermute | solution.py:72
  89.1 4.7 %select_add_fusion = f32[256,2,1024]{2,0,1:T(8,128)S(1)} fusion(f32[256,2,1024]{2,0,1:T(8,128)S(1)} %collective-permute-done.5, pred[]{:T(512)S(6)} %eq.26, f32[256,2,2,1024]{3,0,2,1:T(8,128)} %bitcast.101, pred[]{:T(512)S(6)} %eq.24), kind=kLoop, calls=%fused_computation.40 | loop fusion | flops 2097152 | bytes 12582914 | tf_op jit(solution)/shard_map/add | solution.py:72
  93.8 0.1 select_bitcast_fusion
  94.0 3.3 %collective-permute-start.6 = (f32[256,1024]{1,0:T(8,128)S(1)}, f32[256,1024]{1,0:T(8,128)S(1)}, u32[]{:S(2)}, u32[]{:S(2)}) collective-permute-start(f32[256,1024]{1,0:T(8,128)S(1)} %select_bitcast_fusion), channel_id=1, source_target_pairs={{0,4},{1,3},{2,6},{3,1},{4,0},{5,7},{6,2},{7,5},{8,12},{9,11},{10,... | collective-permute-start | bytes 3145736 | tf_op jit(solution)/shard_map/ppermute | solution.py:75
  97.3 12.8 %collective-permute-done.6 = f32[256,1024]{1,0:T(8,128)S(1)} collective-permute-done((f32[256,1024]{1,0:T(8,128)S(1)}, f32[256,1024]{1,0:T(8,128)S(1)}, u32[]{:S(2)}, u32[]{:S(2)}) %collective-permute-start.6) | collective-permute-done | bytes 1048608 | tf_op jit(solution)/shard_map/ppermute | solution.py:75
  110.1 0.3 bitcast_add_fusion.1
  110.4 0.3 copy.34
  110.8 0.0 reduce-scatter.4.cloned.1.call-done
  110.8 1.6 copy.30
  112.3 1.1 multiply_reduce_fusion
  113.5 13.3 %psum.35 = f32[]{:T(128)} all-reduce(f32[]{:T(128)} %multiply_reduce_fusion), channel_id=1, replica_groups=mesh['island'=4,'chip'=4,'core'=2] {'chip','core'}, use_global_device_ids=true, to_apply=%region_2.3 | all-reduce | flops 1 | bytes 8 | tf_op jit(solution)/shard_map/psum | solution.py:137
  127.5 5.4 %fusion.38 = (f32[1024]{0:T(1024)S(1)}, f32[1024,512]{1,0:T(8,128)S(1)}) fusion(f32[1024,512]{1,0:T(8,128)} %param.10, f32[1,1024,512]{2,1,0:T(8,128)} %param.14, f32[]{:T(128)S(6)} %sqrt.9, f32[1024,256]{1,0:T(8,128)S(1)} %bitcast.103, f32[1024,256]{1,0:T(8,128)S(1)} %bitcast.105, f32[1,1024,512]{2,1,0:T(8,128)} %param.13, f32[1,1024,512]{2,1,0:T(8,128)} %param.12), kind=kLoop, calls=%fused_computation.76 | loop fusion | flops 9960448 | bytes 12587012 | tf_op jit(solution)/shard_map/reduce_sum | solution.py:53
  132.9 0.1 slice.61
  133.0 3.7 %collective-permute-start.7 = (f32[384,512]{1,0:T(8,128)S(1)}, f32[384,512]{1,0:T(8,128)S(1)}, u32[]{:S(2)}, u32[]{:S(2)}) collective-permute-start(f32[384,512]{1,0:T(8,128)S(1)} %slice.61), channel_id=1, source_target_pairs={{0,8},{24,16},{1,9},{25,17},{2,10},{26,18},{3,11},{27,19},{4,12},{... | collective-permute-start | bytes 2359304 | tf_op jit(solution)/shard_map/ppermute | solution.py:80
  136.7 16.2 %collective-permute-done.7 = f32[384,512]{1,0:T(8,128)S(1)} collective-permute-done((f32[384,512]{1,0:T(8,128)S(1)}, f32[384,512]{1,0:T(8,128)S(1)}, u32[]{:S(2)}, u32[]{:S(2)}) %collective-permute-start.7) | collective-permute-done | bytes 786464 | tf_op jit(solution)/shard_map/ppermute | solution.py:80
  152.9 0.1 slice_add_fusion
  153.1 0.0 copy-start.2
  153.1 1.6 collective-permute-start.8
  154.7 1.1 slice.60
  155.9 0.0 all-reduce.3.cloned.1.call-update
  155.9 0.0 copy-start
  155.9 0.0 collective-permute-done.8
  155.9 1.7 add.167
  157.6 0.0 copy-start.1
  157.6 1.3 collective-permute-start.9
  158.9 0.1 copy.32
  159.0 0.1 reduce-window.8
  159.1 0.1 reduce
  159.2 0.4 convolution_bitcast_fusion
  159.6 2.5 psum.37
  162.1 7.9 %psum.38 = f32[48]{0:T(128)S(1)} all-reduce(f32[48]{0:T(128)S(1)} %psum.37), channel_id=1, replica_groups=mesh['island'=4,'chip'=4,'core'=2] {'chip'}, use_global_device_ids=true, to_apply=%region_7.8 | all-reduce | flops 48 | bytes 384 | tf_op jit(solution)/shard_map/psum | solution.py:154
  170.0 66.5 %psum.39 = f32[48]{0:T(128)S(1)} all-reduce(f32[48]{0:T(128)S(1)} %psum.38), channel_id=1, replica_groups=mesh['island'=4,'chip'=4,'core'=2] {'island'}, use_global_device_ids=true, to_apply=%region_8.9 | all-reduce | flops 48 | bytes 384 | tf_op jit(solution)/shard_map/psum | solution.py:153
  236.5 0.5 rsqrt_multiply_fusion
  237.0 0.0 copy-done.1
  237.0 0.0 collective-permute-done.9
  237.1 1.3 broadcast_select_fusion.1
  238.3 0.0 all-reduce.3.cloned.1.call-done
  238.4 4.8 %multiply_subtract_fusion = (f32[1024,512]{1,0:T(8,128)}, f32[1024,512]{1,0:T(8,128)}) fusion(f32[1024,512]{1,0:T(8,128)S(1)} %copy-done, f32[384,512]{1,0:T(8,128)S(1)} %broadcast_select_fusion.1, f32[640,512]{1,0:T(8,128)} %all-reduce.3.cloned.1.call-done, f32[1024,512]{1,0:T(8,128)} %param.11), kind=kLoop, calls=%fused_computation.37 | loop fusion | flops 4194304 | bytes 10485760 | tf_op jit(solution)/shard_map/sub | solution.py:150
  (9 shorter events, 0.1 us)
Async XLA Ops:
  7.2 103.6 %reduce-scatter.4.cloned.1.call-start = ((), (), s32[]{:S(2)}) async-start(), calls=%async_computation.2 | async-start | bytes 5242880
  13.5 8.1 %collective-permute-start.1 = (bf16[512,1024]{1,0:T(8,128)(2,1)}, bf16[512,1024]{1,0:T(8,128)(2,1)}, u32[]{:S(2)}, u32[]{:S(2)}) collective-permute-start(bf16[512,1024]{1,0:T(8,128)(2,1)} %get-tuple-element.9), channel_id=1, source_target_pairs={{0,1},{1,0},{2,3},{3,2},{4,5},{5,4},{6,7},{7,6},{8,9},{9,8},{10,11... | collective-permute-start | bytes 3145736 | tf_op jit(solution)/shard_map/ppermute | solution.py:111
  14.0 7.7 %collective-permute-start.2 = (bf16[512,1024]{1,0:T(8,128)(2,1)}, bf16[512,1024]{1,0:T(8,128)(2,1)}, u32[]{:S(2)}, u32[]{:S(2)}) collective-permute-start(bf16[512,1024]{1,0:T(8,128)(2,1)} %get-tuple-element.10), channel_id=1, source_target_pairs={{0,1},{1,0},{2,3},{3,2},{4,5},{5,4},{6,7},{7,6},{8,9},{9,8},{10,11... | collective-permute-start | bytes 3145736 | tf_op jit(solution)/shard_map/ppermute | solution.py:111
  14.1 7.7 %collective-permute-start.3 = (bf16[512,1024]{1,0:T(8,128)(2,1)S(1)}, bf16[512,1024]{1,0:T(8,128)(2,1)}, u32[]{:S(2)}, u32[]{:S(2)}) collective-permute-start(bf16[512,1024]{1,0:T(8,128)(2,1)S(1)} %get-tuple-element.16), channel_id=1, source_target_pairs={{0,1},{1,0},{2,3},{3,2},{4,5},{5,4},{6,7},{7,6},{8,9},{9,8},{10,11... | collective-permute-start | bytes 3145736 | tf_op jit(solution)/shard_map/ppermute | solution.py:111
  14.5 7.2 %collective-permute-start.4 = (bf16[512,1024]{1,0:T(8,128)(2,1)S(1)}, bf16[512,1024]{1,0:T(8,128)(2,1)}, u32[]{:S(2)}, u32[]{:S(2)}) collective-permute-start(bf16[512,1024]{1,0:T(8,128)(2,1)S(1)} %get-tuple-element.15), channel_id=1, source_target_pairs={{0,1},{1,0},{2,3},{3,2},{4,5},{5,4},{6,7},{7,6},{8,9},{9,8},{10,11... | collective-permute-start | bytes 3145736 | tf_op jit(solution)/shard_map/ppermute | solution.py:111
  16.4 1.2 copy-start.3
  16.4 1.5 copy-start.4
  16.6 5.0 %collective-permute-start = (bf16[512,512]{0,1:T(8,128)(2,1)S(1)}, bf16[512,512]{0,1:T(8,128)(2,1)S(1)}, u32[]{:S(2)}, u32[]{:S(2)}) collective-permute-start(bf16[512,512]{0,1:T(8,128)(2,1)S(1)} %bitcast.107), channel_id=1, source_target_pairs={{0,1},{1,0},{2,3},{3,2},{4,5},{5,4},{6,7},{7,6},{8,9},{9,8},{10,11... | collective-permute-start | bytes 1572872 | tf_op jit(solution)/shard_map/ppermute | solution.py:112
  30.0 208.3 %all-reduce.3.cloned.1.call-start = ((), (), s32[]{:S(2)}) async-start(), calls=%async_computation.1 | async-start | bytes 2621440 | tf_op jit(solution)/shard_map/psum | solution.py:145
  36.1 53.0 %collective-permute-start.5 = (f32[256,2,1024]{2,0,1:T(8,128)}, f32[256,2,1024]{2,0,1:T(8,128)S(1)}, u32[]{:S(2)}, u32[]{:S(2)}) collective-permute-start(f32[256,2,1024]{2,0,1:T(8,128)} %broadcast_select_fusion), channel_id=1, source_target_pairs={{0,2},{1,5},{2,0},{3,7},{4,6},{5,1},{6,4},{7,3},{8,10},{9,13},{10,... | collective-permute-start | bytes 6291464 | tf_op jit(solution)/shard_map/ppermute | solution.py:72
  94.0 16.1 %collective-permute-start.6 = (f32[256,1024]{1,0:T(8,128)S(1)}, f32[256,1024]{1,0:T(8,128)S(1)}, u32[]{:S(2)}, u32[]{:S(2)}) collective-permute-start(f32[256,1024]{1,0:T(8,128)S(1)} %select_bitcast_fusion), channel_id=1, source_target_pairs={{0,4},{1,3},{2,6},{3,1},{4,0},{5,7},{6,2},{7,5},{8,12},{9,11},{10,... | collective-permute-start | bytes 3145736 | tf_op jit(solution)/shard_map/ppermute | solution.py:75
  133.0 20.0 %collective-permute-start.7 = (f32[384,512]{1,0:T(8,128)S(1)}, f32[384,512]{1,0:T(8,128)S(1)}, u32[]{:S(2)}, u32[]{:S(2)}) collective-permute-start(f32[384,512]{1,0:T(8,128)S(1)} %slice.61), channel_id=1, source_target_pairs={{0,8},{24,16},{1,9},{25,17},{2,10},{26,18},{3,11},{27,19},{4,12},{... | collective-permute-start | bytes 2359304 | tf_op jit(solution)/shard_map/ppermute | solution.py:80
  153.1 2.8 %copy-start.2 = (f32[384,512]{1,0:T(8,128)}, f32[384,512]{1,0:T(8,128)S(1)}, u32[]{:S(2)}) copy-start(f32[384,512]{1,0:T(8,128)S(1)} %slice_add_fusion) | copy-start | bytes 2359300
  153.1 2.8 %collective-permute-start.8 = (f32[384,512]{1,0:T(8,128)S(1)}, f32[384,512]{1,0:T(8,128)}, u32[]{:S(2)}, u32[]{:S(2)}) collective-permute-start(f32[384,512]{1,0:T(8,128)S(1)} %slice_add_fusion), channel_id=1, source_target_pairs={{8,16},{16,8},{9,17},{17,9},{10,18},{18,10},{11,19},{19,11},{12,20... | collective-permute-start | bytes 2359304 | tf_op jit(solution)/shard_map/ppermute | solution.py:81
  155.9 3.0 %copy-start.5 = (s32[48]{0:T(128)S(1)}, s32[48]{0:T(128)}, u32[]{:S(2)}) copy-start(s32[48]{0:T(128)} %param.15) | copy-start | bytes 580
  155.9 82.5 %copy-start = (f32[1024,512]{1,0:T(8,128)S(1)}, f32[1024,512]{1,0:T(8,128)}, u32[]{:S(2)}) copy-start(f32[1024,512]{1,0:T(8,128)} %param.10) | copy-start | bytes 6291460
  157.6 79.5 %copy-start.1 = (f32[384,512]{1,0:T(8,128)}, f32[384,512]{1,0:T(8,128)S(1)}, u32[]{:S(2)}) copy-start(f32[384,512]{1,0:T(8,128)S(1)} %add.167) | copy-start | bytes 2359300
  157.6 79.5 %collective-permute-start.9 = (f32[384,512]{1,0:T(8,128)S(1)}, f32[384,512]{1,0:T(8,128)}, u32[]{:S(2)}, u32[]{:S(2)}) collective-permute-start(f32[384,512]{1,0:T(8,128)S(1)} %add.167), channel_id=1, source_target_pairs={{8,0},{16,24},{9,1},{17,25},{10,2},{18,26},{11,3},{19,27},{12,4},{... | collective-permute-start | bytes 2359304 | tf_op jit(solution)/shard_map/ppermute | solution.py:82
Sparse Core Ops, SparseCore 0:
  30.1 68.2 reduce-scatter.3
  156.0 75.8 all-reduce.2

commit v12 on v11

--- a/solution.py
+++ b/solution.py
@@ -150,11 +150,7 @@
     master_out = master - outer_rate * (drift + outer_moment * momentum_out)
     first_row = position * own_rows
     totals = (
-        lax.psum(
-            lax.psum(lax.psum(local_tiles(island_drift, tile_rows, first_row), "core"), "chip"),
-            "island",
-        )
-        / replicas
+        lax.psum(local_tiles(drift, tile_rows, first_row), ("chip", "core"))
     )
     tile_sums = totals / jnp.sqrt(tile_rows.astype(jnp.float32) * master.shape[1])
     return (master_out, momentum_out, tile_sums)

time: 252 us -> 259 us (1.028)
  waiting for transfers between devices: 79.2 us -> 152 us
  blocking collectives: 90.3 us -> 26.5 us
    ppermute x1, waiting for transfers between devices: 0.01 us -> 73.1 us  [island_tree(): back = lax.ppermute(whole, 'island', [(1, 0), (2, 3)])]
    psum x3 -> x1, blocking collectives: 76.9 us -> 13.2 us  [body(): lax.psum(local_tiles(drift, tile_rows, first_row), ('chip', 'core'))]
    reduce_sum x1 -> x0, other arithmetic: 5.4 us -> none  [local_tiles(): jnp.sum(drift_rows, axis=1)]
    sub x0 -> x1, other arithmetic: none -> 5.17 us  [body(): island_drift = master - inner]
  transfers between devices with their start and end apart: 12 -> 12, of which waited for: 3 -> 4; matrix products, arithmetic and copies ran while one was open for 9% -> 8% of each run, Pallas kernels for 0% -> 0%
where the time goes in v12:
time: 259 us
  waiting for transfers between devices  152 us (59%)
  other arithmetic  26.6 us (10%)
  blocking collectives  26.5 us (10%)
  local copies, waits for them, and re-layouts  15.6 us (6%)
  between operations  15 us (6%)
  starting transfers between devices  14.5 us (6%)
  matrix products  8.3 us (3%)
    ppermute x1, waiting for transfers between devices, island_tree(): back = lax.ppermute(whole, 'island', [(1, 0), (2, 3)])  73.1 us
    ppermute x1, waiting for transfers between devices, chip_scatter(): held = keep + lax.ppermute(send, lanes, cross_first)  50.1 us
    ppermute x1, waiting for transfers between devices, island_tree(): pair = values + lax.ppermute(values, 'island', [(0, 1), (3, 2)])  16.2 us
    psum x1, blocking collectives, body(): squares = lax.psum(jnp.sum(gradient * gradient), ('chip', 'core'))  13.4 us
    psum x1, blocking collectives, body(): lax.psum(local_tiles(drift, tile_rows, first_row), ('chip', 'core'))  13.2 us
    ppermute x1, waiting for transfers between devices, chip_scatter(): return (keep + lax.ppermute(send, lanes, cross_second))[:, None]  12.8 us
    dynamic_slice x1, local copies, waits for them, and re-layouts, parity(): lax.dynamic_slice_in_dim(tokens, (2 * k + side) * own_rows, own_rows, axi...  6.33 us
    select_n x1, other arithmetic, chip_scatter(): send = jnp.where(first == 0, upper, lower)  5.96 us
  transfers between devices with their start and end apart: 12, of which 4 were waited for; matrix products, arithmetic and copies ran while one was open for 8% of the time, Pallas kernels for 0%

profile of v12, /device:TPU:0, one launch (start us, length us, event | category | flops | bytes accessed | tf_op | source)
XLA Modules:
  0.0 258.9 jit_solution(13738161734603605938)
XLA Ops:
  7.2 0.0 reduce-scatter.4.cloned.1.call-start
  7.2 6.3 %dynamic-slice_bitcast_fusion.3 = (bf16[512,1024]{1,0:T(8,128)(2,1)}, bf16[512,1024]{1,0:T(8,128)(2,1)}, bf16[512,1,1024]{2,0,1:T(8,128)(2,1)}, bf16[512,1,1024]...) fusion(bf16[1,512,8192]{2,1,0:T(8,128)(2,1)} %param.8, ...), kind=kLoop, calls=%fused_computation.48 | loop fusion | bytes 16777248 | tf_op jit(solution)/shard_map/dynamic_slice | solution.py:107
  13.6 0.5 collective-permute-start.1
  14.0 0.1 collective-permute-start.2
  14.1 0.5 collective-permute-start.3
  14.5 0.1 collective-permute-start.4
  14.6 0.5 multiply_cosine_fusion
  15.1 1.3 copy.35
  16.4 0.0 copy-start.3
  16.4 0.0 copy-start.4
  16.4 0.2 add_convert_fusion
  16.6 0.5 collective-permute-start
  17.2 0.5 copy-done.3
  17.6 0.3 copy-done.4
  17.9 3.7 %fusion = f32[512,4,1024]{2,0,1:T(8,128)S(1)} fusion(bf16[512,512,1]{0,1,2:T(8,128)(2,1)S(1)} %bitcast.105, bf16[512,1,1024]{2,0,1:T(8,128)(2,1)S(1)} %copy-done.3, bf16[512,1,1024]{2,0,1:T(8,128)(2,1)S(1)} %copy-done.4, bf16[512,1,1024]{2,0,1:T(8,128)(2,1)} %get-tuple-element.11, bf16[512,1,1024]{2,0,1:T(8,128)(2,1)} %get-tuple-element.12), kind=kOutput, calls=%fused_computation | convolution fusion | flops 2164260864 | bytes 13107200 | tf_op jit(solution)/shard_map/dot_general | solution.py:114
  21.7 0.0 collective-permute-done
  21.7 0.0 collective-permute-done.1
  21.7 0.0 collective-permute-done.2
  21.7 0.0 collective-permute-done.3
  21.7 0.0 collective-permute-done.4
  21.7 4.2 %fusion.16 = f32[512,4,1024]{2,0,1:T(8,128)S(1)} fusion(f32[512,4,1024]{2,0,1:T(8,128)S(1)} %fusion, bf16[512,1,1024]{2,0,1:T(8,128)(2,1)} %bitcast.16, bf16[512,1,1024]{2,0,1:T(8,128)(2,1)} %bitcast.14, bf16[512,1,1024]{2,0,1:T(8,128)(2,1)} %bitcast.12, bf16[512,1,1024]{2,0,1:T(8,128)(2,1)} %bitcast.10, bf16[512,512]{0,1:T(8,128)(2,1)S(1)} %collective-permute-done), kind=kOutput, calls=%fused_computation.17 | convolution fusion | flops 2166358016 | bytes 21495808 | tf_op jit(solution)/shard_map/dot_general | solution.py:116
  25.9 4.1 %fusion.39 = (f32[256,4,1024]{2,0,1:T(8,128)}, f32[256,4,1024]{2,0,1:T(8,128)}) fusion(f32[512,4,1024]{2,0,1:T(8,128)S(1)} %fusion.16), kind=kLoop, calls=%fused_computation.77 | loop fusion | bytes 16777216 | tf_op jit(solution)/shard_map/slice | solution.py:129
  30.0 0.0 reduce-scatter.4.cloned.1.call-update
  30.0 0.0 all-reduce.3.cloned.1.call-start
  30.1 6.0 %broadcast_select_fusion = f32[256,2,1024]{2,0,1:T(8,128)} fusion(pred[]{:T(512)S(6)} %eq.26, f32[256,2,2,1024]{3,0,2,1:T(8,128)} %bitcast.97, pred[]{:T(512)S(6)} %eq.24), kind=kLoop, calls=%fused_computation.53 | loop fusion | flops 1572864 | bytes 10485762 | tf_op jit(solution)/shard_map/jit(_where)/select_n | solution.py:71
  36.1 2.9 %collective-permute-start.5 = (f32[256,2,1024]{2,0,1:T(8,128)}, f32[256,2,1024]{2,0,1:T(8,128)S(1)}, u32[]{:S(2)}, u32[]{:S(2)}) collective-permute-start(f32[256,2,1024]{2,0,1:T(8,128)} %broadcast_select_fusion), channel_id=1, source_target_pairs={{0,2},{1,5},{2,0},{3,7},{4,6},{5,1},{6,4},{7,3},{8,10},{9,13},{10,... | collective-permute-start | bytes 6291464 | tf_op jit(solution)/shard_map/ppermute | solution.py:72
  39.0 50.1 %collective-permute-done.5 = f32[256,2,1024]{2,0,1:T(8,128)S(1)} collective-permute-done((f32[256,2,1024]{2,0,1:T(8,128)}, f32[256,2,1024]{2,0,1:T(8,128)S(1)}, u32[]{:S(2)}, u32[]{:S(2)}) %collective-permute-start.5) | collective-permute-done | bytes 2097184 | tf_op jit(solution)/shard_map/ppermute | solution.py:72
  89.1 4.7 %select_add_fusion = f32[256,2,1024]{2,0,1:T(8,128)S(1)} fusion(f32[256,2,1024]{2,0,1:T(8,128)S(1)} %collective-permute-done.5, pred[]{:T(512)S(6)} %eq.26, f32[256,2,2,1024]{3,0,2,1:T(8,128)} %bitcast.98, pred[]{:T(512)S(6)} %eq.24), kind=kLoop, calls=%fused_computation.40 | loop fusion | flops 2097152 | bytes 12582914 | tf_op jit(solution)/shard_map/add | solution.py:72
  93.8 0.1 select_bitcast_fusion
  94.0 3.3 %collective-permute-start.6 = (f32[256,1024]{1,0:T(8,128)S(1)}, f32[256,1024]{1,0:T(8,128)S(1)}, u32[]{:S(2)}, u32[]{:S(2)}) collective-permute-start(f32[256,1024]{1,0:T(8,128)S(1)} %select_bitcast_fusion), channel_id=1, source_target_pairs={{0,4},{1,3},{2,6},{3,1},{4,0},{5,7},{6,2},{7,5},{8,12},{9,11},{10,... | collective-permute-start | bytes 3145736 | tf_op jit(solution)/shard_map/ppermute | solution.py:75
  97.3 12.8 %collective-permute-done.6 = f32[256,1024]{1,0:T(8,128)S(1)} collective-permute-done((f32[256,1024]{1,0:T(8,128)S(1)}, f32[256,1024]{1,0:T(8,128)S(1)}, u32[]{:S(2)}, u32[]{:S(2)}) %collective-permute-start.6) | collective-permute-done | bytes 1048608 | tf_op jit(solution)/shard_map/ppermute | solution.py:75
  110.1 0.3 bitcast_add_fusion.1
  110.4 0.3 copy.34
  110.8 0.0 reduce-scatter.4.cloned.1.call-done
  110.8 1.6 copy.30
  112.3 1.1 multiply_reduce_fusion
  113.5 13.4 %psum.21 = f32[]{:T(128)} all-reduce(f32[]{:T(128)} %multiply_reduce_fusion), channel_id=1, replica_groups=mesh['island'=4,'chip'=4,'core'=2] {'chip','core'}, use_global_device_ids=true, to_apply=%region_2.3 | all-reduce | flops 1 | bytes 8 | tf_op jit(solution)/shard_map/psum | solution.py:137
  127.5 5.2 %fusion.28 = f32[1024,512]{1,0:T(8,128)S(1)} fusion(f32[1024,512]{1,0:T(8,128)} %param.10, f32[1,1024,512]{2,1,0:T(8,128)} %param.12, f32[1,1024,512]{2,1,0:T(8,128)} %param.14, f32[1,1024,512]{2,1,0:T(8,128)} %param.13, f32[1024,256]{1,0:T(8,128)S(1)} %bitcast.100, f32[1024,256]{1,0:T(8,128)S(1)} %bitcast.102, f32[]{:T(128)S(6)} %sqrt.9), kind=kLoop, calls=%fused_computation.36 | loop fusion | flops 9437184 | bytes 12582916 | tf_op jit(solution)/shard_map/sub | solution.py:140
  132.7 0.1 slice.61
  132.8 3.7 %collective-permute-start.7 = (f32[384,512]{1,0:T(8,128)S(1)}, f32[384,512]{1,0:T(8,128)S(1)}, u32[]{:S(2)}, u32[]{:S(2)}) collective-permute-start(f32[384,512]{1,0:T(8,128)S(1)} %slice.61), channel_id=1, source_target_pairs={{0,8},{24,16},{1,9},{25,17},{2,10},{26,18},{3,11},{27,19},{4,12},{... | collective-permute-start | bytes 2359304 | tf_op jit(solution)/shard_map/ppermute | solution.py:80
  136.5 16.2 %collective-permute-done.7 = f32[384,512]{1,0:T(8,128)S(1)} collective-permute-done((f32[384,512]{1,0:T(8,128)S(1)}, f32[384,512]{1,0:T(8,128)S(1)}, u32[]{:S(2)}, u32[]{:S(2)}) %collective-permute-start.7) | collective-permute-done | bytes 786464 | tf_op jit(solution)/shard_map/ppermute | solution.py:80
  152.7 0.1 slice_add_fusion
  152.9 0.0 copy-start.2
  152.9 1.6 collective-permute-start.8
  154.5 1.1 slice.60
  155.6 0.0 all-reduce.3.cloned.1.call-update
  155.6 0.0 copy-done.2
  155.6 0.0 copy-start
  155.7 0.0 collective-permute-done.8
  155.7 1.7 add.163
  157.3 0.0 copy-start.1
  157.3 1.3 collective-permute-start.9
  158.7 0.0 copy-done.5
  158.7 0.1 copy.32
  158.8 0.1 reduce-window.8
  158.8 0.1 reduce
  159.0 0.0 copy-done.1
  159.0 73.1 %collective-permute-done.9 = f32[384,512]{1,0:T(8,128)} collective-permute-done((f32[384,512]{1,0:T(8,128)S(1)}, f32[384,512]{1,0:T(8,128)}, u32[]{:S(2)}, u32[]{:S(2)}) %collective-permute-start.9) | collective-permute-done | bytes 786464 | tf_op jit(solution)/shard_map/ppermute | solution.py:82
  232.1 1.3 broadcast_select_fusion.1
  233.4 0.0 all-reduce.3.cloned.1.call-done
  233.4 4.6 %multiply_subtract_fusion = (f32[1024,512]{1,0:T(8,128)}, f32[1024,512]{1,0:T(8,128)}, f32[1024]{0:T(1024)S(1)}) fusion(f32[1024,512]{1,0:T(8,128)S(1)} %copy-done, f32[384,512]{1,0:T(8,128)S(1)} %broadcast_select_fusion.1, f32[640,512]{1,0:T(8,128)} %all-reduce.3.cloned.1.call-done, f32[1024,512]{1,0:T(8,128)} %param.11), kind=kLoop, calls=%fused_computation.37 | loop fusion | flops 4717568 | bytes 10489856 | tf_op jit(solution)/shard_map/sub | solution.py:150
  238.0 0.4 convolution_bitcast_fusion
  238.3 13.2 %psum.23 = f32[48]{0:T(128)S(1)} all-reduce(f32[48]{0:T(128)S(1)} %convolution_bitcast_fusion), channel_id=1, replica_groups=mesh['island'=4,'chip'=4,'core'=2] {'chip','core'}, use_global_device_ids=true, to_apply=%region_6.7 | all-reduce | flops 48 | bytes 384 | tf_op jit(solution)/shard_map/psum | solution.py:153
  251.5 0.5 rsqrt_multiply_fusion
  (7 shorter events, 0.1 us)
Async XLA Ops:
  7.2 103.6 %reduce-scatter.4.cloned.1.call-start = ((), (), s32[]{:S(2)}) async-start(), calls=%async_computation.2 | async-start | bytes 5242880
  13.6 8.1 %collective-permute-start.1 = (bf16[512,1024]{1,0:T(8,128)(2,1)}, bf16[512,1024]{1,0:T(8,128)(2,1)}, u32[]{:S(2)}, u32[]{:S(2)}) collective-permute-start(bf16[512,1024]{1,0:T(8,128)(2,1)} %get-tuple-element.7), channel_id=1, source_target_pairs={{0,1},{1,0},{2,3},{3,2},{4,5},{5,4},{6,7},{7,6},{8,9},{9,8},{10,11... | collective-permute-start | bytes 3145736 | tf_op jit(solution)/shard_map/ppermute | solution.py:111
  14.0 7.7 %collective-permute-start.2 = (bf16[512,1024]{1,0:T(8,128)(2,1)}, bf16[512,1024]{1,0:T(8,128)(2,1)}, u32[]{:S(2)}, u32[]{:S(2)}) collective-permute-start(bf16[512,1024]{1,0:T(8,128)(2,1)} %get-tuple-element.8), channel_id=1, source_target_pairs={{0,1},{1,0},{2,3},{3,2},{4,5},{5,4},{6,7},{7,6},{8,9},{9,8},{10,11... | collective-permute-start | bytes 3145736 | tf_op jit(solution)/shard_map/ppermute | solution.py:111
  14.1 7.7 %collective-permute-start.3 = (bf16[512,1024]{1,0:T(8,128)(2,1)S(1)}, bf16[512,1024]{1,0:T(8,128)(2,1)}, u32[]{:S(2)}, u32[]{:S(2)}) collective-permute-start(bf16[512,1024]{1,0:T(8,128)(2,1)S(1)} %get-tuple-element.14), channel_id=1, source_target_pairs={{0,1},{1,0},{2,3},{3,2},{4,5},{5,4},{6,7},{7,6},{8,9},{9,8},{10,11... | collective-permute-start | bytes 3145736 | tf_op jit(solution)/shard_map/ppermute | solution.py:111
  14.5 7.2 %collective-permute-start.4 = (bf16[512,1024]{1,0:T(8,128)(2,1)S(1)}, bf16[512,1024]{1,0:T(8,128)(2,1)}, u32[]{:S(2)}, u32[]{:S(2)}) collective-permute-start(bf16[512,1024]{1,0:T(8,128)(2,1)S(1)} %get-tuple-element.13), channel_id=1, source_target_pairs={{0,1},{1,0},{2,3},{3,2},{4,5},{5,4},{6,7},{7,6},{8,9},{9,8},{10,11... | collective-permute-start | bytes 3145736 | tf_op jit(solution)/shard_map/ppermute | solution.py:111
  16.4 1.2 copy-start.3
  16.4 1.5 copy-start.4
  16.6 5.0 %collective-permute-start = (bf16[512,512]{0,1:T(8,128)(2,1)S(1)}, bf16[512,512]{0,1:T(8,128)(2,1)S(1)}, u32[]{:S(2)}, u32[]{:S(2)}) collective-permute-start(bf16[512,512]{0,1:T(8,128)(2,1)S(1)} %bitcast.104), channel_id=1, source_target_pairs={{0,1},{1,0},{2,3},{3,2},{4,5},{5,4},{6,7},{7,6},{8,9},{9,8},{10,11... | collective-permute-start | bytes 1572872 | tf_op jit(solution)/shard_map/ppermute | solution.py:112
  30.0 203.3 %all-reduce.3.cloned.1.call-start = ((), (), s32[]{:S(2)}) async-start(), calls=%async_computation.1 | async-start | bytes 2621440 | tf_op jit(solution)/shard_map/psum | solution.py:145
  36.1 53.0 %collective-permute-start.5 = (f32[256,2,1024]{2,0,1:T(8,128)}, f32[256,2,1024]{2,0,1:T(8,128)S(1)}, u32[]{:S(2)}, u32[]{:S(2)}) collective-permute-start(f32[256,2,1024]{2,0,1:T(8,128)} %broadcast_select_fusion), channel_id=1, source_target_pairs={{0,2},{1,5},{2,0},{3,7},{4,6},{5,1},{6,4},{7,3},{8,10},{9,13},{10,... | collective-permute-start | bytes 6291464 | tf_op jit(solution)/shard_map/ppermute | solution.py:72
  94.0 16.1 %collective-permute-start.6 = (f32[256,1024]{1,0:T(8,128)S(1)}, f32[256,1024]{1,0:T(8,128)S(1)}, u32[]{:S(2)}, u32[]{:S(2)}) collective-permute-start(f32[256,1024]{1,0:T(8,128)S(1)} %select_bitcast_fusion), channel_id=1, source_target_pairs={{0,4},{1,3},{2,6},{3,1},{4,0},{5,7},{6,2},{7,5},{8,12},{9,11},{10,... | collective-permute-start | bytes 3145736 | tf_op jit(solution)/shard_map/ppermute | solution.py:75
  132.8 20.0 %collective-permute-start.7 = (f32[384,512]{1,0:T(8,128)S(1)}, f32[384,512]{1,0:T(8,128)S(1)}, u32[]{:S(2)}, u32[]{:S(2)}) collective-permute-start(f32[384,512]{1,0:T(8,128)S(1)} %slice.61), channel_id=1, source_target_pairs={{0,8},{24,16},{1,9},{25,17},{2,10},{26,18},{3,11},{27,19},{4,12},{... | collective-permute-start | bytes 2359304 | tf_op jit(solution)/shard_map/ppermute | solution.py:80
  152.9 2.8 %copy-start.2 = (f32[384,512]{1,0:T(8,128)}, f32[384,512]{1,0:T(8,128)S(1)}, u32[]{:S(2)}) copy-start(f32[384,512]{1,0:T(8,128)S(1)} %slice_add_fusion) | copy-start | bytes 2359300
  152.9 2.8 %collective-permute-start.8 = (f32[384,512]{1,0:T(8,128)S(1)}, f32[384,512]{1,0:T(8,128)}, u32[]{:S(2)}, u32[]{:S(2)}) collective-permute-start(f32[384,512]{1,0:T(8,128)S(1)} %slice_add_fusion), channel_id=1, source_target_pairs={{8,16},{16,8},{9,17},{17,9},{10,18},{18,10},{11,19},{19,11},{12,20... | collective-permute-start | bytes 2359304 | tf_op jit(solution)/shard_map/ppermute | solution.py:81
  155.6 3.0 %copy-start.5 = (s32[48]{0:T(128)S(1)}, s32[48]{0:T(128)}, u32[]{:S(2)}) copy-start(s32[48]{0:T(128)} %param.15) | copy-start | bytes 580
  155.6 77.7 %copy-start = (f32[1024,512]{1,0:T(8,128)S(1)}, f32[1024,512]{1,0:T(8,128)}, u32[]{:S(2)}) copy-start(f32[1024,512]{1,0:T(8,128)} %param.10) | copy-start | bytes 6291460
  157.3 1.6 copy-start.1
  157.3 74.7 %collective-permute-start.9 = (f32[384,512]{1,0:T(8,128)S(1)}, f32[384,512]{1,0:T(8,128)}, u32[]{:S(2)}, u32[]{:S(2)}) collective-permute-start(f32[384,512]{1,0:T(8,128)S(1)} %add.163), channel_id=1, source_target_pairs={{8,0},{16,24},{9,1},{17,25},{10,2},{18,26},{11,3},{19,27},{12,4},{... | collective-permute-start | bytes 2359304 | tf_op jit(solution)/shard_map/ppermute | solution.py:82
Sparse Core Ops, SparseCore 0:
  30.2 68.2 reduce-scatter.3
  155.8 75.7 all-reduce.2

commit v13 on v10

--- a/solution.py
+++ b/solution.py
@@ -53,7 +53,7 @@
     return jnp.dot(jnp.sum(drift_rows, axis=1), member, precision=lax.Precision.HIGHEST)
 
 
-def chip_scatter(partial, chips):
+def chip_scatter(partial, chips, tie):
     core = lax.axis_index("core")
     chip = lax.axis_index("chip")
     along_x, along_y = chip % 2, chip // 2
@@ -69,10 +69,11 @@
     upper = jnp.where(core == 0, by_x[1], by_y[1])
     keep = jnp.where(first == 0, lower, upper)
     send = jnp.where(first == 0, upper, lower)
+    send, tie = lax.optimization_barrier((send, tie))
     held = keep + lax.ppermute(send, lanes, cross_first)
     keep = jnp.where(second == 0, held[:, 0], held[:, 1])
     send = jnp.where(second == 0, held[:, 1], held[:, 0])
-    return (keep + lax.ppermute(send, lanes, cross_second))[:, None]
+    return (keep + lax.ppermute(send, lanes, cross_second))[:, None], tie
 
 
 def body(
@@ -103,29 +104,35 @@
     their_tokens = [lax.ppermute(block, "core", swap) for block in parity(1 - core)]
     their_unrotated = lax.ppermute(unrotated, "core", swap)
     contract = (((0,), (0,)), ((), ()))
-    partial = lax.dot_general(
-        unrotated, jnp.stack(parity(core), axis=1), contract, preferred_element_type=jnp.float32
-    ) + lax.dot_general(
-        their_unrotated, jnp.stack(their_tokens, axis=1), contract,
-        preferred_element_type=jnp.float32,
-    )
+    mine = jnp.stack(parity(core), axis=1)
+    theirs = jnp.stack(their_tokens, axis=1)
+
+    def product(own_lhs, their_lhs):
+        return lax.dot_general(
+            own_lhs, mine, contract, preferred_element_type=jnp.float32
+        ) + lax.dot_general(their_lhs, theirs, contract, preferred_element_type=jnp.float32)
+
     def rows_major(block):
         block = with_layout_constraint(block, Layout((0, 1, 2)))
         return with_layout_constraint(block.reshape(block.shape[0], own_rows).T, Layout((0, 1)))
 
     if chips == 4:
-        split = partial.shape[0] // 2
-        gradient = jnp.concatenate(
-            [
-                rows_major(
-                    lax.psum_scatter(partial[:split], "chip", scatter_dimension=1, tiled=True)
-                ),
-                rows_major(chip_scatter(partial[split:], chips)),
-            ],
-            axis=1,
+        split = unrotated.shape[1] // 2
+        sent, (own_lhs, their_lhs) = chip_scatter(
+            product(unrotated[:, split:], their_unrotated[:, split:]),
+            chips,
+            (unrotated, their_unrotated),
         )
+        summed = lax.psum_scatter(
+            product(own_lhs[:, :split], their_lhs[:, :split]), "chip", scatter_dimension=1, tiled=True
+        )
+        gradient = jnp.concatenate([rows_major(summed), rows_major(sent)], axis=1)
     else:
-        gradient = rows_major(lax.psum_scatter(partial, "chip", scatter_dimension=1, tiled=True))
+        gradient = rows_major(
+            lax.psum_scatter(
+                product(unrotated, their_unrotated), "chip", scatter_dimension=1, tiled=True
+            )
+        )
     squares = lax.psum(jnp.sum(gradient * gradient), ("chip", "core"))
     factor = 1.0 / jnp.sqrt(squares + norm_epsilon)
     inner = adam_update(gradient * factor, island_weights[0], first_moment[0], second_moment[0])

time: 234 us -> 236 us (level)
  matrix products: 8.3 us -> 13.9 us
  local copies, waits for them, and re-layouts: 15 us -> 11.9 us
    ppermute x1, waiting for transfers between devices: 12.8 us -> 19.2 us  [chip_scatter(): return ((keep + lax.ppermute(send, lanes, cross_second))[:, None], tie)]
    dot_general x2 -> x4, matrix products: 7.93 us -> 13.5 us  [the longest x2 8.73 us: product(): lax.dot_general(their_lhs, theirs, contract, preferred_element_type=jnp.f...]
    select_n x1, other arithmetic: 5.96 us -> 1.79 us  [chip_scatter(): send = jnp.where(first == 0, upper, lower)]
    slice x1 -> x0, local copies, waits for them, and re-layouts: 4.07 us -> none  [body(): partial[:split]]
    ppermute x1, waiting for transfers between devices: 50.1 us -> 46.7 us  [chip_scatter(): held = keep + lax.ppermute(send, lanes, cross_first)]
  transfers between devices with their start and end apart: 9 -> 9, of which waited for: 3 -> 3; matrix products, arithmetic and copies ran while one was open for 8% -> 6% of each run, Pallas kernels for 0% -> 0%
where the time goes in v13:
time: 236 us; the launch traced here: 235 us
  waiting for transfers between devices  108 us (46%)
  blocking collectives  56.6 us (24%)
  other arithmetic  23.9 us (10%)
  between operations  14.9 us (6%)
  matrix products  13.9 us (6%)
  local copies, waits for them, and re-layouts  11.9 us (5%)
  starting transfers between devices  6.23 us (3%)
    ppermute x1, waiting for transfers between devices, chip_scatter(): held = keep + lax.ppermute(send, lanes, cross_first)  46.7 us
    psum x1, blocking collectives, body(): lax.psum(local_tiles(island_drift, tile_rows, first_row), ('island', 'chi...  43 us
    psum x1, waiting for transfers between devices, body(): drift = lax.psum(island_drift, 'island') / replicas  42 us
    ppermute x1, waiting for transfers between devices, chip_scatter(): return ((keep + lax.ppermute(send, lanes, cross_second))[:, None], tie)  19.2 us
    psum x1, blocking collectives, body(): squares = lax.psum(jnp.sum(gradient * gradient), ('chip', 'core'))  13.6 us
    dot_general x2, matrix products, product(): lax.dot_general(their_lhs, theirs, contract, preferred_element_type=jnp.f...  8.73 us
    reduce_sum x1, other arithmetic, local_tiles(): jnp.sum(drift_rows, axis=1)  6.65 us
    dynamic_slice x1, local copies, waits for them, and re-layouts, parity(): lax.dynamic_slice_in_dim(tokens, (2 * k + side) * own_rows, own_rows, axi...  6.34 us
  transfers between devices with their start and end apart: 9, of which 3 were waited for; matrix products, arithmetic and copies ran while one was open for 6% of the time, Pallas kernels for 0%

profile of v13, /device:TPU:0, one launch (start us, length us, event | category | flops | bytes accessed | tf_op | source)
XLA Modules:
  0.0 235.4 jit_solution(13306522931450983068)
XLA Ops:
  7.2 0.0 reduce-scatter.4.cloned.1.call-start
  7.2 6.3 %dynamic-slice_bitcast_fusion.3 = (bf16[512,1024]{1,0:T(8,128)(2,1)}, bf16[512,1024]{1,0:T(8,128)(2,1)}, bf16[512,1,1024]{2,0,1:T(8,128)(2,1)S(1)}, bf16[512,1,1...) fusion(bf16[1,512,8192]{2,1,0:T(8,128)(2,1)} %param.8, ...), kind=kLoop, calls=%fused_computation.33 | loop fusion | bytes 16777248 | tf_op jit(solution)/shard_map/dynamic_slice | solution.py:100
  13.6 0.5 collective-permute-start.4
  14.0 0.1 collective-permute-start.3
  14.1 0.5 collective-permute-start.2
  14.5 0.1 collective-permute-start.1
  14.6 0.5 multiply_cosine_fusion
  15.1 2.2 copy.33
  17.4 1.4 add_convert_fusion
  18.8 0.8 pad_maximum_fusion.7
  19.6 0.5 collective-permute-start
  20.0 2.6 %fusion.11 = f32[256,4,1024]{2,0,1:T(8,128)S(1)} fusion(bf16[512,1,1024]{2,0,1:T(8,128)(2,1)S(1)} %get-tuple-element.15, bf16[512,1,1024]{2,0,1:T(8,128)(2,1)S(1)} %get-tuple-element.16, bf16[512,1,1024]{2,0,1:T(8,128)(2,1)S(1)} %get-tuple-element.17, bf16[512,1,1024]{2,0,1:T(8,128)(2,1)} %get-tuple-element.18, bf16[512,512]{0,1:T(8,128)(2,1)} %bitcast.2), kind=kOutput, calls=%fused_computation.40 | convolution fusion | flops 1090519040 | bytes 8650752 | tf_op jit(solution)/shard_map/dot_general | solution.py:111
  22.6 0.0 collective-permute-done
  22.6 0.0 collective-permute-done.4
  22.6 0.0 collective-permute-done.3
  22.6 0.0 collective-permute-done.2
  22.6 0.0 collective-permute-done.1
  22.6 3.2 %convolution_add_fusion.1 = f32[256,4,1024]{2,0,1:T(8,128)S(1)} fusion(f32[256,4,1024]{2,0,1:T(8,128)S(1)} %fusion.11, bf16[512,1,1024]{2,0,1:T(8,128)(2,1)} %bitcast.16, bf16[512,1,1024]{2,0,1:T(8,128)(2,1)} %bitcast.14, bf16[512,1,1024]{2,0,1:T(8,128)(2,1)} %bitcast.12, bf16[512,1,1024]{2,0,1:T(8,128)(2,1)} %bitcast.10, ...), kind=kOutput, calls=%fused_computation.4 | convolution fusion | flops 1091567616 | bytes 12845056 | tf_op jit(solution)/shard_map/dot_general | solution.py:113
  25.9 0.0 copy-start
  25.9 0.0 copy-start.1
  25.9 1.8 broadcast_select_fusion
  27.7 0.7 copy-done
  28.4 0.0 copy-done.1
  28.4 2.2 fusion.10
  30.7 5.5 %convolution_add_fusion = f32[256,4,1024]{2,0,1:T(8,128)} fusion(f32[256,4,1024]{2,0,1:T(8,128)S(1)} %fusion.10, bf16[512,1,1024]{2,0,1:T(8,128)(2,1)} %bitcast.16, bf16[512,1,1024]{2,0,1:T(8,128)(2,1)} %bitcast.14, bf16[512,1,1024]{2,0,1:T(8,128)(2,1)} %bitcast.12, bf16[512,1,1024]{2,0,1:T(8,128)(2,1)} %bitcast.10, bf16[512,512]{0,1:T(8,128)(2,1)} %collective-permute-done), kind=kOutput, calls=%fused_computation.3 | convolution fusion | flops 1091567616 | bytes 12845056 | tf_op jit(solution)/shard_map/dot_general | solution.py:113
  36.2 0.0 reduce-scatter.4.cloned.1.call-update
  36.2 0.0 all-reduce.3.cloned.1.call-start
  36.2 2.6 %collective-permute-start.5 = (f32[256,2,1024]{2,0,1:T(8,128)}, f32[256,2,1024]{2,0,1:T(8,128)S(1)}, u32[]{:S(2)}, u32[]{:S(2)}) collective-permute-start(f32[256,2,1024]{2,0,1:T(8,128)} %broadcast_select_fusion), channel_id=1, source_target_pairs={{0,2},{1,5},{2,0},{3,7},{4,6},{5,1},{6,4},{7,3},{8,10},{9,13},{10,... | collective-permute-start | bytes 6291464 | tf_op jit(solution)/shard_map/ppermute | solution.py:73
  38.8 46.7 %collective-permute-done.5 = f32[256,2,1024]{2,0,1:T(8,128)S(1)} collective-permute-done((f32[256,2,1024]{2,0,1:T(8,128)}, f32[256,2,1024]{2,0,1:T(8,128)S(1)}, u32[]{:S(2)}, u32[]{:S(2)}) %collective-permute-start.5) | collective-permute-done | bytes 2097184 | tf_op jit(solution)/shard_map/ppermute | solution.py:73
  85.5 5.4 %select_add_fusion = f32[256,2,1024]{2,0,1:T(8,128)S(1)} fusion(f32[256,2,1024]{2,0,1:T(8,128)S(1)} %collective-permute-done.5, pred[]{:T(512)S(6)} %eq.11, f32[256,2,2,1024]{3,0,2,1:T(8,128)} %bitcast.107, pred[]{:T(512)S(6)} %eq.10), kind=kLoop, calls=%fused_computation.26 | loop fusion | flops 2097152 | bytes 12582914 | tf_op jit(solution)/shard_map/add | solution.py:73
  90.9 0.1 select_bitcast_fusion
  91.0 2.1 collective-permute-start.6
  93.2 19.2 %collective-permute-done.6 = f32[256,1024]{1,0:T(8,128)S(1)} collective-permute-done((f32[256,1024]{1,0:T(8,128)S(1)}, f32[256,1024]{1,0:T(8,128)S(1)}, u32[]{:S(2)}, u32[]{:S(2)}) %collective-permute-start.6) | collective-permute-done | bytes 1048608 | tf_op jit(solution)/shard_map/ppermute | solution.py:76
  112.4 0.3 bitcast_add_fusion.1
  112.7 0.3 copy.32
  113.1 0.0 reduce-scatter.4.cloned.1.call-done
  113.1 1.6 copy.28
  114.7 1.1 multiply_reduce_fusion
  115.8 13.6 %psum.21 = f32[]{:T(128)} all-reduce(f32[]{:T(128)} %multiply_reduce_fusion), channel_id=1, replica_groups=mesh['island'=4,'chip'=4,'core'=2] {'chip','core'}, use_global_device_ids=true, to_apply=%region_2.3 | all-reduce | flops 1 | bytes 8 | tf_op jit(solution)/shard_map/psum | solution.py:136
  130.1 6.6 %fusion.26 = (f32[1024]{0:T(1024)S(1)}, f32[1024,512]{1,0:T(8,128)}) fusion(f32[1024,512]{1,0:T(8,128)} %param.10, f32[1,1024,512]{2,1,0:T(8,128)} %param.14, f32[]{:T(128)S(6)} %sqrt.9, f32[1024,256]{1,0:T(8,128)S(1)} %bitcast.109, f32[1024,256]{1,0:T(8,128)S(1)} %bitcast.111, f32[1,1024,512]{2,1,0:T(8,128)} %param.13, f32[1,1024,512]{2,1,0:T(8,128)} %param.12), kind=kLoop, calls=%fused_computation.69 | loop fusion | flops 9960448 | bytes 12587012 | tf_op jit(solution)/shard_map/reduce_sum | solution.py:53
  136.7 0.0 copy-start.3
  136.7 0.0 copy-start.2
  136.7 0.0 all-reduce.3.cloned.1.call-update
  136.7 0.6 copy-done.3
  137.4 0.1 copy.30
  137.5 0.1 reduce-window.8
  137.5 0.1 reduce
  137.7 0.4 convolution_bitcast_fusion
  138.0 43.0 %psum.23 = f32[48]{0:T(128)S(1)} all-reduce(f32[48]{0:T(128)S(1)} %convolution_bitcast_fusion), channel_id=1, replica_groups=mesh['island'=4,'chip'=4,'core'=2] {'island','chip','core'}, use_global_device_ids=true, to_apply=%region_6.7 | all-reduce | flops 48 | bytes 384 | tf_op jit(solution)/shard_map/psum | solution.py:146
  181.0 0.5 rsqrt_multiply_fusion
  181.6 42.0 %all-reduce.3.cloned.1.call-done = f32[1024,512]{1,0:T(8,128)} async-done(((f32[1024,512]{1,0:T(8,128)}), f32[1024,512]{1,0:T(8,128)}) %all-reduce.3.cloned.1.call-update) | async-done | bytes 2097168 | tf_op jit(solution)/shard_map/psum | solution.py:141
  223.6 0.0 copy-done.2
  223.6 5.0 %multiply_subtract_fusion = (f32[1024,512]{1,0:T(8,128)}, f32[1024,512]{1,0:T(8,128)}) fusion(f32[1024,512]{1,0:T(8,128)S(1)} %copy-done.2, f32[1024,512]{1,0:T(8,128)} %all-reduce.3.cloned.1.call-done, f32[1024,512]{1,0:T(8,128)} %param.11), kind=kLoop, calls=%fused_computation.23 | loop fusion | flops 3670016 | bytes 10485760 | tf_op jit(solution)/shard_map/sub | solution.py:143
  (4 shorter events, 0.0 us)
Async XLA Ops:
  7.2 105.9 %reduce-scatter.4.cloned.1.call-start = ((), (), s32[]{:S(2)}) async-start(), calls=%async_computation.2 | async-start | bytes 5242880
  13.6 9.0 %collective-permute-start.4 = (bf16[512,1024]{1,0:T(8,128)(2,1)}, bf16[512,1024]{1,0:T(8,128)(2,1)}, u32[]{:S(2)}, u32[]{:S(2)}) collective-permute-start(bf16[512,1024]{1,0:T(8,128)(2,1)} %get-tuple-element.19), channel_id=1, source_target_pairs={{0,1},{1,0},{2,3},{3,2},{4,5},{5,4},{6,7},{7,6},{8,9},{9,8},{10,11... | collective-permute-start | bytes 3145736 | tf_op jit(solution)/shard_map/ppermute | solution.py:104
  14.0 8.6 %collective-permute-start.3 = (bf16[512,1024]{1,0:T(8,128)(2,1)}, bf16[512,1024]{1,0:T(8,128)(2,1)}, u32[]{:S(2)}, u32[]{:S(2)}) collective-permute-start(bf16[512,1024]{1,0:T(8,128)(2,1)} %get-tuple-element.20), channel_id=1, source_target_pairs={{0,1},{1,0},{2,3},{3,2},{4,5},{5,4},{6,7},{7,6},{8,9},{9,8},{10,11... | collective-permute-start | bytes 3145736 | tf_op jit(solution)/shard_map/ppermute | solution.py:104
  14.1 8.5 %collective-permute-start.2 = (bf16[512,1024]{1,0:T(8,128)(2,1)}, bf16[512,1024]{1,0:T(8,128)(2,1)}, u32[]{:S(2)}, u32[]{:S(2)}) collective-permute-start(bf16[512,1024]{1,0:T(8,128)(2,1)} %get-tuple-element.14), channel_id=1, source_target_pairs={{0,1},{1,0},{2,3},{3,2},{4,5},{5,4},{6,7},{7,6},{8,9},{9,8},{10,11... | collective-permute-start | bytes 3145736 | tf_op jit(solution)/shard_map/ppermute | solution.py:104
  14.5 8.1 %collective-permute-start.1 = (bf16[512,1024]{1,0:T(8,128)(2,1)}, bf16[512,1024]{1,0:T(8,128)(2,1)}, u32[]{:S(2)}, u32[]{:S(2)}) collective-permute-start(bf16[512,1024]{1,0:T(8,128)(2,1)} %get-tuple-element.13), channel_id=1, source_target_pairs={{0,1},{1,0},{2,3},{3,2},{4,5},{5,4},{6,7},{7,6},{8,9},{9,8},{10,11... | collective-permute-start | bytes 3145736 | tf_op jit(solution)/shard_map/ppermute | solution.py:104
  19.6 3.0 %collective-permute-start = (bf16[512,512]{0,1:T(8,128)(2,1)}, bf16[512,512]{0,1:T(8,128)(2,1)}, u32[]{:S(2)}, u32[]{:S(2)}) collective-permute-start(bf16[512,512]{0,1:T(8,128)(2,1)} %bitcast.2), channel_id=1, source_target_pairs={{0,1},{1,0},{2,3},{3,2},{4,5},{5,4},{6,7},{7,6},{8,9},{9,8},{10,11... | collective-permute-start | bytes 1572872 | tf_op jit(solution)/shard_map/ppermute | solution.py:105
  25.9 2.6 %copy-start = (f32[256,4,1024]{2,0,1:T(8,128)}, f32[256,4,1024]{2,0,1:T(8,128)S(1)}, u32[]{:S(2)}) copy-start(f32[256,4,1024]{2,0,1:T(8,128)S(1)} %convolution_add_fusion.1) | copy-start | bytes 12582916
  25.9 2.5 %copy-start.1 = (bf16[512,1,1024]{2,0,1:T(8,128)(2,1)S(1)}, bf16[512,1,1024]{2,0,1:T(8,128)(2,1)}, u32[]{:S(2)}) copy-start(bf16[512,1,1024]{2,0,1:T(8,128)(2,1)} %get-tuple-element.18) | copy-start | bytes 3145732
  36.2 187.4 %all-reduce.3.cloned.1.call-start = ((), (), s32[]{:S(2)}) async-start(), calls=%async_computation.1 | async-start | bytes 4194304 | tf_op jit(solution)/shard_map/psum | solution.py:141
  36.2 49.3 %collective-permute-start.5 = (f32[256,2,1024]{2,0,1:T(8,128)}, f32[256,2,1024]{2,0,1:T(8,128)S(1)}, u32[]{:S(2)}, u32[]{:S(2)}) collective-permute-start(f32[256,2,1024]{2,0,1:T(8,128)} %broadcast_select_fusion), channel_id=1, source_target_pairs={{0,2},{1,5},{2,0},{3,7},{4,6},{5,1},{6,4},{7,3},{8,10},{9,13},{10,... | collective-permute-start | bytes 6291464 | tf_op jit(solution)/shard_map/ppermute | solution.py:73
  91.0 21.4 %collective-permute-start.6 = (f32[256,1024]{1,0:T(8,128)S(1)}, f32[256,1024]{1,0:T(8,128)S(1)}, u32[]{:S(2)}, u32[]{:S(2)}) collective-permute-start(f32[256,1024]{1,0:T(8,128)S(1)} %select_bitcast_fusion), channel_id=1, source_target_pairs={{0,4},{1,3},{2,6},{3,1},{4,0},{5,7},{6,2},{7,5},{8,12},{9,11},{10,... | collective-permute-start | bytes 3145736 | tf_op jit(solution)/shard_map/ppermute | solution.py:76
  136.7 0.7 copy-start.3
  136.7 86.8 %copy-start.2 = (f32[1024,512]{1,0:T(8,128)S(1)}, f32[1024,512]{1,0:T(8,128)}, u32[]{:S(2)}) copy-start(f32[1024,512]{1,0:T(8,128)} %param.10) | copy-start | bytes 6291460
Sparse Core Ops, SparseCore 0:
  36.3 70.1 reduce-scatter.3
  136.9 86.6 all-reduce.2

commit v14 on v10

--- a/solution.py
+++ b/solution.py
@@ -114,7 +114,7 @@
         return with_layout_constraint(block.reshape(block.shape[0], own_rows).T, Layout((0, 1)))
 
     if chips == 4:
-        split = partial.shape[0] // 2
+        split = partial.shape[0] * 5 // 8
         gradient = jnp.concatenate(
             [
                 rows_major(

time: 234 us -> 240 us (1.026)
  waiting for transfers between devices: 106 us -> 114 us
  other arithmetic: 25.4 us -> 18.2 us
  local copies, waits for them, and re-layouts: 15 us -> 19.6 us
    ppermute x1, waiting for transfers between devices: 12.8 us -> 22.6 us  [chip_scatter(): return (keep + lax.ppermute(send, lanes, cross_second))[:, None]]
    select_n x1, other arithmetic: 5.96 us -> 1.43 us  [chip_scatter(): send = jnp.where(first == 0, upper, lower)]
    ppermute x1, waiting for transfers between devices: 50.1 us -> 46.3 us  [chip_scatter(): held = keep + lax.ppermute(send, lanes, cross_first)]
    unnamed x8 -> x10, local copies, waits for them, and re-layouts: 1.42 us -> 4.63 us
    add x1, other arithmetic: 4.73 us -> 1.91 us  [chip_scatter(): held = keep + lax.ppermute(send, lanes, cross_first)]
    unnamed x3, waiting for transfers between devices: 0.05 us -> 2.5 us
  transfers between devices with their start and end apart: 9 -> 9, of which waited for: 3 -> 4; matrix products, arithmetic and copies ran while one was open for 8% -> 5% of each run, Pallas kernels for 0% -> 0%
where the time goes in v14:
time: 240 us
  waiting for transfers between devices  114 us (48%)
  blocking collectives  58.2 us (24%)
  local copies, waits for them, and re-layouts  19.6 us (8%)
  other arithmetic  18.2 us (8%)
  between operations  14.9 us (6%)
  matrix products  8.3 us (3%)
  starting transfers between devices  7.18 us (3%)
    ppermute x1, waiting for transfers between devices, chip_scatter(): held = keep + lax.ppermute(send, lanes, cross_first)  46.3 us
    psum x1, blocking collectives, body(): lax.psum(local_tiles(island_drift, tile_rows, first_row), ('island', 'chi...  43.2 us
    psum x1, waiting for transfers between devices, body(): drift = lax.psum(island_drift, 'island') / replicas  42 us
    ppermute x1, waiting for transfers between devices, chip_scatter(): return (keep + lax.ppermute(send, lanes, cross_second))[:, None]  22.6 us
    psum x1, blocking collectives, body(): squares = lax.psum(jnp.sum(gradient * gradient), ('chip', 'core'))  15 us
    reduce_sum x1, other arithmetic, local_tiles(): jnp.sum(drift_rows, axis=1)  6.88 us
    dynamic_slice x1, local copies, waits for them, and re-layouts, parity(): lax.dynamic_slice_in_dim(tokens, (2 * k + side) * own_rows, own_rows, axi...  6.32 us
    sub x1, other arithmetic, body(): master_out = master - outer_rate * (drift + outer_moment * momentum_out)  5.02 us
  transfers between devices with their start and end apart: 9, of which 4 were waited for; matrix products, arithmetic and copies ran while one was open for 5% of the time, Pallas kernels for 0%

profile of v14, /device:TPU:0, one launch (start us, length us, event | category | flops | bytes accessed | tf_op | source)
XLA Modules:
  0.0 239.9 jit_solution(13265137180033342561)
XLA Ops:
  7.2 0.0 reduce-scatter.4.cloned.1.call-start
  7.2 6.3 %dynamic-slice_bitcast_fusion.3 = (bf16[512,1024]{1,0:T(8,128)(2,1)}, bf16[512,1024]{1,0:T(8,128)(2,1)}, bf16[512,1,1024]{2,0,1:T(8,128)(2,1)}, bf16[512,1,1024]...) fusion(bf16[1,512,8192]{2,1,0:T(8,128)(2,1)} %param.8, ...), kind=kLoop, calls=%fused_computation.44 | loop fusion | bytes 16777248 | tf_op jit(solution)/shard_map/dynamic_slice | solution.py:99
  13.5 0.5 collective-permute-start.1
  14.0 0.1 collective-permute-start.2
  14.1 0.5 collective-permute-start.3
  14.5 0.1 collective-permute-start.4
  14.6 0.5 multiply_cosine_fusion
  15.1 1.3 copy.35
  16.4 0.0 copy-start.2
  16.4 0.0 copy-start.3
  16.4 0.2 add_convert_fusion
  16.6 0.5 collective-permute-start
  17.2 0.5 copy-done.2
  17.6 0.3 copy-done.3
  17.9 3.7 %fusion = f32[512,4,1024]{2,0,1:T(8,128)S(1)} fusion(bf16[512,512,1]{0,1,2:T(8,128)(2,1)S(1)} %bitcast.108, bf16[512,1,1024]{2,0,1:T(8,128)(2,1)S(1)} %copy-done.2, bf16[512,1,1024]{2,0,1:T(8,128)(2,1)S(1)} %copy-done.3, bf16[512,1,1024]{2,0,1:T(8,128)(2,1)} %get-tuple-element.11, bf16[512,1,1024]{2,0,1:T(8,128)(2,1)} %get-tuple-element.12), kind=kOutput, calls=%fused_computation | convolution fusion | flops 2164260864 | bytes 13107200 | tf_op jit(solution)/shard_map/dot_general | solution.py:106
  21.7 0.0 collective-permute-done
  21.7 0.0 collective-permute-done.1
  21.7 0.0 collective-permute-done.2
  21.7 0.0 collective-permute-done.3
  21.7 0.0 collective-permute-done.4
  21.7 4.2 %fusion.16 = f32[512,4,1024]{2,0,1:T(8,128)S(1)} fusion(f32[512,4,1024]{2,0,1:T(8,128)S(1)} %fusion, bf16[512,1,1024]{2,0,1:T(8,128)(2,1)} %bitcast.16, bf16[512,1,1024]{2,0,1:T(8,128)(2,1)} %bitcast.14, bf16[512,1,1024]{2,0,1:T(8,128)(2,1)} %bitcast.12, bf16[512,1,1024]{2,0,1:T(8,128)(2,1)} %bitcast.10, bf16[512,512]{0,1:T(8,128)(2,1)S(1)} %collective-permute-done), kind=kOutput, calls=%fused_computation.17 | convolution fusion | flops 2166358016 | bytes 21495808 | tf_op jit(solution)/shard_map/dot_general | solution.py:108
  25.9 0.0 copy-start
  25.9 3.2 %copy-done = f32[512,4,1024]{2,0,1:T(8,128)} copy-done((f32[512,4,1024]{2,0,1:T(8,128)}, f32[512,4,1024]{2,0,1:T(8,128)S(1)}, u32[]{:S(2)}) %copy-start) | copy-done | bytes 8388632
  29.2 3.0 %slice.44 = f32[320,4,1024]{2,0,1:T(8,128)} slice(f32[512,4,1024]{2,0,1:T(8,128)S(1)} %fusion.16), slice={[0:320], [0:4], [0:1024]} | slice | bytes 10485760 | tf_op jit(solution)/shard_map/slice | solution.py:121
  32.2 0.0 reduce-scatter.4.cloned.1.call-update
  32.2 0.0 all-reduce.3.cloned.1.call-start
  32.3 2.1 slice.45
  34.4 1.4 broadcast_select_fusion
  35.8 2.9 %collective-permute-start.5 = (f32[192,2,1024]{2,0,1:T(8,128)}, f32[192,2,1024]{2,0,1:T(8,128)}, u32[]{:S(2)}, u32[]{:S(2)}) collective-permute-start(f32[192,2,1024]{2,0,1:T(8,128)} %broadcast_select_fusion), channel_id=1, source_target_pairs={{0,2},{1,5},{2,0},{3,7},{4,6},{5,1},{6,4},{7,3},{8,10},{9,13},{10,... | collective-permute-start | bytes 4718600 | tf_op jit(solution)/shard_map/ppermute | solution.py:72
  38.8 46.3 %collective-permute-done.5 = f32[192,2,1024]{2,0,1:T(8,128)} collective-permute-done((f32[192,2,1024]{2,0,1:T(8,128)}, f32[192,2,1024]{2,0,1:T(8,128)}, u32[]{:S(2)}, u32[]{:S(2)}) %collective-permute-start.5) | collective-permute-done | bytes 1572896 | tf_op jit(solution)/shard_map/ppermute | solution.py:72
  85.1 1.9 select_add_fusion
  87.0 0.1 select_bitcast_fusion
  87.1 2.6 %collective-permute-start.6 = (f32[192,1024]{1,0:T(8,128)S(1)}, f32[192,1024]{1,0:T(8,128)S(1)}, u32[]{:S(2)}, u32[]{:S(2)}) collective-permute-start(f32[192,1024]{1,0:T(8,128)S(1)} %select_bitcast_fusion), channel_id=1, source_target_pairs={{0,4},{1,3},{2,6},{3,1},{4,0},{5,7},{6,2},{7,5},{8,12},{9,11},{10,... | collective-permute-start | bytes 2359304 | tf_op jit(solution)/shard_map/ppermute | solution.py:75
  89.8 22.6 %collective-permute-done.6 = f32[192,1024]{1,0:T(8,128)S(1)} collective-permute-done((f32[192,1024]{1,0:T(8,128)S(1)}, f32[192,1024]{1,0:T(8,128)S(1)}, u32[]{:S(2)}, u32[]{:S(2)}) %collective-permute-start.6) | collective-permute-done | bytes 786464 | tf_op jit(solution)/shard_map/ppermute | solution.py:75
  112.4 0.2 bitcast_add_fusion.1
  112.6 0.3 copy.34
  112.9 2.5 %reduce-scatter.4.cloned.1.call-done = f32[320,1,1024]{2,0,1:T(8,128)} async-done(((f32[320,4,1024]{2,0,1:T(8,128)}), f32[320,1,1024]{2,0,1:T(8,128)}) %reduce-scatter.4.cloned.1.call-update) | async-done | bytes 1310736
  115.4 1.8 copy.30
  117.2 1.2 multiply_reduce_fusion
  118.3 15.0 %psum.21 = f32[]{:T(128)} all-reduce(f32[]{:T(128)} %multiply_reduce_fusion), channel_id=1, replica_groups=mesh['island'=4,'chip'=4,'core'=2] {'chip','core'}, use_global_device_ids=true, to_apply=%region_2.3 | all-reduce | flops 1 | bytes 8 | tf_op jit(solution)/shard_map/psum | solution.py:129
  134.0 6.9 %fusion.38 = (f32[1024]{0:T(1024)S(1)}, f32[1024,512]{1,0:T(8,128)}) fusion(f32[1024,512]{1,0:T(8,128)} %param.10, f32[1,1024,512]{2,1,0:T(8,128)} %param.14, f32[]{:T(128)S(6)} %sqrt.9, f32[1024,192]{1,0:T(8,128)S(1)} %bitcast.105, f32[1024,320]{1,0:T(8,128)S(1)} %bitcast.103, f32[1,1024,512]{2,1,0:T(8,128)} %param.13, f32[1,1024,512]{2,1,0:T(8,128)} %param.12), kind=kLoop, calls=%fused_computation.73 | loop fusion | flops 9960448 | bytes 12587012 | tf_op jit(solution)/shard_map/reduce_sum | solution.py:53
  140.9 0.0 copy-start.4
  140.9 0.0 copy-start.1
  140.9 0.0 all-reduce.3.cloned.1.call-update
  140.9 0.6 copy-done.4
  141.6 0.1 copy.32
  141.6 0.1 reduce-window.8
  141.7 0.1 reduce
  141.9 0.4 convolution_bitcast_fusion
  142.2 43.2 %psum.23 = f32[48]{0:T(128)S(1)} all-reduce(f32[48]{0:T(128)S(1)} %convolution_bitcast_fusion), channel_id=1, replica_groups=mesh['island'=4,'chip'=4,'core'=2] {'island','chip','core'}, use_global_device_ids=true, to_apply=%region_6.7 | all-reduce | flops 48 | bytes 384 | tf_op jit(solution)/shard_map/psum | solution.py:139
  185.5 0.5 rsqrt_multiply_fusion
  186.0 42.0 %all-reduce.3.cloned.1.call-done = f32[1024,512]{1,0:T(8,128)} async-done(((f32[1024,512]{1,0:T(8,128)}), f32[1024,512]{1,0:T(8,128)}) %all-reduce.3.cloned.1.call-update) | async-done | bytes 2097168 | tf_op jit(solution)/shard_map/psum | solution.py:134
  228.0 0.0 copy-done.1
  228.0 5.0 %multiply_subtract_fusion = (f32[1024,512]{1,0:T(8,128)}, f32[1024,512]{1,0:T(8,128)}) fusion(f32[1024,512]{1,0:T(8,128)S(1)} %copy-done.1, f32[1024,512]{1,0:T(8,128)} %all-reduce.3.cloned.1.call-done, f32[1024,512]{1,0:T(8,128)} %param.11), kind=kLoop, calls=%fused_computation.30 | loop fusion | flops 3670016 | bytes 10485760 | tf_op jit(solution)/shard_map/sub | solution.py:136
  (5 shorter events, 0.1 us)
Async XLA Ops:
  7.2 108.2 %reduce-scatter.4.cloned.1.call-start = ((), (), s32[]{:S(2)}) async-start(), calls=%async_computation.2 | async-start | bytes 6553600
  13.5 8.1 %collective-permute-start.1 = (bf16[512,1024]{1,0:T(8,128)(2,1)}, bf16[512,1024]{1,0:T(8,128)(2,1)}, u32[]{:S(2)}, u32[]{:S(2)}) collective-permute-start(bf16[512,1024]{1,0:T(8,128)(2,1)} %get-tuple-element.7), channel_id=1, source_target_pairs={{0,1},{1,0},{2,3},{3,2},{4,5},{5,4},{6,7},{7,6},{8,9},{9,8},{10,11... | collective-permute-start | bytes 3145736 | tf_op jit(solution)/shard_map/ppermute | solution.py:103
  14.0 7.7 %collective-permute-start.2 = (bf16[512,1024]{1,0:T(8,128)(2,1)}, bf16[512,1024]{1,0:T(8,128)(2,1)}, u32[]{:S(2)}, u32[]{:S(2)}) collective-permute-start(bf16[512,1024]{1,0:T(8,128)(2,1)} %get-tuple-element.8), channel_id=1, source_target_pairs={{0,1},{1,0},{2,3},{3,2},{4,5},{5,4},{6,7},{7,6},{8,9},{9,8},{10,11... | collective-permute-start | bytes 3145736 | tf_op jit(solution)/shard_map/ppermute | solution.py:103
  14.1 7.7 %collective-permute-start.3 = (bf16[512,1024]{1,0:T(8,128)(2,1)S(1)}, bf16[512,1024]{1,0:T(8,128)(2,1)}, u32[]{:S(2)}, u32[]{:S(2)}) collective-permute-start(bf16[512,1024]{1,0:T(8,128)(2,1)S(1)} %get-tuple-element.14), channel_id=1, source_target_pairs={{0,1},{1,0},{2,3},{3,2},{4,5},{5,4},{6,7},{7,6},{8,9},{9,8},{10,11... | collective-permute-start | bytes 3145736 | tf_op jit(solution)/shard_map/ppermute | solution.py:103
  14.5 7.2 %collective-permute-start.4 = (bf16[512,1024]{1,0:T(8,128)(2,1)S(1)}, bf16[512,1024]{1,0:T(8,128)(2,1)}, u32[]{:S(2)}, u32[]{:S(2)}) collective-permute-start(bf16[512,1024]{1,0:T(8,128)(2,1)S(1)} %get-tuple-element.13), channel_id=1, source_target_pairs={{0,1},{1,0},{2,3},{3,2},{4,5},{5,4},{6,7},{7,6},{8,9},{9,8},{10,11... | collective-permute-start | bytes 3145736 | tf_op jit(solution)/shard_map/ppermute | solution.py:103
  16.4 1.2 copy-start.2
  16.4 1.5 copy-start.3
  16.6 5.0 %collective-permute-start = (bf16[512,512]{0,1:T(8,128)(2,1)S(1)}, bf16[512,512]{0,1:T(8,128)(2,1)S(1)}, u32[]{:S(2)}, u32[]{:S(2)}) collective-permute-start(bf16[512,512]{0,1:T(8,128)(2,1)S(1)} %bitcast.107), channel_id=1, source_target_pairs={{0,1},{1,0},{2,3},{3,2},{4,5},{5,4},{6,7},{7,6},{8,9},{9,8},{10,11... | collective-permute-start | bytes 1572872 | tf_op jit(solution)/shard_map/ppermute | solution.py:104
  25.9 3.2 %copy-start = (f32[512,4,1024]{2,0,1:T(8,128)}, f32[512,4,1024]{2,0,1:T(8,128)S(1)}, u32[]{:S(2)}) copy-start(f32[512,4,1024]{2,0,1:T(8,128)S(1)} %fusion.16) | copy-start | bytes 25165828
  32.2 195.8 %all-reduce.3.cloned.1.call-start = ((), (), s32[]{:S(2)}) async-start(), calls=%async_computation.1 | async-start | bytes 4194304 | tf_op jit(solution)/shard_map/psum | solution.py:134
  35.8 49.3 %collective-permute-start.5 = (f32[192,2,1024]{2,0,1:T(8,128)}, f32[192,2,1024]{2,0,1:T(8,128)}, u32[]{:S(2)}, u32[]{:S(2)}) collective-permute-start(f32[192,2,1024]{2,0,1:T(8,128)} %broadcast_select_fusion), channel_id=1, source_target_pairs={{0,2},{1,5},{2,0},{3,7},{4,6},{5,1},{6,4},{7,3},{8,10},{9,13},{10,... | collective-permute-start | bytes 4718600 | tf_op jit(solution)/shard_map/ppermute | solution.py:72
  87.1 25.3 %collective-permute-start.6 = (f32[192,1024]{1,0:T(8,128)S(1)}, f32[192,1024]{1,0:T(8,128)S(1)}, u32[]{:S(2)}, u32[]{:S(2)}) collective-permute-start(f32[192,1024]{1,0:T(8,128)S(1)} %select_bitcast_fusion), channel_id=1, source_target_pairs={{0,4},{1,3},{2,6},{3,1},{4,0},{5,7},{6,2},{7,5},{8,12},{9,11},{10,... | collective-permute-start | bytes 2359304 | tf_op jit(solution)/shard_map/ppermute | solution.py:75
  140.9 0.7 copy-start.4
  140.9 87.1 %copy-start.1 = (f32[1024,512]{1,0:T(8,128)S(1)}, f32[1024,512]{1,0:T(8,128)}, u32[]{:S(2)}) copy-start(f32[1024,512]{1,0:T(8,128)} %param.10) | copy-start | bytes 6291460
Sparse Core Ops, SparseCore 0:
  32.3 83.0 reduce-scatter.3
  141.0 86.9 all-reduce.2

commit v15 on v14

--- a/solution.py
+++ b/solution.py
@@ -114,7 +114,7 @@
         return with_layout_constraint(block.reshape(block.shape[0], own_rows).T, Layout((0, 1)))
 
     if chips == 4:
-        split = partial.shape[0] * 5 // 8
+        split = partial.shape[0] * 3 // 8
         gradient = jnp.concatenate(
             [
                 rows_major(

time: 240 us -> 243 us (1.012)
  other arithmetic: 18.2 us -> 23.2 us
  blocking collectives: 58.2 us -> 55.5 us
    ppermute x1, waiting for transfers between devices: 46.3 us -> 55.1 us  [chip_scatter(): held = keep + lax.ppermute(send, lanes, cross_first)]
    ppermute x1, waiting for transfers between devices: 22.6 us -> 15.8 us  [chip_scatter(): return (keep + lax.ppermute(send, lanes, cross_second))[:, None]]
    add x1, other arithmetic: 1.91 us -> 5.63 us  [chip_scatter(): held = keep + lax.ppermute(send, lanes, cross_first)]
    unnamed x3, waiting for transfers between devices: 2.5 us -> 0.05 us
    unnamed x10 -> x12, local copies, waits for them, and re-layouts: 4.63 us -> 5.31 us
  transfers between devices with their start and end apart: 9 -> 9, of which waited for: 4 -> 3; matrix products, arithmetic and copies ran while one was open for 5% -> 8% of each run, Pallas kernels for 0% -> 0%
where the time goes in v15:
time: 243 us
  waiting for transfers between devices  114 us (47%)
  blocking collectives  55.5 us (23%)
  other arithmetic  23.2 us (10%)
  local copies, waits for them, and re-layouts  20.2 us (8%)
  between operations  15 us (6%)
  matrix products  8.3 us (3%)
  starting transfers between devices  6.45 us (3%)
    ppermute x1, waiting for transfers between devices, chip_scatter(): held = keep + lax.ppermute(send, lanes, cross_first)  55.1 us
    psum x1, waiting for transfers between devices, body(): drift = lax.psum(island_drift, 'island') / replicas  43.3 us
    psum x1, blocking collectives, body(): lax.psum(local_tiles(island_drift, tile_rows, first_row), ('island', 'chi...  42.3 us
    ppermute x1, waiting for transfers between devices, chip_scatter(): return (keep + lax.ppermute(send, lanes, cross_second))[:, None]  15.8 us
    psum x1, blocking collectives, body(): squares = lax.psum(jnp.sum(gradient * gradient), ('chip', 'core'))  13.3 us
    reduce_sum x1, other arithmetic, local_tiles(): jnp.sum(drift_rows, axis=1)  6.96 us
    dynamic_slice x1, local copies, waits for them, and re-layouts, parity(): lax.dynamic_slice_in_dim(tokens, (2 * k + side) * own_rows, own_rows, axi...  6.33 us
    add x1, other arithmetic, chip_scatter(): held = keep + lax.ppermute(send, lanes, cross_first)  5.63 us
  transfers between devices with their start and end apart: 9, of which 3 were waited for; matrix products, arithmetic and copies ran while one was open for 8% of the time, Pallas kernels for 0%

profile of v15, /device:TPU:0, one launch (start us, length us, event | category | flops | bytes accessed | tf_op | source)
XLA Modules:
  0.0 243.0 jit_solution(12464647187681908411)
XLA Ops:
  7.2 0.0 reduce-scatter.4.cloned.1.call-start
  7.2 6.3 %dynamic-slice_bitcast_fusion.3 = (bf16[512,1024]{1,0:T(8,128)(2,1)}, bf16[512,1024]{1,0:T(8,128)(2,1)}, bf16[512,1,1024]{2,0,1:T(8,128)(2,1)}, bf16[512,1,1024]...) fusion(bf16[1,512,8192]{2,1,0:T(8,128)(2,1)} %param.8, ...), kind=kLoop, calls=%fused_computation.47 | loop fusion | bytes 16777248 | tf_op jit(solution)/shard_map/dynamic_slice | solution.py:99
  13.5 0.5 collective-permute-start.1
  14.0 0.1 collective-permute-start.2
  14.1 0.5 collective-permute-start.4
  14.5 0.1 collective-permute-start.3
  14.6 0.5 multiply_cosine_fusion
  15.1 1.3 copy.35
  16.4 0.0 copy-start.3
  16.4 0.0 copy-start.4
  16.4 0.2 add_convert_fusion
  16.6 0.5 collective-permute-start
  17.2 0.5 copy-done.3
  17.6 0.3 copy-done.4
  17.9 3.7 %fusion = f32[512,4,1024]{2,0,1:T(8,128)S(1)} fusion(bf16[512,512,1]{0,1,2:T(8,128)(2,1)S(1)} %bitcast.108, bf16[512,1,1024]{2,0,1:T(8,128)(2,1)S(1)} %copy-done.3, bf16[512,1,1024]{2,0,1:T(8,128)(2,1)S(1)} %copy-done.4, bf16[512,1,1024]{2,0,1:T(8,128)(2,1)} %get-tuple-element.11, bf16[512,1,1024]{2,0,1:T(8,128)(2,1)} %get-tuple-element.12), kind=kOutput, calls=%fused_computation | convolution fusion | flops 2164260864 | bytes 13107200 | tf_op jit(solution)/shard_map/dot_general | solution.py:106
  21.7 0.0 collective-permute-done
  21.7 0.0 collective-permute-done.1
  21.7 0.0 collective-permute-done.2
  21.7 0.0 collective-permute-done.4
  21.7 0.0 collective-permute-done.3
  21.7 4.2 %fusion.16 = f32[512,4,1024]{2,0,1:T(8,128)S(1)} fusion(f32[512,4,1024]{2,0,1:T(8,128)S(1)} %fusion, bf16[512,1,1024]{2,0,1:T(8,128)(2,1)} %bitcast.16, bf16[512,1,1024]{2,0,1:T(8,128)(2,1)} %bitcast.14, bf16[512,1,1024]{2,0,1:T(8,128)(2,1)} %bitcast.12, bf16[512,1,1024]{2,0,1:T(8,128)(2,1)} %bitcast.10, bf16[512,512]{0,1:T(8,128)(2,1)S(1)} %collective-permute-done), kind=kOutput, calls=%fused_computation.17 | convolution fusion | flops 2166358016 | bytes 21495808 | tf_op jit(solution)/shard_map/dot_general | solution.py:108
  25.9 0.0 copy-start.1
  25.9 3.2 %copy-done.1 = f32[512,4,1024]{2,0,1:T(8,128)} copy-done((f32[512,4,1024]{2,0,1:T(8,128)}, f32[512,4,1024]{2,0,1:T(8,128)S(1)}, u32[]{:S(2)}) %copy-start.1) | copy-done | bytes 8388632
  29.2 2.1 slice.44
  31.3 0.0 reduce-scatter.4.cloned.1.call-update
  31.3 0.0 all-reduce.3.cloned.1.call-start
  31.4 3.2 %slice.45 = f32[320,4,1024]{2,0,1:T(8,128)S(1)} slice(f32[512,4,1024]{2,0,1:T(8,128)} %copy-done.1), slice={[192:512], [0:4], [0:1024]} | slice | bytes 10485760 | tf_op jit(solution)/shard_map/slice | solution.py:123
  34.6 0.0 copy-start
  34.6 2.4 broadcast_select_fusion
  37.0 0.7 copy-done
  37.7 2.9 %collective-permute-start.5 = (f32[320,2,1024]{2,0,1:T(8,128)}, f32[320,2,1024]{2,0,1:T(8,128)S(1)}, u32[]{:S(2)}, u32[]{:S(2)}) collective-permute-start(f32[320,2,1024]{2,0,1:T(8,128)} %broadcast_select_fusion), channel_id=1, source_target_pairs={{0,2},{1,5},{2,0},{3,7},{4,6},{5,1},{6,4},{7,3},{8,10},{9,13},{10,... | collective-permute-start | bytes 7864328 | tf_op jit(solution)/shard_map/ppermute | solution.py:72
  40.6 55.1 %collective-permute-done.5 = f32[320,2,1024]{2,0,1:T(8,128)S(1)} collective-permute-done((f32[320,2,1024]{2,0,1:T(8,128)}, f32[320,2,1024]{2,0,1:T(8,128)S(1)}, u32[]{:S(2)}, u32[]{:S(2)}) %collective-permute-start.5) | collective-permute-done | bytes 2621472 | tf_op jit(solution)/shard_map/ppermute | solution.py:72
  95.7 5.6 %select_add_fusion = f32[320,2,1024]{2,0,1:T(8,128)S(1)} fusion(f32[320,2,1024]{2,0,1:T(8,128)S(1)} %collective-permute-done.5, pred[]{:T(512)S(6)} %eq.20, f32[320,2,2,1024]{3,0,2,1:T(8,128)} %bitcast.101, pred[]{:T(512)S(6)} %eq.10), kind=kLoop, calls=%fused_computation.24 | loop fusion | flops 2621440 | bytes 15728642 | tf_op jit(solution)/shard_map/add | solution.py:72
  101.4 0.2 select_bitcast_fusion
  101.6 1.9 collective-permute-start.6
  103.5 15.8 %collective-permute-done.6 = f32[320,1024]{1,0:T(8,128)S(1)} collective-permute-done((f32[320,1024]{1,0:T(8,128)S(1)}, f32[320,1024]{1,0:T(8,128)S(1)}, u32[]{:S(2)}, u32[]{:S(2)}) %collective-permute-start.6) | collective-permute-done | bytes 1310752 | tf_op jit(solution)/shard_map/ppermute | solution.py:75
  119.2 0.4 bitcast_add_fusion.1
  119.6 0.5 copy.34
  120.1 0.0 reduce-scatter.4.cloned.1.call-done
  120.1 1.5 copy.30
  121.6 1.2 multiply_reduce_fusion
  122.7 13.3 %psum.21 = f32[]{:T(128)} all-reduce(f32[]{:T(128)} %multiply_reduce_fusion), channel_id=1, replica_groups=mesh['island'=4,'chip'=4,'core'=2] {'chip','core'}, use_global_device_ids=true, to_apply=%region_2.3 | all-reduce | flops 1 | bytes 8 | tf_op jit(solution)/shard_map/psum | solution.py:129
  136.7 7.0 %fusion.38 = (f32[1024]{0:T(1024)S(1)}, f32[1024,512]{1,0:T(8,128)}) fusion(f32[1024,512]{1,0:T(8,128)} %param.10, f32[1,1024,512]{2,1,0:T(8,128)} %param.14, f32[]{:T(128)S(6)} %sqrt.9, f32[1024,320]{1,0:T(8,128)S(1)} %bitcast.103, f32[1024,192]{1,0:T(8,128)S(1)} %bitcast.105, f32[1,1024,512]{2,1,0:T(8,128)} %param.13, f32[1,1024,512]{2,1,0:T(8,128)} %param.12), kind=kLoop, calls=%fused_computation.73 | loop fusion | flops 9960448 | bytes 12587012 | tf_op jit(solution)/shard_map/reduce_sum | solution.py:53
  143.7 0.0 copy-start.5
  143.7 0.0 copy-start.2
  143.7 0.0 all-reduce.3.cloned.1.call-update
  143.7 0.6 copy-done.5
  144.3 0.1 copy.32
  144.4 0.1 reduce-window.8
  144.5 0.1 reduce
  144.6 0.4 convolution_bitcast_fusion
  145.0 42.3 %psum.23 = f32[48]{0:T(128)S(1)} all-reduce(f32[48]{0:T(128)S(1)} %convolution_bitcast_fusion), channel_id=1, replica_groups=mesh['island'=4,'chip'=4,'core'=2] {'island','chip','core'}, use_global_device_ids=true, to_apply=%region_6.7 | all-reduce | flops 48 | bytes 384 | tf_op jit(solution)/shard_map/psum | solution.py:139
  187.3 0.5 rsqrt_multiply_fusion
  187.8 43.3 %all-reduce.3.cloned.1.call-done = f32[1024,512]{1,0:T(8,128)} async-done(((f32[1024,512]{1,0:T(8,128)}), f32[1024,512]{1,0:T(8,128)}) %all-reduce.3.cloned.1.call-update) | async-done | bytes 2097168 | tf_op jit(solution)/shard_map/psum | solution.py:134
  231.1 0.0 copy-done.2
  231.1 5.0 %multiply_subtract_fusion = (f32[1024,512]{1,0:T(8,128)}, f32[1024,512]{1,0:T(8,128)}) fusion(f32[1024,512]{1,0:T(8,128)S(1)} %copy-done.2, f32[1024,512]{1,0:T(8,128)} %all-reduce.3.cloned.1.call-done, f32[1024,512]{1,0:T(8,128)} %param.11), kind=kLoop, calls=%fused_computation.37 | loop fusion | flops 3670016 | bytes 10485760 | tf_op jit(solution)/shard_map/sub | solution.py:136
  (5 shorter events, 0.1 us)
Async XLA Ops:
  7.2 112.9 %reduce-scatter.4.cloned.1.call-start = ((), (), s32[]{:S(2)}) async-start(), calls=%async_computation.2 | async-start | bytes 3932160
  13.5 8.1 %collective-permute-start.1 = (bf16[512,1024]{1,0:T(8,128)(2,1)}, bf16[512,1024]{1,0:T(8,128)(2,1)}, u32[]{:S(2)}, u32[]{:S(2)}) collective-permute-start(bf16[512,1024]{1,0:T(8,128)(2,1)} %get-tuple-element.7), channel_id=1, source_target_pairs={{0,1},{1,0},{2,3},{3,2},{4,5},{5,4},{6,7},{7,6},{8,9},{9,8},{10,11... | collective-permute-start | bytes 3145736 | tf_op jit(solution)/shard_map/ppermute | solution.py:103
  14.0 7.7 %collective-permute-start.2 = (bf16[512,1024]{1,0:T(8,128)(2,1)}, bf16[512,1024]{1,0:T(8,128)(2,1)}, u32[]{:S(2)}, u32[]{:S(2)}) collective-permute-start(bf16[512,1024]{1,0:T(8,128)(2,1)} %get-tuple-element.8), channel_id=1, source_target_pairs={{0,1},{1,0},{2,3},{3,2},{4,5},{5,4},{6,7},{7,6},{8,9},{9,8},{10,11... | collective-permute-start | bytes 3145736 | tf_op jit(solution)/shard_map/ppermute | solution.py:103
  14.1 7.7 %collective-permute-start.4 = (bf16[512,1024]{1,0:T(8,128)(2,1)S(1)}, bf16[512,1024]{1,0:T(8,128)(2,1)}, u32[]{:S(2)}, u32[]{:S(2)}) collective-permute-start(bf16[512,1024]{1,0:T(8,128)(2,1)S(1)} %get-tuple-element.13), channel_id=1, source_target_pairs={{0,1},{1,0},{2,3},{3,2},{4,5},{5,4},{6,7},{7,6},{8,9},{9,8},{10,11... | collective-permute-start | bytes 3145736 | tf_op jit(solution)/shard_map/ppermute | solution.py:103
  14.5 7.2 %collective-permute-start.3 = (bf16[512,1024]{1,0:T(8,128)(2,1)S(1)}, bf16[512,1024]{1,0:T(8,128)(2,1)}, u32[]{:S(2)}, u32[]{:S(2)}) collective-permute-start(bf16[512,1024]{1,0:T(8,128)(2,1)S(1)} %get-tuple-element.14), channel_id=1, source_target_pairs={{0,1},{1,0},{2,3},{3,2},{4,5},{5,4},{6,7},{7,6},{8,9},{9,8},{10,11... | collective-permute-start | bytes 3145736 | tf_op jit(solution)/shard_map/ppermute | solution.py:103
  16.4 1.2 copy-start.3
  16.4 1.5 copy-start.4
  16.6 5.0 %collective-permute-start = (bf16[512,512]{0,1:T(8,128)(2,1)S(1)}, bf16[512,512]{0,1:T(8,128)(2,1)S(1)}, u32[]{:S(2)}, u32[]{:S(2)}) collective-permute-start(bf16[512,512]{0,1:T(8,128)(2,1)S(1)} %bitcast.107), channel_id=1, source_target_pairs={{0,1},{1,0},{2,3},{3,2},{4,5},{5,4},{6,7},{7,6},{8,9},{9,8},{10,11... | collective-permute-start | bytes 1572872 | tf_op jit(solution)/shard_map/ppermute | solution.py:104
  25.9 3.2 %copy-start.1 = (f32[512,4,1024]{2,0,1:T(8,128)}, f32[512,4,1024]{2,0,1:T(8,128)S(1)}, u32[]{:S(2)}) copy-start(f32[512,4,1024]{2,0,1:T(8,128)S(1)} %fusion.16) | copy-start | bytes 25165828
  31.3 199.8 %all-reduce.3.cloned.1.call-start = ((), (), s32[]{:S(2)}) async-start(), calls=%async_computation.1 | async-start | bytes 4194304 | tf_op jit(solution)/shard_map/psum | solution.py:134
  34.6 3.1 %copy-start = (f32[320,4,1024]{2,0,1:T(8,128)}, f32[320,4,1024]{2,0,1:T(8,128)S(1)}, u32[]{:S(2)}) copy-start(f32[320,4,1024]{2,0,1:T(8,128)S(1)} %slice.45) | copy-start | bytes 15728644
  37.7 58.1 %collective-permute-start.5 = (f32[320,2,1024]{2,0,1:T(8,128)}, f32[320,2,1024]{2,0,1:T(8,128)S(1)}, u32[]{:S(2)}, u32[]{:S(2)}) collective-permute-start(f32[320,2,1024]{2,0,1:T(8,128)} %broadcast_select_fusion), channel_id=1, source_target_pairs={{0,2},{1,5},{2,0},{3,7},{4,6},{5,1},{6,4},{7,3},{8,10},{9,13},{10,... | collective-permute-start | bytes 7864328 | tf_op jit(solution)/shard_map/ppermute | solution.py:72
  101.6 17.7 %collective-permute-start.6 = (f32[320,1024]{1,0:T(8,128)S(1)}, f32[320,1024]{1,0:T(8,128)S(1)}, u32[]{:S(2)}, u32[]{:S(2)}) collective-permute-start(f32[320,1024]{1,0:T(8,128)S(1)} %select_bitcast_fusion), channel_id=1, source_target_pairs={{0,4},{1,3},{2,6},{3,1},{4,0},{5,7},{6,2},{7,5},{8,12},{9,11},{10,... | collective-permute-start | bytes 3932168 | tf_op jit(solution)/shard_map/ppermute | solution.py:75
  143.7 0.7 copy-start.5
  143.7 87.5 %copy-start.2 = (f32[1024,512]{1,0:T(8,128)S(1)}, f32[1024,512]{1,0:T(8,128)}, u32[]{:S(2)}) copy-start(f32[1024,512]{1,0:T(8,128)} %param.10) | copy-start | bytes 6291460
Sparse Core Ops, SparseCore 0:
  31.4 59.2 reduce-scatter.3
  143.8 87.2 all-reduce.2

commit v16 on v10

--- a/solution.py
+++ b/solution.py
@@ -53,7 +53,7 @@
     return jnp.dot(jnp.sum(drift_rows, axis=1), member, precision=lax.Precision.HIGHEST)
 
 
-def chip_scatter(partial, chips):
+def chip_scatter(partial, chips, after=None):
     core = lax.axis_index("core")
     chip = lax.axis_index("chip")
     along_x, along_y = chip % 2, chip // 2
@@ -69,10 +69,13 @@
     upper = jnp.where(core == 0, by_x[1], by_y[1])
     keep = jnp.where(first == 0, lower, upper)
     send = jnp.where(first == 0, upper, lower)
-    held = keep + lax.ppermute(send, lanes, cross_first)
+    if after is not None:
+        send, _ = lax.optimization_barrier((send, after))
+    arrived = lax.ppermute(send, lanes, cross_first)
+    held = keep + arrived
     keep = jnp.where(second == 0, held[:, 0], held[:, 1])
     send = jnp.where(second == 0, held[:, 1], held[:, 0])
-    return (keep + lax.ppermute(send, lanes, cross_second))[:, None]
+    return (keep + lax.ppermute(send, lanes, cross_second))[:, None], arrived
 
 
 def body(
@@ -113,6 +116,12 @@
         block = with_layout_constraint(block, Layout((0, 1, 2)))
         return with_layout_constraint(block.reshape(block.shape[0], own_rows).T, Layout((0, 1)))
 
+    def pieces(block):
+        cut = block.shape[0] // 2
+        first, arrived = chip_scatter(block[:cut], chips)
+        second, _ = chip_scatter(block[cut:], chips, after=arrived)
+        return rows_major(first), rows_major(second)
+
     if chips == 4:
         split = partial.shape[0] // 2
         gradient = jnp.concatenate(
@@ -120,7 +129,7 @@
                 rows_major(
                     lax.psum_scatter(partial[:split], "chip", scatter_dimension=1, tiled=True)
                 ),
-                rows_major(chip_scatter(partial[split:], chips)),
+                *pieces(partial[split:]),
             ],
             axis=1,
         )

time: 234 us -> 240 us (1.026)
  local copies, waits for them, and re-layouts: 15 us -> 22.1 us
  other arithmetic: 25.4 us -> 20.6 us
  waiting for transfers between devices: 106 us -> 110 us
    select_n x1 -> x2, other arithmetic: 5.96 us -> 0.36 us  [chip_scatter(): send = jnp.where(first == 0, upper, lower)]
    unnamed x8 -> x12, local copies, waits for them, and re-layouts: 1.42 us -> 5.78 us
    ppermute x2 -> x4, waiting for transfers between devices: 62.9 us -> 66.5 us  [the longest x2 58.7 us: chip_scatter(): arrived = lax.ppermute(send, lanes, cross_first)]
    slice x0 -> x1, local copies, waits for them, and re-layouts: none -> 2.54 us  [pieces(): first, arrived = chip_scatter(block[:cut], chips)]
    ppermute x2 -> x4, starting transfers between devices: 6.27 us -> 6.99 us  [the longest x2 5.53 us: chip_scatter(): arrived = lax.ppermute(send, lanes, cross_first)]
    add x2 -> x3, other arithmetic: 5.05 us -> 4.76 us  [the longest x2 4.67 us: chip_scatter(): held = keep + arrived]
  transfers between devices with their start and end apart: 9 -> 11, of which waited for: 3 -> 4; matrix products, arithmetic and copies ran while one was open for 8% -> 7% of each run, Pallas kernels for 0% -> 0%
where the time goes in v16:
time: 240 us
  waiting for transfers between devices  110 us (46%)
  blocking collectives  54.7 us (23%)
  local copies, waits for them, and re-layouts  22.1 us (9%)
  other arithmetic  20.6 us (9%)
  between operations  15 us (6%)
  starting transfers between devices  8.61 us (4%)
  matrix products  8.3 us (3%)
    ppermute x2, waiting for transfers between devices, chip_scatter(): arrived = lax.ppermute(send, lanes, cross_first)  58.7 us
    psum x1, waiting for transfers between devices, body(): drift = lax.psum(island_drift, 'island') / replicas  43.8 us
    psum x1, blocking collectives, body(): lax.psum(local_tiles(island_drift, tile_rows, first_row), ('island', 'chi...  42.3 us
    psum x1, blocking collectives, body(): squares = lax.psum(jnp.sum(gradient * gradient), ('chip', 'core'))  12.4 us
    ppermute x2, waiting for transfers between devices, chip_scatter(): return ((keep + lax.ppermute(send, lanes, cross_second))[:, None], arrived)  7.78 us
    reduce_sum x1, other arithmetic, local_tiles(): jnp.sum(drift_rows, axis=1)  6.37 us
    dynamic_slice x1, local copies, waits for them, and re-layouts, parity(): lax.dynamic_slice_in_dim(tokens, (2 * k + side) * own_rows, own_rows, axi...  6.33 us
    unnamed x12, local copies, waits for them, and re-layouts  5.78 us
  transfers between devices with their start and end apart: 11, of which 4 were waited for; matrix products, arithmetic and copies ran while one was open for 7% of the time, Pallas kernels for 0%

profile of v16, /device:TPU:0, one launch (start us, length us, event | category | flops | bytes accessed | tf_op | source)
XLA Modules:
  0.0 239.7 jit_solution(17627024546153795948)
XLA Ops:
  7.2 0.0 reduce-scatter.4.cloned.1.call-start
  7.2 6.3 %dynamic-slice_bitcast_fusion.3 = (bf16[512,1024]{1,0:T(8,128)(2,1)}, bf16[512,1024]{1,0:T(8,128)(2,1)}, bf16[512,1,1024]{2,0,1:T(8,128)(2,1)}, bf16[512,1,1024]...) fusion(bf16[1,512,8192]{2,1,0:T(8,128)(2,1)} %param.8, ...), kind=kLoop, calls=%fused_computation.51 | loop fusion | bytes 16777248 | tf_op jit(solution)/shard_map/dynamic_slice | solution.py:102
  13.6 0.5 collective-permute-start.1
  14.0 0.1 collective-permute-start.2
  14.1 0.5 collective-permute-start.3
  14.5 0.1 collective-permute-start.4
  14.6 0.5 multiply_cosine_fusion
  15.1 1.3 copy.44
  16.4 0.0 copy-start.3
  16.4 0.0 copy-start.4
  16.4 0.2 add_convert_fusion
  16.6 0.5 collective-permute-start
  17.2 0.5 copy-done.3
  17.6 0.3 copy-done.4
  17.9 3.7 %fusion = f32[512,4,1024]{2,0,1:T(8,128)S(1)} fusion(bf16[512,512,1]{0,1,2:T(8,128)(2,1)S(1)} %bitcast.156, bf16[512,1,1024]{2,0,1:T(8,128)(2,1)S(1)} %copy-done.3, bf16[512,1,1024]{2,0,1:T(8,128)(2,1)S(1)} %copy-done.4, bf16[512,1,1024]{2,0,1:T(8,128)(2,1)} %get-tuple-element.15, bf16[512,1,1024]{2,0,1:T(8,128)(2,1)} %get-tuple-element.16), kind=kOutput, calls=%fused_computation | convolution fusion | flops 2164260864 | bytes 13107200 | tf_op jit(solution)/shard_map/dot_general | solution.py:109
  21.7 0.0 collective-permute-done
  21.7 0.0 collective-permute-done.1
  21.7 0.0 collective-permute-done.2
  21.7 0.0 collective-permute-done.3
  21.7 0.0 collective-permute-done.4
  21.7 4.2 %fusion.16 = f32[512,4,1024]{2,0,1:T(8,128)S(1)} fusion(f32[512,4,1024]{2,0,1:T(8,128)S(1)} %fusion, bf16[512,1,1024]{2,0,1:T(8,128)(2,1)} %bitcast.16, bf16[512,1,1024]{2,0,1:T(8,128)(2,1)} %bitcast.14, bf16[512,1,1024]{2,0,1:T(8,128)(2,1)} %bitcast.12, bf16[512,1,1024]{2,0,1:T(8,128)(2,1)} %bitcast.10, bf16[512,512]{0,1:T(8,128)(2,1)S(1)} %collective-permute-done), kind=kOutput, calls=%fused_computation.17 | convolution fusion | flops 2166358016 | bytes 21495808 | tf_op jit(solution)/shard_map/dot_general | solution.py:111
  25.9 0.0 copy-start.1
  25.9 3.2 %copy-done.1 = f32[512,4,1024]{2,0,1:T(8,128)} copy-done((f32[512,4,1024]{2,0,1:T(8,128)}, f32[512,4,1024]{2,0,1:T(8,128)S(1)}, u32[]{:S(2)}) %copy-start.1) | copy-done | bytes 8388632
  29.2 2.5 %slice.77 = f32[256,4,1024]{2,0,1:T(8,128)} slice(f32[512,4,1024]{2,0,1:T(8,128)S(1)} %fusion.16), slice={[0:256], [0:4], [0:1024]} | slice | bytes 8388608 | tf_op jit(solution)/shard_map/slice | solution.py:130
  31.6 0.0 reduce-scatter.4.cloned.1.call-update
  31.6 0.0 all-reduce.3.cloned.1.call-start
  31.7 2.5 %fusion.43 = (f32[128,4,1024]{2,0,1:T(8,128)S(1)}, f32[128,4,1024]{2,0,1:T(8,128)S(1)}) fusion(f32[512,4,1024]{2,0,1:T(8,128)} %copy-done.1), kind=kLoop, calls=%fused_computation.85 | loop fusion | bytes 8388608 | tf_op jit(solution)/shard_map/slice | solution.py:121
  34.3 0.0 copy-start
  34.3 0.2 broadcast_select_fusion.1
  34.4 1.1 copy-done
  35.6 2.9 %collective-permute-start.5 = (f32[128,2,1024]{2,0,1:T(8,128)S(1)}, f32[128,2,1024]{2,0,1:T(8,128)}, u32[]{:S(2)}, u32[]{:S(2)}) collective-permute-start(f32[128,2,1024]{2,0,1:T(8,128)S(1)} %broadcast_select_fusion.1), channel_id=1, source_target_pairs={{0,2},{1,5},{2,0},{3,7},{4,6},{5,1},{6,4},{7,3},{8,10},{9,13},{10,... | collective-permute-start | bytes 3145736 | tf_op jit(solution)/shard_map/ppermute | solution.py:74
  38.5 0.2 broadcast_select_fusion
  38.7 32.0 %collective-permute-done.5 = f32[128,2,1024]{2,0,1:T(8,128)} collective-permute-done((f32[128,2,1024]{2,0,1:T(8,128)S(1)}, f32[128,2,1024]{2,0,1:T(8,128)}, u32[]{:S(2)}, u32[]{:S(2)}) %collective-permute-start.5) | collective-permute-done | bytes 1048608 | tf_op jit(solution)/shard_map/ppermute | solution.py:74
  70.7 2.6 %collective-permute-start.7 = (f32[128,2,1024]{2,0,1:T(8,128)S(1)}, f32[128,2,1024]{2,0,1:T(8,128)}, u32[]{:S(2)}, u32[]{:S(2)}) collective-permute-start(f32[128,2,1024]{2,0,1:T(8,128)S(1)} %broadcast_select_fusion), channel_id=1, source_target_pairs={{0,2},{1,5},{2,0},{3,7},{4,6},{5,1},{6,4},{7,3},{8,10},{9,13},{10,... | collective-permute-start | bytes 3145736 | tf_op jit(solution)/shard_map/ppermute | solution.py:74
  73.3 3.1 %select_add_fusion.1 = f32[128,2,1024]{2,0,1:T(8,128)S(1)} fusion(f32[128,2,1024]{2,0,1:T(8,128)} %collective-permute-done.5, pred[]{:T(512)S(6)} %eq.13, f32[128,2,2,1024]{3,0,2,1:T(8,128)} %bitcast.147, pred[]{:T(512)S(6)} %eq.11), kind=kLoop, calls=%fused_computation.47 | loop fusion | flops 1048576 | bytes 6291458 | tf_op jit(solution)/shard_map/add | solution.py:75
  76.4 0.1 select_bitcast_fusion.1
  76.5 1.1 collective-permute-start.6
  77.6 26.7 %collective-permute-done.7 = f32[128,2,1024]{2,0,1:T(8,128)} collective-permute-done((f32[128,2,1024]{2,0,1:T(8,128)S(1)}, f32[128,2,1024]{2,0,1:T(8,128)}, u32[]{:S(2)}, u32[]{:S(2)}) %collective-permute-start.7) | collective-permute-done | bytes 1048608 | tf_op jit(solution)/shard_map/ppermute | solution.py:74
  104.3 1.6 select_add_fusion
  105.8 0.1 select_bitcast_fusion
  105.9 0.4 collective-permute-start.8
  106.3 0.0 collective-permute-done.6
  106.3 0.1 fusion.31
  106.4 1.0 copy.38
  107.4 7.8 %collective-permute-done.8 = f32[128,1024]{1,0:T(8,128)S(1)} collective-permute-done((f32[128,1024]{1,0:T(8,128)S(1)}, f32[128,1024]{1,0:T(8,128)S(1)}, u32[]{:S(2)}, u32[]{:S(2)}) %collective-permute-start.8) | collective-permute-done | bytes 524320 | tf_op jit(solution)/shard_map/ppermute | solution.py:78
  115.2 0.1 bitcast_add_fusion.1
  115.3 1.0 copy.43
  116.3 0.0 copy-start.2
  116.3 0.0 reduce-scatter.4.cloned.1.call-done
  116.3 1.7 copy.36
  118.0 2.3 multiply_reduce_fusion
  120.3 12.4 %psum.21 = f32[]{:T(128)} all-reduce(f32[]{:T(128)} %multiply_reduce_fusion), channel_id=1, replica_groups=mesh['island'=4,'chip'=4,'core'=2] {'chip','core'}, use_global_device_ids=true, to_apply=%region_2.3 | all-reduce | flops 1 | bytes 8 | tf_op jit(solution)/shard_map/psum | solution.py:138
  133.4 0.0 copy-done.2
  133.4 6.4 %fusion.41 = (f32[1024]{0:T(1024)S(1)}, f32[1024,512]{1,0:T(8,128)}) fusion(f32[1024,512]{1,0:T(8,128)S(1)} %copy-done.2, f32[1,1024,512]{2,1,0:T(8,128)} %param.14, f32[]{:T(128)S(6)} %sqrt.9, f32[1024,128]{1,0:T(8,128)} %bitcast.153, f32[1024,128]{1,0:T(8,128)} %bitcast.151, f32[1024,256]{1,0:T(8,128)S(1)} %bitcast.149, f32[1,1024,512]{2,1,0:T(8,128)} %param.13, ...), kind=kLoop, calls=%fused_computation.84 | loop fusion | flops 10484736 | bytes 12587012 | tf_op jit(solution)/shard_map/reduce_sum | solution.py:53
  139.8 0.0 all-reduce.3.cloned.1.call-update
  139.8 0.6 copy-done.5
  140.5 0.1 copy.40
  140.6 0.1 reduce-window.8
  140.6 0.1 reduce
  140.8 0.4 convolution_bitcast_fusion
  141.1 42.3 %psum.23 = f32[48]{0:T(128)S(1)} all-reduce(f32[48]{0:T(128)S(1)} %convolution_bitcast_fusion), channel_id=1, replica_groups=mesh['island'=4,'chip'=4,'core'=2] {'island','chip','core'}, use_global_device_ids=true, to_apply=%region_6.7 | all-reduce | flops 48 | bytes 384 | tf_op jit(solution)/shard_map/psum | solution.py:148
  183.4 0.5 rsqrt_multiply_fusion
  184.0 43.8 %all-reduce.3.cloned.1.call-done = f32[1024,512]{1,0:T(8,128)} async-done(((f32[1024,512]{1,0:T(8,128)}), f32[1024,512]{1,0:T(8,128)}) %all-reduce.3.cloned.1.call-update) | async-done | bytes 2097168 | tf_op jit(solution)/shard_map/psum | solution.py:143
  227.8 5.0 %multiply_subtract_fusion = (f32[1024,512]{1,0:T(8,128)}, f32[1024,512]{1,0:T(8,128)}) fusion(f32[1024,512]{1,0:T(8,128)S(1)} %copy-done.2, f32[1024,512]{1,0:T(8,128)} %all-reduce.3.cloned.1.call-done, f32[1024,512]{1,0:T(8,128)} %param.11), kind=kLoop, calls=%fused_computation.30 | loop fusion | flops 3670016 | bytes 10485760 | tf_op jit(solution)/shard_map/sub | solution.py:145
  (6 shorter events, 0.1 us)
Async XLA Ops:
  7.2 109.1 %reduce-scatter.4.cloned.1.call-start = ((), (), s32[]{:S(2)}) async-start(), calls=%async_computation.2 | async-start | bytes 5242880
  13.6 8.1 %collective-permute-start.1 = (bf16[512,1024]{1,0:T(8,128)(2,1)}, bf16[512,1024]{1,0:T(8,128)(2,1)}, u32[]{:S(2)}, u32[]{:S(2)}) collective-permute-start(bf16[512,1024]{1,0:T(8,128)(2,1)} %get-tuple-element.11), channel_id=1, source_target_pairs={{0,1},{1,0},{2,3},{3,2},{4,5},{5,4},{6,7},{7,6},{8,9},{9,8},{10,11... | collective-permute-start | bytes 3145736 | tf_op jit(solution)/shard_map/ppermute | solution.py:106
  14.0 7.7 %collective-permute-start.2 = (bf16[512,1024]{1,0:T(8,128)(2,1)}, bf16[512,1024]{1,0:T(8,128)(2,1)}, u32[]{:S(2)}, u32[]{:S(2)}) collective-permute-start(bf16[512,1024]{1,0:T(8,128)(2,1)} %get-tuple-element.12), channel_id=1, source_target_pairs={{0,1},{1,0},{2,3},{3,2},{4,5},{5,4},{6,7},{7,6},{8,9},{9,8},{10,11... | collective-permute-start | bytes 3145736 | tf_op jit(solution)/shard_map/ppermute | solution.py:106
  14.1 7.7 %collective-permute-start.3 = (bf16[512,1024]{1,0:T(8,128)(2,1)S(1)}, bf16[512,1024]{1,0:T(8,128)(2,1)}, u32[]{:S(2)}, u32[]{:S(2)}) collective-permute-start(bf16[512,1024]{1,0:T(8,128)(2,1)S(1)} %get-tuple-element.18), channel_id=1, source_target_pairs={{0,1},{1,0},{2,3},{3,2},{4,5},{5,4},{6,7},{7,6},{8,9},{9,8},{10,11... | collective-permute-start | bytes 3145736 | tf_op jit(solution)/shard_map/ppermute | solution.py:106
  14.5 7.2 %collective-permute-start.4 = (bf16[512,1024]{1,0:T(8,128)(2,1)S(1)}, bf16[512,1024]{1,0:T(8,128)(2,1)}, u32[]{:S(2)}, u32[]{:S(2)}) collective-permute-start(bf16[512,1024]{1,0:T(8,128)(2,1)S(1)} %get-tuple-element.17), channel_id=1, source_target_pairs={{0,1},{1,0},{2,3},{3,2},{4,5},{5,4},{6,7},{7,6},{8,9},{9,8},{10,11... | collective-permute-start | bytes 3145736 | tf_op jit(solution)/shard_map/ppermute | solution.py:106
  16.4 1.2 copy-start.3
  16.4 1.5 copy-start.4
  16.6 5.0 %collective-permute-start = (bf16[512,512]{0,1:T(8,128)(2,1)S(1)}, bf16[512,512]{0,1:T(8,128)(2,1)S(1)}, u32[]{:S(2)}, u32[]{:S(2)}) collective-permute-start(bf16[512,512]{0,1:T(8,128)(2,1)S(1)} %bitcast.155), channel_id=1, source_target_pairs={{0,1},{1,0},{2,3},{3,2},{4,5},{5,4},{6,7},{7,6},{8,9},{9,8},{10,11... | collective-permute-start | bytes 1572872 | tf_op jit(solution)/shard_map/ppermute | solution.py:107
  25.9 3.2 %copy-start.1 = (f32[512,4,1024]{2,0,1:T(8,128)}, f32[512,4,1024]{2,0,1:T(8,128)S(1)}, u32[]{:S(2)}) copy-start(f32[512,4,1024]{2,0,1:T(8,128)S(1)} %fusion.16) | copy-start | bytes 25165828
  31.6 196.2 %all-reduce.3.cloned.1.call-start = ((), (), s32[]{:S(2)}) async-start(), calls=%async_computation.1 | async-start | bytes 4194304 | tf_op jit(solution)/shard_map/psum | solution.py:143
  34.3 1.3 copy-start
  35.6 35.1 %collective-permute-start.5 = (f32[128,2,1024]{2,0,1:T(8,128)S(1)}, f32[128,2,1024]{2,0,1:T(8,128)}, u32[]{:S(2)}, u32[]{:S(2)}) collective-permute-start(f32[128,2,1024]{2,0,1:T(8,128)S(1)} %broadcast_select_fusion.1), channel_id=1, source_target_pairs={{0,2},{1,5},{2,0},{3,7},{4,6},{5,1},{6,4},{7,3},{8,10},{9,13},{10,... | collective-permute-start | bytes 3145736 | tf_op jit(solution)/shard_map/ppermute | solution.py:74
  70.7 33.6 %collective-permute-start.7 = (f32[128,2,1024]{2,0,1:T(8,128)S(1)}, f32[128,2,1024]{2,0,1:T(8,128)}, u32[]{:S(2)}, u32[]{:S(2)}) collective-permute-start(f32[128,2,1024]{2,0,1:T(8,128)S(1)} %broadcast_select_fusion), channel_id=1, source_target_pairs={{0,2},{1,5},{2,0},{3,7},{4,6},{5,1},{6,4},{7,3},{8,10},{9,13},{10,... | collective-permute-start | bytes 3145736 | tf_op jit(solution)/shard_map/ppermute | solution.py:74
  76.5 29.8 %collective-permute-start.6 = (f32[128,1024]{1,0:T(8,128)S(1)}, f32[128,1024]{1,0:T(8,128)S(1)}, u32[]{:S(2)}, u32[]{:S(2)}) collective-permute-start(f32[128,1024]{1,0:T(8,128)S(1)} %select_bitcast_fusion.1), channel_id=1, source_target_pairs={{0,4},{1,3},{2,6},{3,1},{4,0},{5,7},{6,2},{7,5},{8,12},{9,11},{10,... | collective-permute-start | bytes 1572872 | tf_op jit(solution)/shard_map/ppermute | solution.py:78
  105.9 9.2 %collective-permute-start.8 = (f32[128,1024]{1,0:T(8,128)S(1)}, f32[128,1024]{1,0:T(8,128)S(1)}, u32[]{:S(2)}, u32[]{:S(2)}) collective-permute-start(f32[128,1024]{1,0:T(8,128)S(1)} %select_bitcast_fusion), channel_id=1, source_target_pairs={{0,4},{1,3},{2,6},{3,1},{4,0},{5,7},{6,2},{7,5},{8,12},{9,11},{10,... | collective-permute-start | bytes 1572872 | tf_op jit(solution)/shard_map/ppermute | solution.py:78
  116.3 17.2 %copy-start.2 = (f32[1024,512]{1,0:T(8,128)S(1)}, f32[1024,512]{1,0:T(8,128)}, u32[]{:S(2)}) copy-start(f32[1024,512]{1,0:T(8,128)} %param.10) | copy-start | bytes 6291460
  139.8 0.7 copy-start.5
Sparse Core Ops, SparseCore 0:
  31.8 73.0 reduce-scatter.3
  140.0 87.7 all-reduce.2

commit v17 on v15

--- a/solution.py
+++ b/solution.py
@@ -114,7 +114,7 @@
         return with_layout_constraint(block.reshape(block.shape[0], own_rows).T, Layout((0, 1)))
 
     if chips == 4:
-        split = partial.shape[0] * 3 // 8
+        split = partial.shape[0] * 9 // 16
         gradient = jnp.concatenate(
             [
                 rows_major(

time: 243 us -> 236 us (0.971)
  waiting for transfers between devices: 114 us -> 107 us
  other arithmetic: 23.2 us -> 20.7 us
    ppermute x1, waiting for transfers between devices: 55.1 us -> 46.6 us  [chip_scatter(): held = keep + lax.ppermute(send, lanes, cross_first)]
    ppermute x1, waiting for transfers between devices: 15.8 us -> 18.7 us  [chip_scatter(): return (keep + lax.ppermute(send, lanes, cross_second))[:, None]]
  transfers between devices with their start and end apart: 9 -> 9, of which waited for: 3 -> 3; matrix products, arithmetic and copies ran while one was open for 8% -> 7% of each run, Pallas kernels for 0% -> 0%
where the time goes in v17:
time: 236 us
  waiting for transfers between devices  107 us (45%)
  blocking collectives  56.6 us (24%)
  local copies, waits for them, and re-layouts  21.4 us (9%)
  other arithmetic  20.7 us (9%)
  between operations  15 us (6%)
  matrix products  8.3 us (4%)
  starting transfers between devices  6.73 us (3%)
    ppermute x1, waiting for transfers between devices, chip_scatter(): held = keep + lax.ppermute(send, lanes, cross_first)  46.6 us
    psum x1, blocking collectives, body(): lax.psum(local_tiles(island_drift, tile_rows, first_row), ('island', 'chi...  43 us
    psum x1, waiting for transfers between devices, body(): drift = lax.psum(island_drift, 'island') / replicas  42 us
    ppermute x1, waiting for transfers between devices, chip_scatter(): return (keep + lax.ppermute(send, lanes, cross_second))[:, None]  18.7 us
    psum x1, blocking collectives, body(): squares = lax.psum(jnp.sum(gradient * gradient), ('chip', 'core'))  13.6 us
    reduce_sum x1, other arithmetic, local_tiles(): jnp.sum(drift_rows, axis=1)  6.88 us
    unnamed x12, local copies, waits for them, and re-layouts  6.42 us
    dynamic_slice x1, local copies, waits for them, and re-layouts, parity(): lax.dynamic_slice_in_dim(tokens, (2 * k + side) * own_rows, own_rows, axi...  6.33 us
  transfers between devices with their start and end apart: 9, of which 3 were waited for; matrix products, arithmetic and copies ran while one was open for 7% of the time, Pallas kernels for 0%

profile of v17, /device:TPU:0, one launch (start us, length us, event | category | flops | bytes accessed | tf_op | source)
XLA Modules:
  0.0 236.0 jit_solution(12583074545184184040)
XLA Ops:
  7.2 0.0 reduce-scatter.4.cloned.1.call-start
  7.2 6.3 %dynamic-slice_bitcast_fusion.3 = (bf16[512,1024]{1,0:T(8,128)(2,1)}, bf16[512,1024]{1,0:T(8,128)(2,1)}, bf16[512,1,1024]{2,0,1:T(8,128)(2,1)}, bf16[512,1,1024]...) fusion(bf16[1,512,8192]{2,1,0:T(8,128)(2,1)} %param.8, ...), kind=kLoop, calls=%fused_computation.44 | loop fusion | bytes 16777248 | tf_op jit(solution)/shard_map/dynamic_slice | solution.py:99
  13.5 0.5 collective-permute-start.1
  14.0 0.1 collective-permute-start.2
  14.1 0.5 collective-permute-start.3
  14.5 0.1 collective-permute-start.4
  14.6 0.5 multiply_cosine_fusion
  15.1 1.3 copy.35
  16.4 0.0 copy-start.3
  16.4 0.0 copy-start.4
  16.4 0.2 add_convert_fusion
  16.6 0.5 collective-permute-start
  17.2 0.5 copy-done.3
  17.6 0.3 copy-done.4
  17.9 3.7 %fusion = f32[512,4,1024]{2,0,1:T(8,128)S(1)} fusion(bf16[512,512,1]{0,1,2:T(8,128)(2,1)S(1)} %bitcast.108, bf16[512,1,1024]{2,0,1:T(8,128)(2,1)S(1)} %copy-done.3, bf16[512,1,1024]{2,0,1:T(8,128)(2,1)S(1)} %copy-done.4, bf16[512,1,1024]{2,0,1:T(8,128)(2,1)} %get-tuple-element.11, bf16[512,1,1024]{2,0,1:T(8,128)(2,1)} %get-tuple-element.12), kind=kOutput, calls=%fused_computation | convolution fusion | flops 2164260864 | bytes 13107200 | tf_op jit(solution)/shard_map/dot_general | solution.py:106
  21.7 0.0 collective-permute-done
  21.7 0.0 collective-permute-done.1
  21.7 0.0 collective-permute-done.2
  21.7 0.0 collective-permute-done.3
  21.7 0.0 collective-permute-done.4
  21.7 4.2 %fusion.16 = f32[512,4,1024]{2,0,1:T(8,128)S(1)} fusion(f32[512,4,1024]{2,0,1:T(8,128)S(1)} %fusion, bf16[512,1,1024]{2,0,1:T(8,128)(2,1)} %bitcast.16, bf16[512,1,1024]{2,0,1:T(8,128)(2,1)} %bitcast.14, bf16[512,1,1024]{2,0,1:T(8,128)(2,1)} %bitcast.12, bf16[512,1,1024]{2,0,1:T(8,128)(2,1)} %bitcast.10, bf16[512,512]{0,1:T(8,128)(2,1)S(1)} %collective-permute-done), kind=kOutput, calls=%fused_computation.17 | convolution fusion | flops 2166358016 | bytes 21495808 | tf_op jit(solution)/shard_map/dot_general | solution.py:108
  25.9 0.0 copy-start.1
  25.9 3.2 %copy-done.1 = f32[512,4,1024]{2,0,1:T(8,128)} copy-done((f32[512,4,1024]{2,0,1:T(8,128)}, f32[512,4,1024]{2,0,1:T(8,128)S(1)}, u32[]{:S(2)}) %copy-start.1) | copy-done | bytes 8388632
  29.2 2.7 %slice.44 = f32[288,4,1024]{2,0,1:T(8,128)} slice(f32[512,4,1024]{2,0,1:T(8,128)S(1)} %fusion.16), slice={[0:288], [0:4], [0:1024]} | slice | bytes 9437184 | tf_op jit(solution)/shard_map/slice | solution.py:121
  31.9 0.0 reduce-scatter.4.cloned.1.call-update
  31.9 0.0 all-reduce.3.cloned.1.call-start
  32.0 2.5 %slice.45 = f32[224,4,1024]{2,0,1:T(8,128)S(1)} slice(f32[512,4,1024]{2,0,1:T(8,128)} %copy-done.1), slice={[288:512], [0:4], [0:1024]} | slice | bytes 7340032 | tf_op jit(solution)/shard_map/slice | solution.py:123
  34.5 0.0 copy-start
  34.5 1.8 copy-done
  36.3 0.3 broadcast_select_fusion
  36.7 3.0 %collective-permute-start.5 = (f32[224,2,1024]{2,0,1:T(8,128)S(1)}, f32[224,2,1024]{2,0,1:T(8,128)}, u32[]{:S(2)}, u32[]{:S(2)}) collective-permute-start(f32[224,2,1024]{2,0,1:T(8,128)S(1)} %broadcast_select_fusion), channel_id=1, source_target_pairs={{0,2},{1,5},{2,0},{3,7},{4,6},{5,1},{6,4},{7,3},{8,10},{9,13},{10,... | collective-permute-start | bytes 5505032 | tf_op jit(solution)/shard_map/ppermute | solution.py:72
  39.7 46.6 %collective-permute-done.5 = f32[224,2,1024]{2,0,1:T(8,128)} collective-permute-done((f32[224,2,1024]{2,0,1:T(8,128)S(1)}, f32[224,2,1024]{2,0,1:T(8,128)}, u32[]{:S(2)}, u32[]{:S(2)}) %collective-permute-start.5) | collective-permute-done | bytes 1835040 | tf_op jit(solution)/shard_map/ppermute | solution.py:72
  86.3 5.5 %select_add_fusion = f32[224,2,1024]{2,0,1:T(8,128)S(1)} fusion(f32[224,2,1024]{2,0,1:T(8,128)} %collective-permute-done.5, pred[]{:T(512)S(6)} %eq.20, f32[224,2,2,1024]{3,0,2,1:T(8,128)} %bitcast.101, pred[]{:T(512)S(6)} %eq.10), kind=kLoop, calls=%fused_computation.39 | loop fusion | flops 1835008 | bytes 11010050 | tf_op jit(solution)/shard_map/add | solution.py:72
  91.8 0.1 select_bitcast_fusion
  91.9 2.1 collective-permute-start.6
  94.0 18.7 %collective-permute-done.6 = f32[224,1024]{1,0:T(8,128)S(1)} collective-permute-done((f32[224,1024]{1,0:T(8,128)S(1)}, f32[224,1024]{1,0:T(8,128)S(1)}, u32[]{:S(2)}, u32[]{:S(2)}) %collective-permute-start.6) | collective-permute-done | bytes 917536 | tf_op jit(solution)/shard_map/ppermute | solution.py:75
  112.7 0.2 bitcast_add_fusion.1
  112.9 0.3 copy.34
  113.2 0.0 reduce-scatter.4.cloned.1.call-done
  113.3 1.7 copy.30
  115.0 1.2 multiply_reduce_fusion
  116.2 13.6 %psum.21 = f32[]{:T(128)} all-reduce(f32[]{:T(128)} %multiply_reduce_fusion), channel_id=1, replica_groups=mesh['island'=4,'chip'=4,'core'=2] {'chip','core'}, use_global_device_ids=true, to_apply=%region_2.3 | all-reduce | flops 1 | bytes 8 | tf_op jit(solution)/shard_map/psum | solution.py:129
  130.4 6.9 %fusion.38 = (f32[1024]{0:T(1024)S(1)}, f32[1024,512]{1,0:T(8,128)}) fusion(f32[1024,512]{1,0:T(8,128)} %param.10, f32[1,1024,512]{2,1,0:T(8,128)} %param.14, f32[]{:T(128)S(6)} %sqrt.9, f32[1024,224]{1,0:T(8,128)S(1)} %bitcast.105, f32[1024,288]{1,0:T(8,128)S(1)} %bitcast.103, f32[1,1024,512]{2,1,0:T(8,128)} %param.13, f32[1,1024,512]{2,1,0:T(8,128)} %param.12), kind=kLoop, calls=%fused_computation.73 | loop fusion | flops 9960448 | bytes 12587012 | tf_op jit(solution)/shard_map/reduce_sum | solution.py:53
  137.3 0.0 copy-start.5
  137.3 0.0 copy-start.2
  137.3 0.0 all-reduce.3.cloned.1.call-update
  137.4 0.6 copy-done.5
  138.0 0.1 copy.32
  138.1 0.1 reduce-window.8
  138.1 0.1 reduce
  138.3 0.4 convolution_bitcast_fusion
  138.7 43.0 %psum.23 = f32[48]{0:T(128)S(1)} all-reduce(f32[48]{0:T(128)S(1)} %convolution_bitcast_fusion), channel_id=1, replica_groups=mesh['island'=4,'chip'=4,'core'=2] {'island','chip','core'}, use_global_device_ids=true, to_apply=%region_6.7 | all-reduce | flops 48 | bytes 384 | tf_op jit(solution)/shard_map/psum | solution.py:139
  181.6 0.5 rsqrt_multiply_fusion
  182.2 42.0 %all-reduce.3.cloned.1.call-done = f32[1024,512]{1,0:T(8,128)} async-done(((f32[1024,512]{1,0:T(8,128)}), f32[1024,512]{1,0:T(8,128)}) %all-reduce.3.cloned.1.call-update) | async-done | bytes 2097168 | tf_op jit(solution)/shard_map/psum | solution.py:134
  224.2 0.0 copy-done.2
  224.2 5.0 %multiply_subtract_fusion = (f32[1024,512]{1,0:T(8,128)}, f32[1024,512]{1,0:T(8,128)}) fusion(f32[1024,512]{1,0:T(8,128)S(1)} %copy-done.2, f32[1024,512]{1,0:T(8,128)} %all-reduce.3.cloned.1.call-done, f32[1024,512]{1,0:T(8,128)} %param.11), kind=kLoop, calls=%fused_computation.30 | loop fusion | flops 3670016 | bytes 10485760 | tf_op jit(solution)/shard_map/sub | solution.py:136
  (5 shorter events, 0.1 us)
Async XLA Ops:
  7.2 106.1 %reduce-scatter.4.cloned.1.call-start = ((), (), s32[]{:S(2)}) async-start(), calls=%async_computation.2 | async-start | bytes 5898240
  13.5 8.1 %collective-permute-start.1 = (bf16[512,1024]{1,0:T(8,128)(2,1)}, bf16[512,1024]{1,0:T(8,128)(2,1)}, u32[]{:S(2)}, u32[]{:S(2)}) collective-permute-start(bf16[512,1024]{1,0:T(8,128)(2,1)} %get-tuple-element.7), channel_id=1, source_target_pairs={{0,1},{1,0},{2,3},{3,2},{4,5},{5,4},{6,7},{7,6},{8,9},{9,8},{10,11... | collective-permute-start | bytes 3145736 | tf_op jit(solution)/shard_map/ppermute | solution.py:103
  14.0 7.7 %collective-permute-start.2 = (bf16[512,1024]{1,0:T(8,128)(2,1)}, bf16[512,1024]{1,0:T(8,128)(2,1)}, u32[]{:S(2)}, u32[]{:S(2)}) collective-permute-start(bf16[512,1024]{1,0:T(8,128)(2,1)} %get-tuple-element.8), channel_id=1, source_target_pairs={{0,1},{1,0},{2,3},{3,2},{4,5},{5,4},{6,7},{7,6},{8,9},{9,8},{10,11... | collective-permute-start | bytes 3145736 | tf_op jit(solution)/shard_map/ppermute | solution.py:103
  14.1 7.7 %collective-permute-start.3 = (bf16[512,1024]{1,0:T(8,128)(2,1)S(1)}, bf16[512,1024]{1,0:T(8,128)(2,1)}, u32[]{:S(2)}, u32[]{:S(2)}) collective-permute-start(bf16[512,1024]{1,0:T(8,128)(2,1)S(1)} %get-tuple-element.14), channel_id=1, source_target_pairs={{0,1},{1,0},{2,3},{3,2},{4,5},{5,4},{6,7},{7,6},{8,9},{9,8},{10,11... | collective-permute-start | bytes 3145736 | tf_op jit(solution)/shard_map/ppermute | solution.py:103
  14.5 7.2 %collective-permute-start.4 = (bf16[512,1024]{1,0:T(8,128)(2,1)S(1)}, bf16[512,1024]{1,0:T(8,128)(2,1)}, u32[]{:S(2)}, u32[]{:S(2)}) collective-permute-start(bf16[512,1024]{1,0:T(8,128)(2,1)S(1)} %get-tuple-element.13), channel_id=1, source_target_pairs={{0,1},{1,0},{2,3},{3,2},{4,5},{5,4},{6,7},{7,6},{8,9},{9,8},{10,11... | collective-permute-start | bytes 3145736 | tf_op jit(solution)/shard_map/ppermute | solution.py:103
  16.4 1.2 copy-start.3
  16.4 1.5 copy-start.4
  16.6 5.0 %collective-permute-start = (bf16[512,512]{0,1:T(8,128)(2,1)S(1)}, bf16[512,512]{0,1:T(8,128)(2,1)S(1)}, u32[]{:S(2)}, u32[]{:S(2)}) collective-permute-start(bf16[512,512]{0,1:T(8,128)(2,1)S(1)} %bitcast.107), channel_id=1, source_target_pairs={{0,1},{1,0},{2,3},{3,2},{4,5},{5,4},{6,7},{7,6},{8,9},{9,8},{10,11... | collective-permute-start | bytes 1572872 | tf_op jit(solution)/shard_map/ppermute | solution.py:104
  25.9 3.2 %copy-start.1 = (f32[512,4,1024]{2,0,1:T(8,128)}, f32[512,4,1024]{2,0,1:T(8,128)S(1)}, u32[]{:S(2)}) copy-start(f32[512,4,1024]{2,0,1:T(8,128)S(1)} %fusion.16) | copy-start | bytes 25165828
  31.9 192.3 %all-reduce.3.cloned.1.call-start = ((), (), s32[]{:S(2)}) async-start(), calls=%async_computation.1 | async-start | bytes 4194304 | tf_op jit(solution)/shard_map/psum | solution.py:134
  34.5 1.8 copy-start
  36.7 49.6 %collective-permute-start.5 = (f32[224,2,1024]{2,0,1:T(8,128)S(1)}, f32[224,2,1024]{2,0,1:T(8,128)}, u32[]{:S(2)}, u32[]{:S(2)}) collective-permute-start(f32[224,2,1024]{2,0,1:T(8,128)S(1)} %broadcast_select_fusion), channel_id=1, source_target_pairs={{0,2},{1,5},{2,0},{3,7},{4,6},{5,1},{6,4},{7,3},{8,10},{9,13},{10,... | collective-permute-start | bytes 5505032 | tf_op jit(solution)/shard_map/ppermute | solution.py:72
  91.9 20.8 %collective-permute-start.6 = (f32[224,1024]{1,0:T(8,128)S(1)}, f32[224,1024]{1,0:T(8,128)S(1)}, u32[]{:S(2)}, u32[]{:S(2)}) collective-permute-start(f32[224,1024]{1,0:T(8,128)S(1)} %select_bitcast_fusion), channel_id=1, source_target_pairs={{0,4},{1,3},{2,6},{3,1},{4,0},{5,7},{6,2},{7,5},{8,12},{9,11},{10,... | collective-permute-start | bytes 2752520 | tf_op jit(solution)/shard_map/ppermute | solution.py:75
  137.3 0.7 copy-start.5
  137.3 86.9 %copy-start.2 = (f32[1024,512]{1,0:T(8,128)S(1)}, f32[1024,512]{1,0:T(8,128)}, u32[]{:S(2)}) copy-start(f32[1024,512]{1,0:T(8,128)} %param.10) | copy-start | bytes 6291460
Sparse Core Ops, SparseCore 0:
  32.0 76.8 reduce-scatter.3
  137.5 86.6 all-reduce.2
